TPU v7x, 256 devices: a whole 4x4x8 slice. The times are simulated.
256 devices in a mesh: fsdp: 8 (over z_lo, core), seq: 32 (over x, z_hi, y).
Axes of the slice: x: 4, y: 4, z: 8 (z_hi: 2, z_lo: 4; z = z_hi * 4 + z_lo), core: 2. Of those that a mesh axis runs over, the one named last changes fastest.
Arguments:
- tokens: bfloat16 [2, 4096, 4096], P(None, 'seq'), may hold values from -6 to 6
- positions: int32 [2, 4096], replicated, may hold values from 0 to 4095, as said below
- cached_len: int32 [2], replicated, may hold values from 16 to 4096, as said below
- cache_keys: bfloat16 [2, 4096, 8, 128], P(None, 'seq', 'fsdp'), may hold values from -6 to 6
- cache_values: bfloat16 [2, 4096, 8, 128], P(None, 'seq', 'fsdp'), may hold values from -6 to 6
- w_query: bfloat16 [4096, 4096], P('seq', 'fsdp')
- w_key: bfloat16 [4096, 1024], P('seq', 'fsdp')
- w_value: bfloat16 [4096, 1024], P('seq', 'fsdp'), may hold values from -0.09375 to 0.09375
- w_out_t: bfloat16 [4096, 4096], P('seq', 'fsdp'), may hold values from -1.5 to 1.5
Outputs:
- mixed: bfloat16 [2, 4096, 4096], P(None, 'seq', 'fsdp')
- new_keys: bfloat16 [2, 4096, 8, 128], P(None, 'seq', 'fsdp')
- new_values: bfloat16 [2, 4096, 8, 128], P(None, 'seq', 'fsdp')
Inputs may be any that keep to these rules, and one draw needn't show every extreme that they name: For each request the stored order is a permutation of 0 to 4095: the span is cut into 64 blocks of 64 positions, and the 128 stored rows of each index of seq are one block b followed by the block 63 - b, each in rising order; b is drawn per request and index. `cached_len`: some request has exactly 4096 cached positions.
All inputs are finite; a program needn't handle non-finite values.
Results may differ from a plain program's by a relative error of at most 0.015.
The roundings to bfloat16 on the way count: a program that leaves them out, or rounds other values in their place, can miss the bound.
Values may be sent and summed in bfloat16 or wider, within the bound.
No kernel may reach another device: no remote copies, remote signals or barrier semaphores. Data moves between devices by JAX's collectives and lax.ppermute only.
A program may use at most 128 MiB of HBM per device.

v0:
```python
import math

import jax
import jax.numpy as jnp
from jax import lax
from jax.sharding import PartitionSpec as P

SINKS = 4


NEGATIVE = -1e30


def attend_block(running_state, queries, key_block, value_block, allowed):
    top_old, denom_old, numer_old = running_state
    scores = jnp.einsum("rqkgd,rpkd->rkgqp", queries, key_block, preferred_element_type=jnp.float32)
    scores = scores * (1.0 / math.sqrt(queries.shape[-1]))
    visible = allowed[:, None, None, :, :]
    scores = jnp.where(visible, scores, NEGATIVE)
    top_new = jnp.maximum(top_old, jnp.max(scores, axis=-1))
    rescale = jnp.exp(top_old - top_new)
    weights = jnp.where(visible, jnp.exp(scores - top_new[..., None]), 0.0)
    denom_new = denom_old * rescale + jnp.sum(weights, axis=-1)
    numer_new = numer_old * rescale[..., None] + jnp.einsum(
        "rkgqp,rpkd->rkgqd",
        weights.astype(jnp.bfloat16),
        value_block,
        preferred_element_type=jnp.float32,
    )
    return (top_new, denom_new, numer_new)


def shards(
    tokens, positions, cached_len, cache_keys, cache_values, w_query, w_key, w_value, w_out_t
):
    requests, rows, width = tokens.shape
    head_size = cache_keys.shape[3]
    kv_local = cache_keys.shape[2]
    group_size = w_query.shape[1] // (kv_local * head_size)
    seq_index = lax.axis_index("seq")
    seq_count = lax.axis_size("seq")
    window_len = rows * seq_count // 2
    my_positions = lax.dynamic_slice_in_dim(positions, seq_index * rows, rows, 1)
    flat_tokens = tokens.reshape(requests * rows, width)
    weight_pieces = (
        lax.all_gather(w_query, "seq", axis=0, tiled=True),
        lax.all_gather(w_key, "seq", axis=0, tiled=True),
        lax.all_gather(w_value, "seq", axis=0, tiled=True),
    )
    query_sum, key_sum, value_sum = tuple(
        (
            jnp.dot(flat_tokens, weight_piece, preferred_element_type=jnp.float32)
            for weight_piece in weight_pieces
        )
    )
    queries = query_sum.astype(jnp.bfloat16).reshape(
        requests, rows, kv_local, group_size, head_size
    )
    new_keys = key_sum.astype(jnp.bfloat16).reshape(requests, rows, kv_local, head_size)
    new_values = value_sum.astype(jnp.bfloat16).reshape(requests, rows, kv_local, head_size)
    lengths = cached_len[:, None]
    window_floor = lengths + my_positions - window_len
    running_state = (
        jnp.full((requests, kv_local, group_size, rows), NEGATIVE, jnp.float32),
        jnp.zeros((requests, kv_local, group_size, rows), jnp.float32),
        jnp.zeros((requests, kv_local, group_size, rows, head_size), jnp.float32),
    )
    block_pieces = (
        lax.all_gather(cache_keys, "seq", axis=1, tiled=True),
        lax.all_gather(cache_values, "seq", axis=1, tiled=True),
    )
    key_pos = jnp.arange(block_pieces[0].shape[1], dtype=jnp.int32)
    key_pos = key_pos[None, None, :]
    allowed = (key_pos < lengths[:, :, None]) & (
        (key_pos < SINKS) | (key_pos > window_floor[:, :, None])
    )
    running_state = attend_block(running_state, queries, block_pieces[0], block_pieces[1], allowed)
    block_pieces = (
        lax.all_gather(new_keys, "seq", axis=1, tiled=True),
        lax.all_gather(new_values, "seq", axis=1, tiled=True),
    )
    before = my_positions[:, :, None] - positions[:, None, :]
    allowed = (before >= 0) & (before < window_len)
    running_state = attend_block(running_state, queries, block_pieces[0], block_pieces[1], allowed)
    top_final, denom_final, numer_final = running_state
    attended = (numer_final / denom_final[..., None]).astype(jnp.bfloat16)
    attended = jnp.transpose(attended, (0, 3, 1, 2, 4)).reshape(
        requests * rows, kv_local * group_size * head_size
    )
    partial_out = lax.dot_general(
        attended,
        lax.all_gather(w_out_t, "seq", axis=0, tiled=True),
        (((1,), (1,)), ((), ())),
        preferred_element_type=jnp.float32,
    )
    mixed = lax.psum_scatter(
        partial_out.reshape(requests, rows, width).astype(jnp.bfloat16),
        "fsdp",
        scatter_dimension=2,
        tiled=True,
    )
    return (mixed, new_keys, new_values)


def solution(mesh):
    placed = (
        P(None, "seq", None),
        P(),
        P(),
        P(None, "seq", "fsdp", None),
        P(None, "seq", "fsdp", None),
        P("seq", "fsdp"),
        P("seq", "fsdp"),
        P("seq", "fsdp"),
        P("seq", "fsdp"),
    )
    return jax.shard_map(
        shards,
        mesh=mesh,
        in_specs=placed,
        out_specs=(
            P(None, "seq", "fsdp"),
            P(None, "seq", "fsdp", None),
            P(None, "seq", "fsdp", None),
        ),
        check_vma=False,
    )
```

profile of v0, /device:TPU:6, one launch (start us, length us, event | category | flops | bytes accessed | tf_op | source)
XLA Modules:
  0.0 814.5 jit_solution(16966259465033407726)
XLA Ops:
  7.2 0.0 copy-start
  7.2 0.0 all-gather.15.cloned.1.call-start
  7.2 0.7 all-gather.15.cloned.1.call-update
  7.9 0.0 all-gather.19.cloned.1.call-start
  8.0 0.7 all-gather.19.cloned.1.call-update
  8.7 0.0 all-gather.9.cloned.1.call-start
  8.7 0.7 all-gather.9.cloned.1.call-update
  9.4 0.0 all-gather.17.cloned.1.call-start
  9.4 84.8 %all-gather.15.cloned.1.call-done = bf16[4096,128]{1,0:T(8,128)(2,1)} async-done(((bf16[128,128]{1,0:T(8,128)(2,1)}), bf16[4096,128]{1,0:T(8,128)(2,1)}) %all-gather.15.cloned.1.call-update) | async-done | bytes 1048592 | tf_op jit(solution)/shard_map/all_gather | solution.py:47
  94.2 0.0 copy-done
  94.2 2.6 convolution_convert_fusion.3
  96.7 0.0 all-gather.17.cloned.1.call-update
  96.8 0.0 all-gather.11.cloned.1.call-start
  96.8 0.5 all-gather.11.cloned.1.call-update
  97.4 0.0 all-gather.13.cloned.1.call-start
  97.4 1.6 copy.14
  99.0 0.0 all-gather.13.cloned.1.call-update
  99.0 0.0 all-gather.21.cloned.1.call-start
  99.1 74.3 %all-gather.19.cloned.1.call-done = bf16[4096,128]{1,0:T(8,128)(2,1)} async-done(((bf16[128,128]{1,0:T(8,128)(2,1)}), bf16[4096,128]{1,0:T(8,128)(2,1)}) %all-gather.19.cloned.1.call-update) | async-done | bytes 1048592 | tf_op jit(solution)/shard_map/all_gather | solution.py:48
  173.3 1.9 convolution_convert_fusion.2
  175.3 0.0 copy-start.2
  175.3 0.7 copy.17
  176.0 0.0 all-gather.21.cloned.1.call-update
  176.0 0.0 all-gather.23.cloned.1.call-start
  176.1 0.7 all-gather.23.cloned.1.call-update
  176.8 0.0 reduce-scatter.2.cloned.1.call-start
  176.9 0.7 iota_compare_fusion.1
  177.6 0.8 add_add_fusion
  178.4 3.5 fusion.16
  181.9 100.4 %all-gather.9.cloned.1.call-done = bf16[4096,512]{1,0:T(8,128)(2,1)} async-done(((bf16[128,512]{1,0:T(8,128)(2,1)}), bf16[4096,512]{1,0:T(8,128)(2,1)}) %all-gather.9.cloned.1.call-update) | async-done | bytes 4194320 | tf_op jit(solution)/shard_map/all_gather | solution.py:46
  282.3 4.1 convolution_convert_fusion.1
  286.4 1.0 reshape.173
  287.4 84.5 %all-gather.17.cloned.1.call-done = bf16[2,4096,1,128]{3,1,0,2:T(8,128)(2,1)} async-done(((bf16[2,128,1,128]{3,1,0,2:T(8,128)(2,1)}), bf16[2,4096,1,128]{3,1,0,2:T(8,128)(2,1)}) %all-gather.17.cloned.1.call-update) | async-done | bytes 2097168 | tf_op jit(solution)/shard_map/all_gather | solution.py:79
  371.9 9.3 %fusion.1 = (f32[2,4,128]{2,1,0:T(4,128)S(1)}, f32[2,4096,128,4]{1,2,3,0:T(8,128)}) fusion(pred[2,128,4096]{2,1,0:T(8,128)(4,1)S(1)} %get-tuple-element.18, bf16[2,128,4,128]{3,2,1,0:T(4,128)(2,1)S(1)} %reshape.173, bf16[2,4096,1,128]{3,1,0,2:T(8,128)(2,1)} %all-gather.17.cloned.1.call-done), kind=kOutput, calls=%fused_computation.5 | convolution fusion | flops 1086323712 | bytes 20189184 | tf_op jit(solution)/shard_map/rqkgd,rpkd->rkgqp/dot_general | solution.py:16
  381.2 0.0 copy-done.2
  381.2 79.6 %all-gather.11.cloned.1.call-done = bf16[2,4096,1,128]{3,1,0,2:T(8,128)(2,1)} async-done(((bf16[2,128,1,128]{3,1,0,2:T(8,128)(2,1)}), bf16[2,4096,1,128]{3,1,0,2:T(8,128)(2,1)}) %all-gather.11.cloned.1.call-update) | async-done | bytes 2097168 | tf_op jit(solution)/shard_map/all_gather | solution.py:69
  460.8 0.0 copy-start.1
  460.8 0.0 slice-start
  460.8 0.0 slice-start.1
  460.8 0.0 slice-start.2
  460.8 10.4 %fusion = (f32[2,4,128]{2,1,0:T(4,128)S(1)}, f32[2,128,4,4096]{3,1,2,0:T(8,128)}) fusion(pred[2,128,4096]{2,1,0:T(8,128)(4,1)} %get-tuple-element.17, bf16[2,4096,1,128]{3,1,0,2:T(8,128)(2,1)} %all-gather.11.cloned.1.call-done, bf16[2,128,4,128]{3,2,1,0:T(4,128)(2,1)S(1)} %reshape.173), kind=kOutput, calls=%fused_computation.4 | convolution fusion | flops 1086323712 | bytes 20189184 | tf_op jit(solution)/shard_map/rqkgd,rpkd->rkgqp/dot_general | solution.py:16
  471.2 0.0 copy-done.1
  471.2 0.0 slice-start.3
  471.2 8.7 %fusion.2 = f32[2,4,128]{2,1,0:T(4,128)S(1)} fusion(f32[2,128,4,4096]{3,1,2,0:T(8,128)} %get-tuple-element.14, f32[2,4,128]{2,1,0:T(4,128)S(1)} %get-tuple-element.12, pred[2,128,4096]{2,1,0:T(8,128)(4,1)S(1)} %copy-done.1), kind=kLoop, calls=%fused_computation.6 | loop fusion | flops 20970496 | bytes 17833984 | tf_op jit(solution)/shard_map/reduce_sum | solution.py:23
  479.9 0.0 slice-done
  479.9 0.0 slice-done.1
  479.9 0.0 slice-done.2
  479.9 0.0 slice-done.3
  479.9 5.0 fusion.4
  484.9 72.1 %all-gather.13.cloned.1.call-done = bf16[2,4096,1,128]{1,3,0,2:T(8,128)(2,1)} async-done(((bf16[2,128,1,128]{1,3,0,2:T(8,128)(2,1)}), bf16[2,4096,1,128]{1,3,0,2:T(8,128)(2,1)}) %all-gather.13.cloned.1.call-update) | async-done | bytes 2097168 | tf_op jit(solution)/shard_map/all_gather | solution.py:70
  557.0 10.6 %fusion.34 = f32[2,4,128,128]{2,3,1,0:T(8,128)} fusion(bf16[2,4096,1,128]{1,3,0,2:T(8,128)(2,1)} %all-gather.13.cloned.1.call-done, f32[2,128,4,4096]{3,1,2,0:T(8,128)} %get-tuple-element.14, f32[2,4,128]{2,1,0:T(4,128)S(1)} %get-tuple-element.12, pred[2,128,4096]{2,1,0:T(8,128)(4,1)} %get-tuple-element.17, f32[2,4,128]{2,1,0:T(4,128)S(1)} %get-tuple-element.7, ...), kind=kOutput, calls=%fused_computation.32 | convolution fusion | flops 1094975488 | bytes 20459520 | tf_op jit(solution)/shard_map/rkgqp,rpkd->rkgqd/dot_general | solution.py:24
  567.7 87.5 %all-gather.21.cloned.1.call-done = bf16[2,4096,1,128]{1,3,0,2:T(8,128)(2,1)} async-done(((bf16[2,128,1,128]{1,3,0,2:T(8,128)(2,1)}), bf16[2,4096,1,128]{1,3,0,2:T(8,128)(2,1)}) %all-gather.21.cloned.1.call-update) | async-done | bytes 2097168 | tf_op jit(solution)/shard_map/all_gather | solution.py:80
  655.1 9.7 %fusion.44 = bf16[2,4,128,128]{2,3,1,0:T(8,128)(2,1)S(1)} fusion(f32[2,4,128,128]{2,3,1,0:T(8,128)} %fusion.34, bf16[2,4096,1,128]{1,3,0,2:T(8,128)(2,1)} %all-gather.21.cloned.1.call-done, f32[2,4096,128,4]{1,2,3,0:T(8,128)} %get-tuple-element.16, f32[2,4,128]{2,1,0:T(4,128)S(1)} %get-tuple-element.11, pred[2,128,4096]{2,1,0:T(8,128)(4,1)S(1)} %get-tuple-element.18, ...), kind=kOutput, calls=%fused_computation.37 | convolution fusion | flops 1095106560 | bytes 20717568 | tf_op jit(solution)/shard_map/rkgqp,rpkd->rkgqd/dot_general | solution.py:24
  664.9 100.7 %all-gather.23.cloned.1.call-done = bf16[4096,512]{1,0:T(8,128)(2,1)} async-done(((bf16[128,512]{1,0:T(8,128)(2,1)}), bf16[4096,512]{1,0:T(8,128)(2,1)}) %all-gather.23.cloned.1.call-update) | async-done | bytes 4194320 | tf_op jit(solution)/shard_map/all_gather | solution.py:92
  765.6 4.8 convolution_convert_fusion
  770.5 0.0 reduce-scatter.2.cloned.1.call-update
  770.5 37.5 %reduce-scatter.2.cloned.1.call-done = bf16[2,128,512]{2,1,0:T(8,128)(2,1)} async-done(((bf16[2,128,4096]{2,1,0:T(8,128)(2,1)}), bf16[2,128,512]{2,1,0:T(8,128)(2,1)}) %reduce-scatter.2.cloned.1.call-update) | async-done | bytes 262160 | tf_op jit(solution)/shard_map/reduce_scatter | solution.py:96
  (4 shorter events, 0.0 us)
Async XLA Ops:
  7.2 87.0 %copy-start = (bf16[2,128,4096]{2,1,0:T(8,128)(2,1)S(1)}, bf16[2,128,4096]{2,1,0:T(8,128)(2,1)}, u32[]{:S(2)}) copy-start(bf16[2,128,4096]{2,1,0:T(8,128)(2,1)} %param.9) | copy-start | bytes 6291460
  7.2 87.0 %all-gather.15.cloned.1.call-start = ((), (), s32[]{:S(2)}) async-start(), calls=%async_computation.4 | async-start | bytes 1081344 | tf_op jit(solution)/shard_map/all_gather | solution.py:47
  7.9 165.4 %all-gather.19.cloned.1.call-start = ((), (), s32[]{:S(2)}) async-start(), calls=%async_computation.6 | async-start | bytes 1081344 | tf_op jit(solution)/shard_map/all_gather | solution.py:48
  8.7 273.6 %all-gather.9.cloned.1.call-start = ((), (), s32[]{:S(2)}) async-start(), calls=%async_computation.1 | async-start | bytes 4325376 | tf_op jit(solution)/shard_map/all_gather | solution.py:46
  9.4 362.5 %all-gather.17.cloned.1.call-start = ((), (), s32[]{:S(2)}) async-start(), calls=%async_computation.5 | async-start | bytes 2162688 | tf_op jit(solution)/shard_map/all_gather | solution.py:79
  96.8 364.0 %all-gather.11.cloned.1.call-start = ((), (), s32[]{:S(2)}) async-start(), calls=%async_computation.2 | async-start | bytes 2162688 | tf_op jit(solution)/shard_map/all_gather | solution.py:69
  97.4 459.7 %all-gather.13.cloned.1.call-start = ((), (), s32[]{:S(2)}) async-start(), calls=%async_computation.3 | async-start | bytes 2162688 | tf_op jit(solution)/shard_map/all_gather | solution.py:70
  99.0 556.1 %all-gather.21.cloned.1.call-start = ((), (), s32[]{:S(2)}) async-start(), calls=%async_computation.7 | async-start | bytes 2162688 | tf_op jit(solution)/shard_map/all_gather | solution.py:80
  175.3 205.9 %copy-start.2 = (bf16[256,128]{1,0:T(8,128)(2,1)}, bf16[256,128]{1,0:T(8,128)(2,1)S(1)}, u32[]{:S(2)}) copy-start(bf16[256,128]{1,0:T(8,128)(2,1)S(1)} %convolution_convert_fusion.2) | copy-start | bytes 196612
  176.0 589.6 %all-gather.23.cloned.1.call-start = ((), (), s32[]{:S(2)}) async-start(), calls=%async_computation.8 | async-start | bytes 4325376 | tf_op jit(solution)/shard_map/all_gather | solution.py:92
  176.8 631.2 %reduce-scatter.2.cloned.1.call-start = ((), (), s32[]{:S(2)}) async-start(), calls=%async_computation.9 | async-start | bytes 2359296 | tf_op jit(solution)/shard_map/reduce_scatter | solution.py:96
  460.8 10.4 %copy-start.1 = (pred[2,128,4096]{2,1,0:T(8,128)(4,1)S(1)}, pred[2,128,4096]{2,1,0:T(8,128)(4,1)}, u32[]{:S(2)}) copy-start(pred[2,128,4096]{2,1,0:T(8,128)(4,1)} %get-tuple-element.17) | copy-start | bytes 3145732
  460.8 19.1 %slice-start = ((s8[16777216]{0:T(1024)(128)(4,1)}), s8[4194304]{0:T(1024)(128)(4,1)S(1)}, s32[]{:S(2)}) async-start(s8[16777216]{0:T(1024)(128)(4,1)} %bitcast.122), calls=%async_computation.10 | async-start | bytes 8388608
  460.8 19.1 %slice-start.1 = ((s8[16777216]{0:T(1024)(128)(4,1)}), s8[4194304]{0:T(1024)(128)(4,1)S(1)}, s32[]{:S(2)}) async-start(s8[16777216]{0:T(1024)(128)(4,1)} %bitcast.122), calls=%async_computation.11 | async-start | bytes 8388608
  460.8 19.1 %slice-start.2 = ((s8[16777216]{0:T(1024)(128)(4,1)}), s8[4194304]{0:T(1024)(128)(4,1)S(1)}, s32[]{:S(2)}) async-start(s8[16777216]{0:T(1024)(128)(4,1)} %bitcast.122), calls=%async_computation.12 | async-start | bytes 8388608
  471.2 8.7 %slice-start.3 = ((s8[16777216]{0:T(1024)(128)(4,1)}), s8[4194304]{0:T(1024)(128)(4,1)S(1)}, s32[]{:S(2)}) async-start(s8[16777216]{0:T(1024)(128)(4,1)} %bitcast.122), calls=%async_computation.13 | async-start | bytes 8388608
Sparse Core Ops, SparseCore 0:
  11.4 82.7 all-gather.14
  97.6 75.6 all-gather.18
  176.9 105.3 all-gather.8
  286.3 85.6 all-gather.16
  375.3 85.4 all-gather.10
  463.9 93.1 all-gather.12
  560.2 94.8 all-gather.20
  658.7 106.9 all-gather.22
  770.6 37.3 reduce-scatter.1
where the time goes:
time: 815 us; the launch traced here: 814 us
  waiting for transfers between devices  725 us (89%)
  matrix products  53.4 us (7%)
  other arithmetic  18.7 us (2%)
  between operations  14 us (2%)
    all_gather x1, waiting for transfers between devices, shards(): lax.all_gather(w_out_t, 'seq', axis=0, tiled=True)  101 us
    all_gather x1, waiting for transfers between devices, shards(): lax.all_gather(w_query, 'seq', axis=0, tiled=True)  100 us
    all_gather x1, waiting for transfers between devices, shards(): lax.all_gather(new_values, 'seq', axis=1, tiled=True)  87.5 us
    all_gather x1, waiting for transfers between devices, shards(): lax.all_gather(w_key, 'seq', axis=0, tiled=True)  84.8 us
    all_gather x1, waiting for transfers between devices, shards(): lax.all_gather(new_keys, 'seq', axis=1, tiled=True)  84.5 us
    all_gather x1, waiting for transfers between devices, shards(): lax.all_gather(cache_keys, 'seq', axis=1, tiled=True)  79.6 us
    all_gather x1, waiting for transfers between devices, shards(): lax.all_gather(w_value, 'seq', axis=0, tiled=True)  74.3 us
    all_gather x1, waiting for transfers between devices, shards(): lax.all_gather(cache_values, 'seq', axis=1, tiled=True)  72.1 us
  transfers between devices with their start and end apart: 9, of which 9 were waited for; matrix products, arithmetic and copies ran while one was open for 9% of the time, Pallas kernels for 0%

commit v1 on v0

v1 whole, which is shorter than its diff:
```python
import math

import jax
import jax.numpy as jnp
from jax import lax
from jax.sharding import Mesh
from jax.sharding import PartitionSpec as P

SINKS = 4
NEGATIVE = -1e30

SEQ = ("x", "z_hi", "y")
FSDP = ("z_lo", "core")


def attend_block(running_state, queries, key_block, value_block, allowed):
    top_old, denom_old, numer_old = running_state
    scores = jnp.einsum("rqkgd,rpkd->rkgqp", queries, key_block, preferred_element_type=jnp.float32)
    scores = scores * (1.0 / math.sqrt(queries.shape[-1]))
    visible = allowed[:, None, None, :, :]
    scores = jnp.where(visible, scores, NEGATIVE)
    top_new = jnp.maximum(top_old, jnp.max(scores, axis=-1))
    rescale = jnp.exp(top_old - top_new)
    weights = jnp.where(visible, jnp.exp(scores - top_new[..., None]), 0.0)
    denom_new = denom_old * rescale + jnp.sum(weights, axis=-1)
    numer_new = numer_old * rescale[..., None] + jnp.einsum(
        "rkgqp,rpkd->rkgqd",
        weights.astype(jnp.bfloat16),
        value_block,
        preferred_element_type=jnp.float32,
    )
    return (top_new, denom_new, numer_new)


def gather_seq(piece, sizes):
    rows, cols = piece.shape
    nx, nz, ny = sizes
    piece = lax.all_gather(piece, "z_hi", axis=0, tiled=False)
    piece = lax.all_gather(piece, ("x", "y"), axis=0, tiled=False)
    piece = piece.reshape(nx, ny, nz, rows, cols).transpose(0, 2, 1, 3, 4)
    return piece.reshape(nx * nz * ny * rows, cols)


def shards(
    sizes, tokens, positions, cached_len, cache_keys, cache_values, w_query, w_key, w_value, w_out_t
):
    requests, rows, width = tokens.shape
    head_size = cache_keys.shape[3]
    kv_local = cache_keys.shape[2]
    group_size = w_query.shape[1] // (kv_local * head_size)
    nx, nz, ny = sizes
    seq_index = (lax.axis_index("x") * nz + lax.axis_index("z_hi")) * ny + lax.axis_index("y")
    seq_count = nx * nz * ny
    window_len = rows * seq_count // 2
    my_positions = lax.dynamic_slice_in_dim(positions, seq_index * rows, rows, 1)
    flat_tokens = tokens.reshape(requests * rows, width)

    q_cols = w_query.shape[1]
    k_cols = w_key.shape[1]
    o_cols = w_out_t.shape[1]
    cache_k_local = jnp.transpose(cache_keys, (1, 0, 2, 3)).reshape(rows, -1)
    cache_v_local = jnp.transpose(cache_values, (1, 0, 2, 3)).reshape(rows, -1)
    packed = jnp.concatenate(
        [w_query, w_key, w_value, w_out_t, cache_k_local, cache_v_local], axis=1
    )
    gathered = gather_seq(packed, sizes)
    total_rows = gathered.shape[0]
    offs = [0]
    for c in (q_cols, k_cols, k_cols, o_cols, cache_k_local.shape[1], cache_v_local.shape[1]):
        offs.append(offs[-1] + c)
    w_qkv = gathered[:, : offs[3]]
    w_out_full = gathered[:, offs[3] : offs[4]]
    cache_k_full = gathered[:, offs[4] : offs[5]].reshape(total_rows, requests, kv_local, head_size)
    cache_v_full = gathered[:, offs[5] : offs[6]].reshape(total_rows, requests, kv_local, head_size)
    cache_k_full = jnp.transpose(cache_k_full, (1, 0, 2, 3))
    cache_v_full = jnp.transpose(cache_v_full, (1, 0, 2, 3))

    qkv_sum = jnp.dot(flat_tokens, w_qkv, preferred_element_type=jnp.float32)
    qkv = qkv_sum.astype(jnp.bfloat16)
    queries = qkv[:, :q_cols].reshape(requests, rows, kv_local, group_size, head_size)
    new_keys = qkv[:, q_cols : q_cols + k_cols].reshape(requests, rows, kv_local, head_size)
    new_values = qkv[:, q_cols + k_cols :].reshape(requests, rows, kv_local, head_size)

    lengths = cached_len[:, None]
    window_floor = lengths + my_positions - window_len
    running_state = (
        jnp.full((requests, kv_local, group_size, rows), NEGATIVE, jnp.float32),
        jnp.zeros((requests, kv_local, group_size, rows), jnp.float32),
        jnp.zeros((requests, kv_local, group_size, rows, head_size), jnp.float32),
    )
    key_pos = jnp.arange(total_rows, dtype=jnp.int32)
    key_pos = key_pos[None, None, :]
    allowed = (key_pos < lengths[:, :, None]) & (
        (key_pos < SINKS) | (key_pos > window_floor[:, :, None])
    )
    running_state = attend_block(running_state, queries, cache_k_full, cache_v_full, allowed)

    new_k_local = jnp.transpose(new_keys, (1, 0, 2, 3)).reshape(rows, -1)
    new_v_local = jnp.transpose(new_values, (1, 0, 2, 3)).reshape(rows, -1)
    new_gathered = gather_seq(jnp.concatenate([new_k_local, new_v_local], axis=1), sizes)
    half = new_k_local.shape[1]
    new_k_full = jnp.transpose(
        new_gathered[:, :half].reshape(total_rows, requests, kv_local, head_size), (1, 0, 2, 3)
    )
    new_v_full = jnp.transpose(
        new_gathered[:, half:].reshape(total_rows, requests, kv_local, head_size), (1, 0, 2, 3)
    )
    before = my_positions[:, :, None] - positions[:, None, :]
    allowed = (before >= 0) & (before < window_len)
    running_state = attend_block(running_state, queries, new_k_full, new_v_full, allowed)
    top_final, denom_final, numer_final = running_state
    attended = (numer_final / denom_final[..., None]).astype(jnp.bfloat16)
    attended = jnp.transpose(attended, (0, 3, 1, 2, 4)).reshape(
        requests * rows, kv_local * group_size * head_size
    )
    partial_out = lax.dot_general(
        attended,
        w_out_full,
        (((1,), (1,)), ((), ())),
        preferred_element_type=jnp.float32,
    )
    mixed = lax.psum_scatter(
        partial_out.reshape(requests, rows, width).astype(jnp.bfloat16),
        FSDP,
        scatter_dimension=2,
        tiled=True,
    )
    return (mixed, new_keys, new_values)


def solution(mesh):
    n_fsdp = mesh.shape["fsdp"]
    n_seq = mesh.shape["seq"]
    n_core = 2
    n_zlo = n_fsdp // n_core
    ny = 4
    nz = 2
    nx = n_seq // (ny * nz)
    fine = Mesh(mesh.devices.reshape(n_zlo, n_core, nx, nz, ny), ("z_lo", "core", "x", "z_hi", "y"))
    placed = (
        P(None, SEQ, None),
        P(),
        P(),
        P(None, SEQ, FSDP, None),
        P(None, SEQ, FSDP, None),
        P(SEQ, FSDP),
        P(SEQ, FSDP),
        P(SEQ, FSDP),
        P(SEQ, FSDP),
    )

    def body(*args):
        return shards((nx, nz, ny), *args)

    return jax.shard_map(
        body,
        mesh=fine,
        in_specs=placed,
        out_specs=(
            P(None, SEQ, FSDP),
            P(None, SEQ, FSDP, None),
            P(None, SEQ, FSDP, None),
        ),
        check_vma=False,
    )
```

time: 815 us -> 339 us (0.42)
  waiting for transfers between devices: 725 us -> 180 us
  local copies, waits for them, and re-layouts: 3.35 us -> 46.1 us
  blocking collectives: 0 us -> 32.6 us
  matrix products: 53.4 us -> 40.8 us
    all_gather x8 -> x2, waiting for transfers between devices: 684 us -> 139 us  [gather_seq(): piece = lax.all_gather(piece, ('x', 'y'), axis=0, tiled=False)]
    all_gather x0 -> x2, blocking collectives: none -> 32.6 us  [gather_seq(): piece = lax.all_gather(piece, 'z_hi', axis=0, tiled=False)]
    slice x0 -> x8, local copies, waits for them, and re-layouts: none -> 19.1 us  [the longest x2 7.47 us: shards(): gathered[:, offs[4]:offs[5]]]
    transpose x0 -> x4, local copies, waits for them, and re-layouts: none -> 12.1 us  [the longest x2 10.2 us: gather_seq(): piece = piece.reshape(nx, ny, nz, rows, cols).transpose(0, 2, 1, 3, 4)]
  transfers between devices with their start and end apart: 9 -> 3, of which waited for: 9 -> 3; matrix products, arithmetic and copies ran while one was open for 9% -> 10% of each run, Pallas kernels for 0% -> 0%
where the time goes in v1:
time: 339 us; the launch traced here: 338 us
  waiting for transfers between devices  180 us (53%)
  local copies, waits for them, and re-layouts  46.1 us (14%)
  matrix products  40.8 us (12%)
  blocking collectives  32.6 us (10%)
  other arithmetic  24.8 us (7%)
  between operations  14 us (4%)
    all_gather x2, waiting for transfers between devices, gather_seq(): piece = lax.all_gather(piece, ('x', 'y'), axis=0, tiled=False)  139 us
    reduce_scatter x1, waiting for transfers between devices, shards(): lax.psum_scatter(partial_out.reshape(requests, rows, width).astype(jnp.bf...  41.3 us
    all_gather x2, blocking collectives, gather_seq(): piece = lax.all_gather(piece, 'z_hi', axis=0, tiled=False)  32.6 us
    dot_general x2, matrix products, attend_block(): jnp.einsum('rqkgd,rpkd->rkgqp', queries, key_block, preferred_element_typ...  17.7 us
    dot_general x2, matrix products, attend_block(): jnp.einsum('rkgqp,rpkd->rkgqd', weights.astype(jnp.bfloat16), value_block...  16.5 us
    reduce_sum x1, other arithmetic, attend_block(): denom_new = denom_old * rescale + jnp.sum(weights, axis=-1)  15.4 us
    transpose x2, local copies, waits for them, and re-layouts, gather_seq(): piece = piece.reshape(nx, ny, nz, rows, cols).transpose(0, 2, 1, 3, 4)  10.2 us
    unnamed x27, local copies, waits for them, and re-layouts  8.66 us
  transfers between devices with their start and end apart: 3, of which 3 were waited for; matrix products, arithmetic and copies ran while one was open for 10% of the time, Pallas kernels for 0%

profile of v1, /device:TPU:6, one launch (start us, length us, event | category | flops | bytes accessed | tf_op | source)
XLA Modules:
  0.0 338.3 jit_solution(9477148280793496970)
XLA Ops:
  7.2 0.0 copy-start
  7.2 0.0 all-gather.7.cloned.1.call-start
  7.2 1.0 copy.59
  8.3 0.9 copy.60
  9.2 0.9 constant_dynamic-update-slice_fusion.3
  10.1 0.8 constant_dynamic-update-slice_fusion.2
  10.9 0.8 constant_dynamic-update-slice_fusion.1
  11.7 0.9 constant_dynamic-update-slice_fusion
  12.6 20.7 %all-gather = bf16[256,1792]{1,0:T(8,128)(2,1)} all-gather(bf16[128,1792]{1,0:T(8,128)(2,1)S(1)} %bitcast_dynamic-update-slice_fusion), channel_id=2, replica_groups=mesh['z_lo'=4,'core'=2,'x'=4,'z_hi'=2,'y'=4] {'z_hi'}, dimensions={0}, use_global_device_ids=true | all-gather | bytes 1376256 | tf_op jit(solution)/shard_map/all_gather | solution.py:38
  33.3 0.0 all-gather.7.cloned.1.call-update
  33.3 0.0 all-gather.9.cloned.1.call-start
  33.4 114.1 %all-gather.7.cloned.1.call-done = bf16[32,128,1792]{2,1,0:T(8,128)(2,1)} async-done(((bf16[2,128,1792]{2,1,0:T(8,128)(2,1)}), bf16[32,128,1792]{2,1,0:T(8,128)(2,1)}) %all-gather.7.cloned.1.call-update) | async-done | bytes 14680080 | tf_op jit(solution)/shard_map/all_gather | solution.py:39
  147.5 7.5 %copy.61 = bf16[4,2,4,128,1792]{4,3,2,1,0:T(8,128)(2,1)S(1)} copy(bf16[4,2,4,128,1792]{4,3,1,2,0:T(8,128)(2,1)} %bitcast.154) | data formatting | bytes 29360128 | tf_op jit(solution)/shard_map/transpose | solution.py:40
  155.0 0.0 copy-done
  155.0 0.0 copy-start.2
  155.1 0.0 copy-start.6
  155.1 5.2 %copy-done.2 = bf16[4,2,4,128,1792]{4,3,2,1,0:T(8,128)(2,1)} copy-done((bf16[4,2,4,128,1792]{4,3,2,1,0:T(8,128)(2,1)}, bf16[4,2,4,128,1792]{4,3,2,1,0:T(8,128)(2,1)S(1)}, u32[]{:S(2)}) %copy-start.2) | copy-done | bytes 14680088
  160.3 1.8 fusion.35
  162.1 0.0 copy-start.4
  162.1 0.0 copy-start.5
  162.1 0.1 copy.68
  162.2 0.1 copy.67
  162.4 11.9 %all-gather.2 = bf16[256,512]{0,1:T(8,128)(2,1)S(1)} all-gather(bf16[128,512]{0,1:T(8,128)(2,1)S(1)} %pad_maximum_fusion), channel_id=4, replica_groups=mesh['z_lo'=4,'core'=2,'x'=4,'z_hi'=2,'y'=4] {'z_hi'}, dimensions={0}, use_global_device_ids=true | all-gather | bytes 393216 | tf_op jit(solution)/shard_map/all_gather | solution.py:38
  174.3 0.8 copy.86
  175.1 0.0 all-gather.9.cloned.1.call-update
  175.1 0.0 reduce-scatter.2.cloned.1.call-start
  175.2 0.0 copy-done.6
  175.2 0.8 add_add_fusion
  176.0 0.1 iota_compare_fusion.1
  176.1 4.4 %fusion.17 = pred[2,128,4096]{1,2,0:T(8,128)(4,1)} fusion(s32[2,128]{1,0:T(2,128)S(1)} %get-tuple-element.17, pred[4096]{0:T(1024)(128)(4,1)S(1)} %iota_compare_fusion.2, pred[2,4096]{1,0:T(4,128)(4,1)S(1)} %iota_compare_fusion.1), kind=kLoop, calls=%fused_computation.24 | loop fusion | flops 3145728 | bytes 1061888 | tf_op jit(solution)/shard_map/and | solution.py:93
  180.4 0.0 copy-done.4
  180.4 0.0 copy-done.5
  180.4 4.1 %fusion.18 = pred[2,128,4096]{1,2,0:T(8,128)(4,1)S(1)} fusion(s32[2,4096]{1,0:T(2,128)} %param.10, s32[2,128]{1,0:T(2,128)S(1)} %get-tuple-element.18), kind=kLoop, calls=%fused_computation.25 | loop fusion | flops 4194304 | bytes 1082368 | tf_op jit(solution)/shard_map/and | solution.py:109
  184.6 0.1 reshape.215
  184.7 4.6 %fusion.53 = (bf16[4096,256]{1,0:T(8,128)(2,1)}, bf16[4096,256]{1,0:T(8,128)(2,1)}) fusion(bf16[4096,1792]{1,0:T(8,128)(2,1)} %bitcast.149), kind=kLoop, calls=%fused_computation.61 | loop fusion | bytes 8388608 | tf_op jit(solution)/shard_map/slice | solution.py:73
  189.2 2.9 copy.62
  192.1 2.5 copy.63
  194.6 4.2 %copy.65 = bf16[4096,256]{0,1:T(8,128)(2,1)} copy(bf16[4096,256]{1,0:T(8,128)(2,1)} %get-tuple-element.20) | data formatting | bytes 4194304 | tf_op jit(solution)/shard_map/slice | solution.py:74
  198.8 8.9 %fusion = (f32[2,4,128]{2,1,0:T(4,128)S(1)}, f32[2,4096,128,4]{2,1,3,0:T(8,128)}) fusion(pred[2,128,4096]{1,2,0:T(8,128)(4,1)} %fusion.17, bf16[2,128,4,128]{3,2,1,0:T(4,128)(2,1)S(1)} %reshape.215, bf16[4096,2,1,128]{3,0,1,2:T(8,128)(2,1)} %copy.63), kind=kOutput, calls=%fused_computation.4 | convolution fusion | flops 1086323712 | bytes 20189184 | tf_op jit(solution)/shard_map/rqkgd,rpkd->rkgqp/dot_general | solution.py:18
  207.7 24.4 %all-gather.9.cloned.1.call-done = bf16[32,128,512]{2,1,0:T(8,128)(2,1)} async-done(((bf16[2,128,512]{2,1,0:T(8,128)(2,1)}), bf16[32,128,512]{2,1,0:T(8,128)(2,1)}) %all-gather.9.cloned.1.call-update) | async-done | bytes 4194320 | tf_op jit(solution)/shard_map/all_gather | solution.py:39
  232.1 2.6 copy.70
  234.7 1.6 fusion.54
  236.3 2.9 copy.74
  239.3 2.9 copy.71
  242.2 2.5 copy.72
  244.7 0.0 copy-start.3
  244.7 0.0 slice-start
  244.7 0.0 slice-start.1
  244.7 8.8 %fusion.1 = (f32[2,4,128]{2,1,0:T(4,128)S(1)}, f32[2,4096,128,4]{2,1,3,0:T(8,128)}) fusion(pred[2,128,4096]{1,2,0:T(8,128)(4,1)S(1)} %fusion.18, bf16[2,128,4,128]{3,2,1,0:T(4,128)(2,1)S(1)} %reshape.215, bf16[4096,2,1,128]{3,0,1,2:T(8,128)(2,1)} %copy.72), kind=kOutput, calls=%fused_computation.5 | convolution fusion | flops 1086323712 | bytes 20189184 | tf_op jit(solution)/shard_map/rqkgd,rpkd->rkgqp/dot_general | solution.py:18
  253.5 0.0 copy-done.3
  253.5 0.0 slice-start.2
  253.5 0.0 slice-start.3
  253.5 15.4 %fusion.2 = (f32[2,4,128]{2,1,0:T(4,128)S(1)}, f32[2,4,128]{2,1,0:T(4,128)S(1)}) fusion(f32[2,4096,128,4]{2,1,3,0:T(8,128)} %get-tuple-element.29, f32[2,4,128]{2,1,0:T(4,128)S(1)} %get-tuple-element.27, pred[2,128,4096]{1,2,0:T(8,128)(4,1)S(1)} %copy-done.3, f32[2,4,128]{2,1,0:T(4,128)S(1)} %get-tuple-element.26, f32[2,4096,128,4]{2,1,3,0:T(8,128)} %get-tuple-element.31, ...), kind=kLoop, calls=%fused_computation.6 | loop fusion | flops 41940992 | bytes 35667968 | tf_op jit(solution)/shard_map/reduce_sum | solution.py:25
  269.0 0.0 slice-done
  269.0 0.0 slice-done.1
  269.0 0.0 slice-done.2
  269.0 0.0 slice-done.3
  269.1 6.2 %fusion.32 = f32[2,4,128,128]{2,3,1,0:T(8,128)} fusion(bf16[2,4096,128,1]{1,2,3,0:T(8,128)(2,1)} %bitcast.159, f32[2,4096,128,4]{2,1,3,0:T(8,128)S(1)} %bitcast.152, f32[2,4,128]{2,1,0:T(4,128)S(1)} %get-tuple-element.27, pred[2,128,4096]{1,2,0:T(8,128)(4,1)S(1)} %copy-done.3, f32[2,4,128]{2,1,0:T(4,128)S(1)} %get-tuple-element.16, ...), kind=kOutput, calls=%fused_computation.33 | convolution fusion | flops 1094975488 | bytes 20459520 | tf_op jit(solution)/shard_map/rkgqp,rpkd->rkgqd/dot_general | solution.py:26
  275.3 0.0 copy-start.1
  275.3 10.3 %fusion.41 = bf16[2,4,128,128]{2,3,1,0:T(8,128)(2,1)S(1)} fusion(f32[2,4,128,128]{2,3,1,0:T(8,128)} %fusion.32, bf16[2,4096,128,1]{1,2,3,0:T(8,128)(2,1)} %bitcast.160, f32[2,4096,128,4]{2,1,3,0:T(8,128)} %get-tuple-element.31, f32[2,4,128]{2,1,0:T(4,128)S(1)} %get-tuple-element.26, pred[2,128,4096]{1,2,0:T(8,128)(4,1)S(1)} %fusion.18, ...), kind=kOutput, calls=%fused_computation.36 | convolution fusion | flops 1095106560 | bytes 20717568 | tf_op jit(solution)/shard_map/rkgqp,rpkd->rkgqd/dot_general | solution.py:26
  285.6 4.9 %convolution_convert_fusion = bf16[2,128,4096]{2,1,0:T(8,128)(2,1)} fusion(bf16[2,128,512]{1,2,0:T(8,128)(2,1)S(1)} %bitcast.172, bf16[4096,1792]{1,0:T(8,128)(2,1)} %bitcast.150), kind=kOutput, calls=%fused_computation.20 | convolution fusion | flops 1074790400 | bytes 6553600 | tf_op jit(solution)/shard_map/dot_general | solution.py:116
  290.5 0.0 reduce-scatter.2.cloned.1.call-update
  290.5 41.3 %reduce-scatter.2.cloned.1.call-done = bf16[2,128,512]{2,1,0:T(8,128)(2,1)} async-done(((bf16[2,128,4096]{2,1,0:T(8,128)(2,1)}), bf16[2,128,512]{2,1,0:T(8,128)(2,1)}) %reduce-scatter.2.cloned.1.call-update) | async-done | bytes 262160 | tf_op jit(solution)/shard_map/reduce_scatter | solution.py:122
  331.7 0.0 copy-done.1
  (9 shorter events, 0.1 us)
Async XLA Ops:
  7.2 147.9 %copy-start = (bf16[2,128,4096]{2,1,0:T(8,128)(2,1)S(1)}, bf16[2,128,4096]{2,1,0:T(8,128)(2,1)}, u32[]{:S(2)}) copy-start(bf16[2,128,4096]{2,1,0:T(8,128)(2,1)} %param.9) | copy-start | bytes 6291460
  7.2 140.3 %all-gather.7.cloned.1.call-start = ((), (), s32[]{:S(2)}) async-start(), calls=%async_computation.2 | async-start | bytes 15597568 | tf_op jit(solution)/shard_map/all_gather | solution.py:39
  33.3 198.7 %all-gather.9.cloned.1.call-start = ((), (), s32[]{:S(2)}) async-start(), calls=%async_computation.3 | async-start | bytes 4456448 | tf_op jit(solution)/shard_map/all_gather | solution.py:39
  155.0 5.2 %copy-start.2 = (bf16[4,2,4,128,1792]{4,3,2,1,0:T(8,128)(2,1)}, bf16[4,2,4,128,1792]{4,3,2,1,0:T(8,128)(2,1)S(1)}, u32[]{:S(2)}) copy-start(bf16[4,2,4,128,1792]{4,3,2,1,0:T(8,128)(2,1)S(1)} %copy.61) | copy-start | bytes 44040196
  155.1 20.1 %copy-start.6 = (s32[2]{0:T(128)S(1)}, s32[2]{0:T(128)}, u32[]{:S(2)}) copy-start(s32[2]{0:T(128)} %param.11) | copy-start | bytes 28
  162.1 18.3 %copy-start.4 = (bf16[256,128]{1,0:T(8,128)(2,1)}, bf16[256,128]{1,0:T(8,128)(2,1)S(1)}, u32[]{:S(2)}) copy-start(bf16[256,128]{1,0:T(8,128)(2,1)S(1)} %get-tuple-element.23) | copy-start | bytes 196612
  162.1 18.3 %copy-start.5 = (bf16[256,128]{1,0:T(8,128)(2,1)}, bf16[256,128]{1,0:T(8,128)(2,1)S(1)}, u32[]{:S(2)}) copy-start(bf16[256,128]{1,0:T(8,128)(2,1)S(1)} %get-tuple-element.24) | copy-start | bytes 196612
  175.1 156.6 %reduce-scatter.2.cloned.1.call-start = ((), (), s32[]{:S(2)}) async-start(), calls=%async_computation.1 | async-start | bytes 2359296 | tf_op jit(solution)/shard_map/reduce_scatter | solution.py:122
  244.7 8.8 %copy-start.3 = (pred[2,128,4096]{1,2,0:T(8,128)(4,1)S(1)}, pred[2,128,4096]{1,2,0:T(8,128)(4,1)}, u32[]{:S(2)}) copy-start(pred[2,128,4096]{1,2,0:T(8,128)(4,1)} %fusion.17) | copy-start | bytes 3145732
  244.7 24.3 %slice-start = ((s8[16777216]{0:T(1024)(128)(4,1)}), s8[4194304]{0:T(1024)(128)(4,1)S(1)}, s32[]{:S(2)}) async-start(s8[16777216]{0:T(1024)(128)(4,1)} %bitcast.151), calls=%async_computation.4 | async-start | bytes 8388608
  244.7 24.3 %slice-start.1 = ((s8[16777216]{0:T(1024)(128)(4,1)}), s8[4194304]{0:T(1024)(128)(4,1)S(1)}, s32[]{:S(2)}) async-start(s8[16777216]{0:T(1024)(128)(4,1)} %bitcast.151), calls=%async_computation.5 | async-start | bytes 8388608
  253.5 15.5 %slice-start.2 = ((s8[16777216]{0:T(1024)(128)(4,1)}), s8[4194304]{0:T(1024)(128)(4,1)S(1)}, s32[]{:S(2)}) async-start(s8[16777216]{0:T(1024)(128)(4,1)} %bitcast.151), calls=%async_computation.6 | async-start | bytes 8388608
  253.5 15.5 %slice-start.3 = ((s8[16777216]{0:T(1024)(128)(4,1)}), s8[4194304]{0:T(1024)(128)(4,1)S(1)}, s32[]{:S(2)}) async-start(s8[16777216]{0:T(1024)(128)(4,1)} %bitcast.151), calls=%async_computation.7 | async-start | bytes 8388608
  275.3 56.4 %copy-start.1 = (bf16[2,128,4096]{2,1,0:T(8,128)(2,1)S(1)}, bf16[2,128,4096]{2,1,0:T(8,128)(2,1)}, u32[]{:S(2)}) copy-start(bf16[2,128,4096]{2,1,0:T(8,128)(2,1)} %param.9) | copy-start | bytes 6291460
Sparse Core Ops, SparseCore 0:
  33.5 113.9 all-gather.6
  175.3 56.7 all-gather.8
  290.6 41.0 reduce-scatter.1

commit v2 on v1

v2 whole, which is shorter than its diff:
```python
import math

import jax
import jax.numpy as jnp
from jax import lax
from jax.sharding import Mesh
from jax.sharding import PartitionSpec as P

SINKS = 4
NEGATIVE = -1e30

SEQ = ("x", "z_hi", "y")
FSDP = ("z_lo", "core")


def z_first_pair(piece, z_index, use_permute):
    if use_permute:
        other = lax.ppermute(piece, "z_hi", [(0, 1), (1, 0)])
        return jnp.where(z_index == 0, jnp.stack([piece, other]), jnp.stack([other, piece]))
    return lax.all_gather(piece, "z_hi", axis=0, tiled=False)


def xy_gather(pair):
    gathered = lax.all_gather(pair, ("x", "y"), axis=0, tiled=False)
    return gathered.reshape(-1, pair.shape[-1])


def to_gather_order(array, axis, sizes):
    nx, nz, ny = sizes
    shape = array.shape
    split = shape[:axis] + (nx, nz, ny, shape[axis] // (nx * nz * ny)) + shape[axis + 1 :]
    perm = list(range(len(split)))
    perm[axis + 1], perm[axis + 2] = perm[axis + 2], perm[axis + 1]
    return jnp.transpose(array.reshape(split), perm).reshape(shape)


def from_gather_order(array, axis, sizes):
    nx, nz, ny = sizes
    shape = array.shape
    split = shape[:axis] + (nx, ny, nz, shape[axis] // (nx * nz * ny)) + shape[axis + 1 :]
    perm = list(range(len(split)))
    perm[axis + 1], perm[axis + 2] = perm[axis + 2], perm[axis + 1]
    return jnp.transpose(array.reshape(split), perm).reshape(shape)


def attend_block(running_state, queries, keys, values, allowed):
    top_old, denom_old, numer_old = running_state
    rows = allowed.shape[0]
    scores = jnp.dot(queries, keys.T, preferred_element_type=jnp.float32)
    scores = scores * (1.0 / math.sqrt(queries.shape[-1]))
    scores = scores.reshape(rows, -1, keys.shape[0])
    visible = allowed[:, None, :]
    scores = jnp.where(visible, scores, NEGATIVE)
    top_new = jnp.maximum(top_old, jnp.max(scores, axis=-1))
    rescale = jnp.exp(top_old - top_new)
    weights = jnp.where(visible, jnp.exp(scores - top_new[..., None]), 0.0)
    denom_new = denom_old * rescale + jnp.sum(weights, axis=-1)
    numer_new = numer_old * rescale[..., None] + jnp.dot(
        weights.astype(jnp.bfloat16).reshape(queries.shape[0], -1),
        values,
        preferred_element_type=jnp.float32,
    ).reshape(numer_old.shape)
    return (top_new, denom_new, numer_new)


def shards(
    sizes, tokens, positions, cached_len, cache_keys, cache_values, w_query, w_key, w_value, w_out_t
):
    requests, rows, width = tokens.shape
    head_size = cache_keys.shape[3]
    kv_local = cache_keys.shape[2]
    group_size = w_query.shape[1] // (kv_local * head_size)
    nx, nz, ny = sizes
    z_index = lax.axis_index("z_hi")
    seq_index = (lax.axis_index("x") * nz + z_index) * ny + lax.axis_index("y")
    seq_count = nx * nz * ny
    total_rows = rows * seq_count
    window_len = total_rows // 2
    my_positions = lax.dynamic_slice_in_dim(positions, seq_index * rows, rows, 1)

    q_cols = w_query.shape[1]
    k_cols = w_key.shape[1]
    o_cols = w_out_t.shape[1]
    kv_cols = kv_local * head_size
    cache_k_local = jnp.transpose(cache_keys, (1, 0, 2, 3)).reshape(rows, -1)
    cache_v_local = jnp.transpose(cache_values, (1, 0, 2, 3)).reshape(rows, -1)
    packed = jnp.concatenate(
        [w_query, w_key, w_value, w_out_t, cache_k_local, cache_v_local], axis=1
    )
    gathered = xy_gather(z_first_pair(packed, z_index, False))
    o_off = q_cols + 2 * k_cols
    ck_off = o_off + o_cols
    cv_off = ck_off + requests * kv_cols

    flat_tokens = to_gather_order(tokens.reshape(requests * rows, width), 1, sizes)
    qkv = jnp.dot(
        flat_tokens, gathered[:, :o_off], preferred_element_type=jnp.float32
    ).astype(jnp.bfloat16)
    queries = qkv[:, :q_cols].reshape(requests, rows, kv_local, group_size, head_size)
    new_keys = qkv[:, q_cols : q_cols + k_cols].reshape(requests, rows, kv_local, head_size)
    new_values = qkv[:, q_cols + k_cols : o_off].reshape(requests, rows, kv_local, head_size)

    new_k_local = jnp.transpose(new_keys, (1, 0, 2, 3)).reshape(rows, -1)
    new_v_local = jnp.transpose(new_values, (1, 0, 2, 3)).reshape(rows, -1)
    new_gathered = xy_gather(
        z_first_pair(jnp.concatenate([new_k_local, new_v_local], axis=1), z_index, True)
    )
    nv_off = requests * kv_cols

    key_pos = to_gather_order(jnp.arange(total_rows, dtype=jnp.int32), 0, sizes)
    new_pos = to_gather_order(positions, 1, sizes)

    outs = []
    for r in range(requests):
        length = cached_len[r]
        t = my_positions[r]
        cache_allowed = (key_pos[None, :] < length) & (
            (key_pos[None, :] < SINKS) | (key_pos[None, :] > (length + t - window_len)[:, None])
        )
        before = t[:, None] - new_pos[r][None, :]
        new_allowed = (before >= 0) & (before < window_len)
        heads = []
        for k in range(kv_local):
            col = (r * kv_local + k) * head_size
            q_rows = queries[r, :, k].reshape(rows * group_size, head_size)
            state = (
                jnp.full((rows, group_size), NEGATIVE, jnp.float32),
                jnp.zeros((rows, group_size), jnp.float32),
                jnp.zeros((rows, group_size, head_size), jnp.float32),
            )
            state = attend_block(
                state,
                q_rows,
                gathered[:, ck_off + col : ck_off + col + head_size],
                gathered[:, cv_off + col : cv_off + col + head_size],
                cache_allowed,
            )
            state = attend_block(
                state,
                q_rows,
                new_gathered[:, col : col + head_size],
                new_gathered[:, nv_off + col : nv_off + col + head_size],
                new_allowed,
            )
            _, denom, numer = state
            heads.append((numer / denom[..., None]).astype(jnp.bfloat16).reshape(rows, -1))
        outs.append(jnp.concatenate(heads, axis=1) if kv_local > 1 else heads[0])
    attended = jnp.concatenate(outs, axis=0)
    partial_out = lax.dot_general(
        attended,
        gathered[:, o_off:ck_off],
        (((1,), (1,)), ((), ())),
        preferred_element_type=jnp.float32,
    )
    partial_out = from_gather_order(partial_out.astype(jnp.bfloat16), 1, sizes)
    mixed = lax.psum_scatter(
        partial_out.reshape(requests, rows, width),
        FSDP,
        scatter_dimension=2,
        tiled=True,
    )
    return (mixed, new_keys, new_values)


def solution(mesh):
    n_fsdp = mesh.shape["fsdp"]
    n_seq = mesh.shape["seq"]
    n_core = 2
    n_zlo = n_fsdp // n_core
    ny = 4
    nz = 2
    nx = n_seq // (ny * nz)
    fine = Mesh(mesh.devices.reshape(n_zlo, n_core, nx, nz, ny), ("z_lo", "core", "x", "z_hi", "y"))
    placed = (
        P(None, SEQ, None),
        P(),
        P(),
        P(None, SEQ, FSDP, None),
        P(None, SEQ, FSDP, None),
        P(SEQ, FSDP),
        P(SEQ, FSDP),
        P(SEQ, FSDP),
        P(SEQ, FSDP),
    )

    def body(*args):
        return shards((nx, nz, ny), *args)

    return jax.shard_map(
        body,
        mesh=fine,
        in_specs=placed,
        out_specs=(
            P(None, SEQ, FSDP),
            P(None, SEQ, FSDP, None),
            P(None, SEQ, FSDP, None),
        ),
        check_vma=False,
    )
```

time: 339 us -> 391 us (1.15); the launches traced: 338 us -> 386 us
  local copies, waits for them, and re-layouts: 46.1 us -> 83 us
  matrix products: 40.8 us -> 62.2 us
  waiting for transfers between devices: 180 us -> 162 us
  other arithmetic: 24.8 us -> 36.8 us
  blocking collectives: 32.6 us -> 20.7 us
  starting transfers between devices: 0.12 us -> 6.12 us
    broadcast_in_dim x0 -> x8, local copies, waits for them, and re-layouts: none -> 30.2 us  [attend_block(): scores = jnp.where(visible, scores, NEGATIVE)]
    dot_general x0 -> x4, local copies, waits for them, and re-layouts: none -> 28.9 us  [attend_block(): jnp.dot(weights.astype(jnp.bfloat16).reshape(queries.shape[0], -1), value...]
    dot_general x6 -> x10, matrix products: 40.8 us -> 62.2 us  [the longest x4 27.1 us: attend_block(): scores = jnp.dot(queries, keys.T, preferred_element_type=jnp.float32)]
    all_gather x2, waiting for transfers between devices: 139 us -> 118 us  [xy_gather(): gathered = lax.all_gather(pair, ('x', 'y'), axis=0, tiled=False)]
    slice x7 -> x3, local copies, waits for them, and re-layouts: 19.1 us -> 0.69 us  [the longest x1 0.66 us: shards(): length = cached_len[r]]
    convert_element_type x0 -> x2, other arithmetic: none -> 16.7 us  [attend_block(): weights.astype(jnp.bfloat16).reshape(queries.shape[0], -1)]
    all_gather x2 -> x1, blocking collectives: 32.6 us -> 20.7 us  [z_first_pair(): return lax.all_gather(piece, 'z_hi', axis=0, tiled=False)]
    another operation x1 -> x8, local copies, waits for them, and re-layouts: 0.07 us -> 8.29 us  [the longest x1 4.47 us: shards(): partial_out.reshape(requests, rows, width)]
  transfers between devices with their start and end apart: 3 -> 4, of which waited for: 3 -> 4; matrix products, arithmetic and copies ran while one was open for 10% -> 14% of each run, Pallas kernels for 0% -> 0%
where the time goes in v2:
time: 391 us; the launch traced here: 386 us
  waiting for transfers between devices  162 us (41%)
  local copies, waits for them, and re-layouts  83 us (21%)
  matrix products  62.2 us (16%)
  other arithmetic  36.8 us (9%)
  blocking collectives  20.7 us (5%)
  between operations  14.4 us (4%)
  starting transfers between devices  6.12 us (2%)
    all_gather x2, waiting for transfers between devices, xy_gather(): gathered = lax.all_gather(pair, ('x', 'y'), axis=0, tiled=False)  118 us
    reduce_scatter x1, waiting for transfers between devices, shards(): lax.psum_scatter(partial_out.reshape(requests, rows, width), FSDP, scatte...  41.3 us
    broadcast_in_dim x8, local copies, waits for them, and re-layouts, attend_block(): scores = jnp.where(visible, scores, NEGATIVE)  30.2 us
    dot_general x4, local copies, waits for them, and re-layouts, attend_block(): jnp.dot(weights.astype(jnp.bfloat16).reshape(queries.shape[0], -1), value...  28.9 us
    dot_general x4, matrix products, attend_block(): scores = jnp.dot(queries, keys.T, preferred_element_type=jnp.float32)  27.1 us
    dot_general x4, matrix products, attend_block(): jnp.dot(weights.astype(jnp.bfloat16).reshape(queries.shape[0], -1), value...  25.1 us
    all_gather x1, blocking collectives, z_first_pair(): return lax.all_gather(piece, 'z_hi', axis=0, tiled=False)  20.7 us
    convert_element_type x2, other arithmetic, attend_block(): weights.astype(jnp.bfloat16).reshape(queries.shape[0], -1)  16.7 us
  transfers between devices with their start and end apart: 4, of which 4 were waited for; matrix products, arithmetic and copies ran while one was open for 14% of the time, Pallas kernels for 0%

profile of v2, /device:TPU:6, one launch (start us, length us, event | category | flops | bytes accessed | tf_op | source)
XLA Modules:
  0.0 385.6 jit_solution(17159304724525152378)
XLA Ops:
  7.2 0.9 constant_dynamic-update-slice_fusion.3
  8.1 0.9 copy.90
  9.0 0.9 copy.91
  10.0 0.8 constant_dynamic-update-slice_fusion.2
  10.7 0.8 constant_dynamic-update-slice_fusion.1
  11.5 0.9 constant_dynamic-update-slice_fusion
  12.4 20.7 %all-gather = bf16[256,1792]{1,0:T(8,128)(2,1)} all-gather(bf16[128,1792]{1,0:T(8,128)(2,1)S(1)} %bitcast_dynamic-update-slice_fusion), channel_id=2, replica_groups=mesh['z_lo'=4,'core'=2,'x'=4,'z_hi'=2,'y'=4] {'z_hi'}, dimensions={0}, use_global_device_ids=true | all-gather | bytes 1376256 | tf_op jit(solution)/shard_map/all_gather | solution.py:20
  33.2 3.2 reshape_reshape.6
  36.5 2.8 copy.93
  39.2 108.1 %all-gather.7.cloned.1.call-done = bf16[32,128,1792]{2,1,0:T(8,128)(2,1)} async-done(((bf16[2,128,1792]{2,1,0:T(8,128)(2,1)}), bf16[32,128,1792]{2,1,0:T(8,128)(2,1)}) %all-gather.7.cloned.1.call-update) | async-done | bytes 14680080 | tf_op jit(solution)/shard_map/all_gather | solution.py:24
  147.3 5.3 %fusion.28 = bf16[256,768]{1,0:T(8,128)(2,1)S(1)} fusion(bf16[256,4096]{0,1:T(8,128)(2,1)} %bitcast.76, bf16[4096,1792]{1,0:T(8,128)(2,1)} %bitcast.83), kind=kOutput, calls=%fused_computation.41 | convolution fusion | flops 1610809344 | bytes 8781824 | tf_op jit(solution)/shard_map/dot_general | solution.py:96
  152.7 0.1 copy.97
  152.8 0.1 copy.98
  152.9 5.8 %collective-permute-start = (bf16[128,512]{0,1:T(8,128)(2,1)S(1)}, bf16[128,512]{0,1:T(8,128)(2,1)S(1)}, u32[]{:S(2)}, u32[]{:S(2)}) collective-permute-start(bf16[128,512]{0,1:T(8,128)(2,1)S(1)} %pad_maximum_fusion), channel_id=1, source_target_pairs={{0,4},{4,0},{1,5},{5,1},{2,6},{6,2},{3,7},{7,3},{8,12},{12,8},{9,1... | collective-permute-start | bytes 393224 | tf_op jit(solution)/shard_map/ppermute | solution.py:18
  158.8 0.1 copy.99
  158.9 3.3 collective-permute-done
  162.2 0.1 copy.100
  162.3 0.7 maximum_select_fusion
  163.1 0.2 reduce-scatter.2.cloned.1.call-start
  163.4 1.0 fusion.23
  164.4 2.4 broadcast_in_dim.76
  166.9 4.5 %broadcast_in_dim.77 = pred[512,4096]{1,0:T(32,128)(4,1)} reshape(pred[128,4,4096]{2,1,0:T(4,128)(4,1)S(1)} %broadcast_in_dim.76) | data formatting | bytes 4194304 | tf_op jit(solution)/shard_map/jit(_where)/broadcast_in_dim | solution.py:53
  171.3 0.7 fusion.82
  172.0 1.3 add_add_fusion.1
  173.3 1.3 broadcast_compare_fusion.2
  174.5 0.9 or_and_fusion.1
  175.4 2.4 broadcast_in_dim.72
  177.9 4.4 %broadcast_in_dim.73 = pred[512,4096]{1,0:T(32,128)(4,1)} reshape(pred[128,4,4096]{2,1,0:T(4,128)(4,1)S(1)} %broadcast_in_dim.72) | data formatting | bytes 4194304 | tf_op jit(solution)/shard_map/jit(_where)/broadcast_in_dim | solution.py:53
  182.3 2.4 broadcast_in_dim.80
  184.7 4.5 %broadcast_in_dim.81 = pred[512,4096]{1,0:T(32,128)(4,1)} reshape(pred[128,4,4096]{2,1,0:T(4,128)(4,1)S(1)} %broadcast_in_dim.80) | data formatting | bytes 4194304 | tf_op jit(solution)/shard_map/jit(_where)/broadcast_in_dim | solution.py:53
  189.2 3.7 broadcast_in_dim.78
  192.9 5.9 %broadcast_in_dim.79 = pred[512,4096]{1,0:T(32,128)(4,1)S(1)} reshape(pred[128,4,4096]{2,1,0:T(4,128)(4,1)} %broadcast_in_dim.78) | data formatting | bytes 4194304 | tf_op jit(solution)/shard_map/jit(_where)/broadcast_in_dim | solution.py:53
  198.9 0.1 reshape_squeeze.6
  199.0 0.1 reshape_squeeze.7
  199.1 7.0 %fusion = (f32[512]{0:T(512)S(1)}, f32[512,4096]{1,0:T(8,128)}) fusion(pred[512,4096]{1,0:T(32,128)(4,1)} %broadcast_in_dim.73, bf16[512,128]{1,0:T(8,128)(2,1)S(1)} %reshape_squeeze.6, bf16[4096,1792]{1,0:T(8,128)(2,1)} %bitcast.84), kind=kOutput, calls=%fused_computation.8 | convolution fusion | flops 543161856 | bytes 11667456 | tf_op jit(solution)/shard_map/dot_general | solution.py:49
  206.0 6.3 %fusion.2 = (f32[512]{0:T(512)S(1)}, f32[512,4096]{1,0:T(8,128)}) fusion(pred[512,4096]{1,0:T(32,128)(4,1)S(1)} %broadcast_in_dim.79, bf16[512,128]{1,0:T(8,128)(2,1)S(1)} %reshape_squeeze.7, bf16[4096,1792]{1,0:T(8,128)(2,1)} %bitcast.85), kind=kOutput, calls=%fused_computation.10 | convolution fusion | flops 543161856 | bytes 11667456 | tf_op jit(solution)/shard_map/dot_general | solution.py:49
  212.3 9.7 %all-gather.5.cloned.1.call-done = bf16[16,2,128,512]{3,2,1,0:T(8,128)(2,1)} async-done(((bf16[1,2,128,512]{3,2,1,0:T(8,128)(2,1)}), bf16[16,2,128,512]{3,2,1,0:T(8,128)(2,1)}) %all-gather.5.cloned.1.call-update) | async-done | bytes 4194320 | tf_op jit(solution)/shard_map/all_gather | solution.py:24
  222.0 6.9 %fusion.1 = (f32[512]{0:T(512)S(1)}, f32[512,4096]{1,0:T(8,128)}) fusion(pred[512,4096]{1,0:T(32,128)(4,1)} %broadcast_in_dim.77, bf16[512,128]{1,0:T(8,128)(2,1)S(1)} %reshape_squeeze.6, bf16[4096,512]{1,0:T(8,128)(2,1)} %bitcast.77), kind=kOutput, calls=%fused_computation.9 | convolution fusion | flops 543161856 | bytes 11667456 | tf_op jit(solution)/shard_map/dot_general | solution.py:49
  228.9 0.1 reduce_max.42
  229.0 8.6 %fusion.9 = (bf16[512,4096]{1,0:T(8,128)(2,1)}, f32[512]{0:T(512)S(1)}) fusion(pred[512,4096]{1,0:T(32,128)(4,1)} %broadcast_in_dim.77, f32[512,4096]{1,0:T(8,128)} %get-tuple-element.58, f32[512]{0:T(512)S(1)} %get-tuple-element.42), kind=kLoop, calls=%fused_computation.18 | loop fusion | flops 12582400 | bytes 14684160 | tf_op jit(solution)/shard_map/convert_element_type | solution.py:59
  237.6 7.2 %dot_general.43 = bf16[128,4,4096]{2,1,0:T(4,128)(2,1)} reshape(bf16[512,4096]{1,0:T(8,128)(2,1)} %get-tuple-element.22) | data formatting | bytes 8388608 | tf_op jit(solution)/shard_map/dot_general | solution.py:58
  244.8 0.1 reduce_sum.47
  245.0 0.1 max_broadcast_in_dim.45
  245.1 8.0 %fusion.6 = (f32[512]{0:T(512)S(1)}, bf16[512,4096]{1,0:T(8,128)(2,1)}) fusion(pred[512,4096]{1,0:T(32,128)(4,1)} %broadcast_in_dim.73, f32[512,4096]{1,0:T(8,128)} %get-tuple-element.60, f32[512]{0:T(512)S(1)} %get-tuple-element.43), kind=kLoop, calls=%fused_computation.15 | loop fusion | flops 12582400 | bytes 14684160 | tf_op jit(solution)/shard_map/reduce_sum | solution.py:57
  253.1 0.1 reduce_sum.45
  253.5 7.2 %dot_general.40 = bf16[128,4,4096]{2,1,0:T(4,128)(2,1)} reshape(bf16[512,4096]{1,0:T(8,128)(2,1)} %get-tuple-element.25) | data formatting | bytes 8388608 | tf_op jit(solution)/shard_map/dot_general | solution.py:58
  260.7 7.0 %fusion.3 = (f32[512]{0:T(512)S(1)}, f32[512,4096]{1,0:T(8,128)}) fusion(pred[512,4096]{1,0:T(32,128)(4,1)} %broadcast_in_dim.81, bf16[512,128]{1,0:T(8,128)(2,1)S(1)} %reshape_squeeze.7, bf16[4096,512]{1,0:T(8,128)(2,1)} %bitcast.78), kind=kOutput, calls=%fused_computation.11 | convolution fusion | flops 543161856 | bytes 11667456 | tf_op jit(solution)/shard_map/dot_general | solution.py:49
  267.6 0.1 reduce_max.45
  267.8 8.0 %fusion.13 = (bf16[512,4096]{1,0:T(8,128)(2,1)}, f32[512]{0:T(512)S(1)}) fusion(pred[512,4096]{1,0:T(32,128)(4,1)} %broadcast_in_dim.81, f32[512,4096]{1,0:T(8,128)} %get-tuple-element.54, f32[512]{0:T(512)S(1)} %get-tuple-element.45), kind=kLoop, calls=%fused_computation.22 | loop fusion | flops 12582400 | bytes 14684160 | tf_op jit(solution)/shard_map/convert_element_type | solution.py:59
  275.8 7.2 %dot_general.49 = bf16[128,4,4096]{2,1,0:T(4,128)(2,1)} reshape(bf16[512,4096]{1,0:T(8,128)(2,1)} %get-tuple-element.26) | data formatting | bytes 8388608 | tf_op jit(solution)/shard_map/dot_general | solution.py:58
  283.0 0.1 reduce_sum.51
  283.1 0.1 max_broadcast_in_dim.47
  283.3 6.9 %fusion.10 = (f32[512]{0:T(512)S(1)}, bf16[512,4096]{1,0:T(8,128)(2,1)}) fusion(pred[512,4096]{1,0:T(32,128)(4,1)S(1)} %broadcast_in_dim.79, f32[512,4096]{1,0:T(8,128)} %get-tuple-element.56, f32[512]{0:T(512)S(1)} %get-tuple-element.46), kind=kLoop, calls=%fused_computation.19 | loop fusion | flops 12582400 | bytes 14684160 | tf_op jit(solution)/shard_map/reduce_sum | solution.py:57
  290.1 0.1 reduce_sum.49
  290.5 7.4 %dot_general.46 = bf16[128,4,4096]{2,1,0:T(4,128)(2,1)} reshape(bf16[512,4096]{1,0:T(8,128)(2,1)} %get-tuple-element.29) | data formatting | bytes 8388608 | tf_op jit(solution)/shard_map/dot_general | solution.py:58
  297.9 7.2 %fusion.46 = f32[128,4,128]{0,2,1:T(8,128)S(1)} fusion(bf16[128,4,4096]{2,1,0:T(4,128)(2,1)} %dot_general.40, bf16[4096,1792]{1,0:T(8,128)(2,1)} %bitcast.86, f32[128,4]{0,1:T(4,128)S(1)} %get-tuple-element.19, f32[128,4]{0,1:T(4,128)S(1)} %get-tuple-element.41), kind=kOutput, calls=%fused_computation.47 | convolution fusion | flops 537001984 | bytes 5509120 | tf_op jit(solution)/shard_map/dot_general | solution.py:58
  305.1 5.9 %fusion.58 = bf16[128,4,128]{0,2,1:T(8,128)(2,1)S(1)} fusion(f32[128,4,128]{0,2,1:T(8,128)S(1)} %fusion.46, bf16[128,4,4096]{2,1,0:T(4,128)(2,1)S(1)} %copy-done, bf16[4096,512]{1,0:T(8,128)(2,1)} %bitcast.79, f32[128,4]{0,1:T(4,128)S(1)} %get-tuple-element.18), kind=kOutput, calls=%fused_computation.51 | convolution fusion | flops 537067520 | bytes 5638144 | tf_op jit(solution)/shard_map/dot_general | solution.py:58
  311.1 6.1 %fusion.43 = f32[128,4,128]{0,2,1:T(8,128)S(1)} fusion(bf16[128,4,4096]{2,1,0:T(4,128)(2,1)S(1)} %copy-done.2, bf16[4096,1792]{1,0:T(8,128)(2,1)} %bitcast.87, f32[128,4]{0,1:T(4,128)S(1)} %get-tuple-element.21, f32[128,4]{0,1:T(4,128)S(1)} %get-tuple-element.44), kind=kOutput, calls=%fused_computation.46 | convolution fusion | flops 537001984 | bytes 5509120 | tf_op jit(solution)/shard_map/dot_general | solution.py:58
  317.2 5.8 %fusion.52 = bf16[128,4,128]{0,2,1:T(8,128)(2,1)S(1)} fusion(f32[128,4,128]{0,2,1:T(8,128)S(1)} %fusion.43, bf16[128,4,4096]{2,1,0:T(4,128)(2,1)S(1)} %copy-done.1, bf16[4096,512]{1,0:T(8,128)(2,1)} %bitcast.80, f32[128,4]{0,1:T(4,128)S(1)} %get-tuple-element.20), kind=kOutput, calls=%fused_computation.49 | convolution fusion | flops 537067520 | bytes 5638144 | tf_op jit(solution)/shard_map/dot_general | solution.py:58
  323.0 4.8 %convolution_convert_fusion = bf16[256,4096]{1,0:T(8,128)(2,1)} fusion(bf16[4096,1792]{1,0:T(8,128)(2,1)} %bitcast.88, bf16[128,512]{0,1:T(8,128)(2,1)S(1)} %bitcast.105, bf16[128,512]{0,1:T(8,128)(2,1)S(1)} %bitcast.104), kind=kOutput, calls=%fused_computation.14 | convolution fusion | flops 1075314688 | bytes 6553600 | tf_op jit(solution)/shard_map/dot_general | solution.py:149
  327.8 3.2 reshape.657
  331.1 2.1 copy.116
  333.1 4.5 %reshape_reshape.7 = bf16[2,128,4096]{2,1,0:T(8,128)(2,1)} reshape(bf16[256,4,2,4,128]{4,3,2,1,0:T(4,128)(2,1)} %copy.116) | data formatting | bytes 4194304 | tf_op jit(solution)/shard_map/reshape;reshape | solution.py:157
  337.6 41.3 %reduce-scatter.2.cloned.1.call-done = bf16[2,128,512]{2,1,0:T(8,128)(2,1)} async-done(((bf16[2,128,4096]{2,1,0:T(8,128)(2,1)}), bf16[2,128,512]{2,1,0:T(8,128)(2,1)}) %reduce-scatter.2.cloned.1.call-update) | async-done | bytes 262160 | tf_op jit(solution)/shard_map/reduce_scatter | solution.py:156
  (42 shorter events, 0.9 us)
Async XLA Ops:
  7.2 140.2 %all-gather.7.cloned.1.call-start = ((), (), s32[]{:S(2)}) async-start(), calls=%async_computation.3 | async-start | bytes 15597568 | tf_op jit(solution)/shard_map/all_gather | solution.py:24
  33.2 188.8 %all-gather.5.cloned.1.call-start = ((), (), s32[]{:S(2)}) async-start(), calls=%async_computation.1 | async-start | bytes 4456448 | tf_op jit(solution)/shard_map/all_gather | solution.py:24
  147.3 16.0 %copy-start.5 = (s32[2,4096]{1,0:T(2,128)S(1)}, s32[2,4096]{1,0:T(2,128)}, u32[]{:S(2)}) copy-start(s32[2,4096]{1,0:T(2,128)} %param.10) | copy-start | bytes 98308
  152.6 6.1 %copy-start.3 = (bf16[256,128]{1,0:T(8,128)(2,1)}, bf16[256,128]{1,0:T(8,128)(2,1)S(1)}, u32[]{:S(2)}) copy-start(bf16[256,128]{1,0:T(8,128)(2,1)S(1)} %get-tuple-element.32) | copy-start | bytes 196612
  152.6 6.1 %copy-start.4 = (bf16[256,128]{1,0:T(8,128)(2,1)}, bf16[256,128]{1,0:T(8,128)(2,1)S(1)}, u32[]{:S(2)}) copy-start(bf16[256,128]{1,0:T(8,128)(2,1)S(1)} %get-tuple-element.33) | copy-start | bytes 196612
  152.9 9.3 %collective-permute-start = (bf16[128,512]{0,1:T(8,128)(2,1)S(1)}, bf16[128,512]{0,1:T(8,128)(2,1)S(1)}, u32[]{:S(2)}, u32[]{:S(2)}) collective-permute-start(bf16[128,512]{0,1:T(8,128)(2,1)S(1)} %pad_maximum_fusion), channel_id=1, source_target_pairs={{0,4},{4,0},{1,5},{5,1},{2,6},{6,2},{3,7},{7,3},{8,12},{12,8},{9,1... | collective-permute-start | bytes 393224 | tf_op jit(solution)/shard_map/ppermute | solution.py:18
  163.0 8.3 %copy-start.6 = (s32[2]{0:T(128)S(1)}, s32[2]{0:T(128)}, u32[]{:S(2)}) copy-start(s32[2]{0:T(128)} %param.11) | copy-start | bytes 28
  163.1 215.8 %reduce-scatter.2.cloned.1.call-start = ((), (), s32[]{:S(2)}) async-start(), calls=%async_computation.2 | async-start | bytes 2359296 | tf_op jit(solution)/shard_map/reduce_scatter | solution.py:156
  297.8 7.2 %copy-start = (bf16[128,4,4096]{2,1,0:T(4,128)(2,1)S(1)}, bf16[128,4,4096]{2,1,0:T(4,128)(2,1)}, u32[]{:S(2)}) copy-start(bf16[128,4,4096]{2,1,0:T(4,128)(2,1)} %dot_general.43) | copy-start | bytes 12582916
  305.1 6.0 %copy-start.2 = (bf16[128,4,4096]{2,1,0:T(4,128)(2,1)S(1)}, bf16[128,4,4096]{2,1,0:T(4,128)(2,1)}, u32[]{:S(2)}) copy-start(bf16[128,4,4096]{2,1,0:T(4,128)(2,1)} %dot_general.46) | copy-start | bytes 12582916
  311.0 6.2 %copy-start.1 = (bf16[128,4,4096]{2,1,0:T(4,128)(2,1)S(1)}, bf16[128,4,4096]{2,1,0:T(4,128)(2,1)}, u32[]{:S(2)}) copy-start(bf16[128,4,4096]{2,1,0:T(4,128)(2,1)} %dot_general.49) | copy-start | bytes 12582916
Sparse Core Ops, SparseCore 0:
  33.3 113.9 all-gather.6
  163.2 58.7 all-gather.4
  337.7 41.0 reduce-scatter.1

commit v3 on v1

--- a/solution.py
+++ b/solution.py
@@ -32,13 +32,32 @@
     return (top_new, denom_new, numer_new)
 
 
-def gather_seq(piece, sizes):
-    rows, cols = piece.shape
+def gather_seq(piece, z_index, use_permute):
+    if use_permute:
+        other = lax.ppermute(piece, "z_hi", [(0, 1), (1, 0)])
+        pair = jnp.where(z_index == 0, jnp.stack([piece, other]), jnp.stack([other, piece]))
+    else:
+        pair = lax.all_gather(piece, "z_hi", axis=0, tiled=False)
+    gathered = lax.all_gather(pair, ("x", "y"), axis=0, tiled=False)
+    return gathered.reshape(-1, piece.shape[-1])
+
+
+def to_gather_order(array, axis, sizes):
     nx, nz, ny = sizes
-    piece = lax.all_gather(piece, "z_hi", axis=0, tiled=False)
-    piece = lax.all_gather(piece, ("x", "y"), axis=0, tiled=False)
-    piece = piece.reshape(nx, ny, nz, rows, cols).transpose(0, 2, 1, 3, 4)
-    return piece.reshape(nx * nz * ny * rows, cols)
+    shape = array.shape
+    split = shape[:axis] + (nx, nz, ny, shape[axis] // (nx * nz * ny)) + shape[axis + 1 :]
+    perm = list(range(len(split)))
+    perm[axis + 1], perm[axis + 2] = perm[axis + 2], perm[axis + 1]
+    return jnp.transpose(array.reshape(split), perm).reshape(shape)
+
+
+def from_gather_order(array, axis, sizes):
+    nx, nz, ny = sizes
+    shape = array.shape
+    split = shape[:axis] + (nx, ny, nz, shape[axis] // (nx * nz * ny)) + shape[axis + 1 :]
+    perm = list(range(len(split)))
+    perm[axis + 1], perm[axis + 2] = perm[axis + 2], perm[axis + 1]
+    return jnp.transpose(array.reshape(split), perm).reshape(shape)
 
 
 def shards(
@@ -49,11 +68,12 @@
     kv_local = cache_keys.shape[2]
     group_size = w_query.shape[1] // (kv_local * head_size)
     nx, nz, ny = sizes
-    seq_index = (lax.axis_index("x") * nz + lax.axis_index("z_hi")) * ny + lax.axis_index("y")
+    z_index = lax.axis_index("z_hi")
+    seq_index = (lax.axis_index("x") * nz + z_index) * ny + lax.axis_index("y")
     seq_count = nx * nz * ny
     window_len = rows * seq_count // 2
     my_positions = lax.dynamic_slice_in_dim(positions, seq_index * rows, rows, 1)
-    flat_tokens = tokens.reshape(requests * rows, width)
+    flat_tokens = to_gather_order(tokens.reshape(requests * rows, width), 1, sizes)
 
     q_cols = w_query.shape[1]
     k_cols = w_key.shape[1]
@@ -63,7 +83,7 @@
     packed = jnp.concatenate(
         [w_query, w_key, w_value, w_out_t, cache_k_local, cache_v_local], axis=1
     )
-    gathered = gather_seq(packed, sizes)
+    gathered = gather_seq(packed, z_index, False)
     total_rows = gathered.shape[0]
     offs = [0]
     for c in (q_cols, k_cols, k_cols, o_cols, cache_k_local.shape[1], cache_v_local.shape[1]):
@@ -88,7 +108,7 @@
         jnp.zeros((requests, kv_local, group_size, rows), jnp.float32),
         jnp.zeros((requests, kv_local, group_size, rows, head_size), jnp.float32),
     )
-    key_pos = jnp.arange(total_rows, dtype=jnp.int32)
+    key_pos = to_gather_order(jnp.arange(total_rows, dtype=jnp.int32), 0, sizes)
     key_pos = key_pos[None, None, :]
     allowed = (key_pos < lengths[:, :, None]) & (
         (key_pos < SINKS) | (key_pos > window_floor[:, :, None])
@@ -97,7 +117,7 @@
 
     new_k_local = jnp.transpose(new_keys, (1, 0, 2, 3)).reshape(rows, -1)
     new_v_local = jnp.transpose(new_values, (1, 0, 2, 3)).reshape(rows, -1)
-    new_gathered = gather_seq(jnp.concatenate([new_k_local, new_v_local], axis=1), sizes)
+    new_gathered = gather_seq(jnp.concatenate([new_k_local, new_v_local], axis=1), z_index, True)
     half = new_k_local.shape[1]
     new_k_full = jnp.transpose(
         new_gathered[:, :half].reshape(total_rows, requests, kv_local, head_size), (1, 0, 2, 3)
@@ -105,7 +125,8 @@
     new_v_full = jnp.transpose(
         new_gathered[:, half:].reshape(total_rows, requests, kv_local, head_size), (1, 0, 2, 3)
     )
-    before = my_positions[:, :, None] - positions[:, None, :]
+    new_pos = to_gather_order(positions, 1, sizes)
+    before = my_positions[:, :, None] - new_pos[:, None, :]
     allowed = (before >= 0) & (before < window_len)
     running_state = attend_block(running_state, queries, new_k_full, new_v_full, allowed)
     top_final, denom_final, numer_final = running_state
@@ -119,8 +140,9 @@
         (((1,), (1,)), ((), ())),
         preferred_element_type=jnp.float32,
     )
+    partial_out = from_gather_order(partial_out.astype(jnp.bfloat16), 1, sizes)
     mixed = lax.psum_scatter(
-        partial_out.reshape(requests, rows, width).astype(jnp.bfloat16),
+        partial_out.reshape(requests, rows, width),
         FSDP,
         scatter_dimension=2,
         tiled=True,

time: 339 us -> 344 us (1.015)
  blocking collectives: 32.6 us -> 20.7 us
  local copies, waits for them, and re-layouts: 46.1 us -> 53.3 us
  starting transfers between devices: 0.12 us -> 6.12 us
  matrix products: 40.8 us -> 46.7 us
    all_gather x2 -> x1, blocking collectives: 32.6 us -> 20.7 us  [gather_seq(): pair = lax.all_gather(piece, 'z_hi', axis=0, tiled=False)]
    reshape x0 -> x5, local copies, waits for them, and re-layouts: none -> 8.28 us  [the longest x1 3.23 us: from_gather_order(): return jnp.transpose(array.reshape(split), perm).reshape(shape)]
    another operation x1 -> x3, local copies, waits for them, and re-layouts: 0.07 us -> 7.78 us  [the longest x1 4.48 us: shards(): partial_out.reshape(requests, rows, width)]
    ppermute x0 -> x1, starting transfers between devices: none -> 5.82 us  [gather_seq(): other = lax.ppermute(piece, 'z_hi', [(0, 1), (1, 0)])]
    transpose x2 -> x3, local copies, waits for them, and re-layouts: 10.2 us -> 5.03 us  [the longest x1 2.77 us: to_gather_order(): return jnp.transpose(array.reshape(split), perm).reshape(shape)]
    all_gather x2, waiting for transfers between devices: 139 us -> 134 us  [gather_seq(): gathered = lax.all_gather(pair, ('x', 'y'), axis=0, tiled=False)]
    slice x1 -> x0, local copies, waits for them, and re-layouts: 4.16 us -> none  [shards(): gathered[:, offs[5]:offs[6]]]
    dot_general x1, matrix products: 1.78 us -> 5.26 us  [shards(): qkv_sum = jnp.dot(flat_tokens, w_qkv, preferred_element_type=jnp.float32)]
  transfers between devices with their start and end apart: 3 -> 4, of which waited for: 3 -> 4; matrix products, arithmetic and copies ran while one was open for 10% -> 11% of each run, Pallas kernels for 0% -> 0%
where the time goes in v3:
time: 344 us; the launch traced here: 343 us
  waiting for transfers between devices  179 us (52%)
  local copies, waits for them, and re-layouts  53.3 us (15%)
  matrix products  46.7 us (14%)
  other arithmetic  23.7 us (7%)
  blocking collectives  20.7 us (6%)
  between operations  14.1 us (4%)
  starting transfers between devices  6.12 us (2%)
    all_gather x2, waiting for transfers between devices, gather_seq(): gathered = lax.all_gather(pair, ('x', 'y'), axis=0, tiled=False)  134 us
    reduce_scatter x1, waiting for transfers between devices, shards(): lax.psum_scatter(partial_out.reshape(requests, rows, width), FSDP, scatte...  41.3 us
    all_gather x1, blocking collectives, gather_seq(): pair = lax.all_gather(piece, 'z_hi', axis=0, tiled=False)  20.7 us
    dot_general x2, matrix products, attend_block(): jnp.einsum('rkgqp,rpkd->rkgqd', weights.astype(jnp.bfloat16), value_block...  19 us
    dot_general x2, matrix products, attend_block(): jnp.einsum('rqkgd,rpkd->rkgqp', queries, key_block, preferred_element_typ...  17.7 us
    reduce_sum x1, other arithmetic, attend_block(): denom_new = denom_old * rescale + jnp.sum(weights, axis=-1)  15.3 us
    unnamed x25, local copies, waits for them, and re-layouts  9.29 us
    slice x2, local copies, waits for them, and re-layouts, shards(): new_gathered[:, half:].reshape(total_rows, requests, kv_local, head_size)  7.4 us
  transfers between devices with their start and end apart: 4, of which 4 were waited for; matrix products, arithmetic and copies ran while one was open for 11% of the time, Pallas kernels for 0%

profile of v3, /device:TPU:6, one launch (start us, length us, event | category | flops | bytes accessed | tf_op | source)
XLA Modules:
  0.0 343.2 jit_solution(8853464136007864357)
XLA Ops:
  7.2 0.0 all-gather.7.cloned.1.call-start
  7.2 0.9 copy.61
  8.1 0.9 copy.62
  9.0 0.9 constant_dynamic-update-slice_fusion.3
  10.0 0.8 constant_dynamic-update-slice_fusion.2
  10.7 0.8 constant_dynamic-update-slice_fusion.1
  11.5 0.9 constant_dynamic-update-slice_fusion
  12.4 20.7 %all-gather = bf16[256,1792]{1,0:T(8,128)(2,1)} all-gather(bf16[128,1792]{1,0:T(8,128)(2,1)S(1)} %bitcast_dynamic-update-slice_fusion), channel_id=2, replica_groups=mesh['z_lo'=4,'core'=2,'x'=4,'z_hi'=2,'y'=4] {'z_hi'}, dimensions={0}, use_global_device_ids=true | all-gather | bytes 1376256 | tf_op jit(solution)/shard_map/all_gather | solution.py:40
  33.2 0.0 all-gather.7.cloned.1.call-update
  33.2 0.0 all-gather.5.cloned.1.call-start
  33.2 3.2 reshape_reshape.6
  36.5 2.8 copy.65
  39.3 108.1 %all-gather.7.cloned.1.call-done = bf16[32,128,1792]{2,1,0:T(8,128)(2,1)} async-done(((bf16[2,128,1792]{2,1,0:T(8,128)(2,1)}), bf16[32,128,1792]{2,1,0:T(8,128)(2,1)}) %all-gather.7.cloned.1.call-update) | async-done | bytes 14680080 | tf_op jit(solution)/shard_map/all_gather | solution.py:41
  147.3 0.0 copy-start.4
  147.3 5.3 %fusion.42 = bf16[256,768]{1,0:T(8,128)(2,1)S(1)} fusion(bf16[256,4096]{0,1:T(8,128)(2,1)} %bitcast.176, bf16[4096,1792]{1,0:T(8,128)(2,1)} %bitcast.177), kind=kOutput, calls=%fused_computation.34 | convolution fusion | flops 1610809344 | bytes 8781824 | tf_op jit(solution)/shard_map/dot_general | solution.py:98
  152.6 0.0 copy-start.1
  152.6 0.0 copy-start.2
  152.7 0.1 copy.71
  152.8 0.1 copy.70
  152.9 5.8 %collective-permute-start = (bf16[128,512]{0,1:T(8,128)(2,1)S(1)}, bf16[128,512]{0,1:T(8,128)(2,1)S(1)}, u32[]{:S(2)}, u32[]{:S(2)}) collective-permute-start(bf16[128,512]{0,1:T(8,128)(2,1)S(1)} %get-tuple-element.26), channel_id=1, source_target_pairs={{0,4},{4,0},{1,5},{5,1},{2,6},{6,2},{3,7},{7,3},{8,12},{12,8},{9,1... | collective-permute-start | bytes 393224 | tf_op jit(solution)/shard_map/ppermute | solution.py:37
  158.8 3.4 collective-permute-done
  162.2 0.9 copy.72
  163.1 0.0 all-gather.5.cloned.1.call-update
  163.1 0.2 reduce-scatter.2.cloned.1.call-start
  163.3 0.0 copy-done.3
  163.5 0.0 copy-done.4
  163.5 0.1 add_add_fusion
  163.6 0.1 broadcast_compare_fusion
  163.7 3.5 %fusion.17 = pred[2,128,4096]{1,2,0:T(8,128)(4,1)S(1)} fusion(s32[2,4096]{1,0:T(2,128)S(1)} %sub.70, s32[2,128]{1,0:T(2,128)S(1)} %get-tuple-element.18), kind=kLoop, calls=%fused_computation.22 | loop fusion | flops 4194304 | bytes 1082368 | tf_op jit(solution)/shard_map/and | solution.py:130
  167.2 4.6 %or_and_fusion = pred[2,128,4096]{1,2,0:T(8,128)(4,1)} fusion(s32[2,128]{1,0:T(2,128)S(1)} %get-tuple-element.17, s32[4096]{0:T(1024)S(1)} %bitcast.182, pred[4096]{0:T(1024)(128)(4,1)S(1)} %broadcast_compare_fusion.1, pred[2,4096]{1,0:T(4,128)(4,1)S(1)} %broadcast_compare_fusion), kind=kLoop, calls=%fused_computation.23 | loop fusion | flops 3145728 | bytes 1078272 | tf_op jit(solution)/shard_map/and | solution.py:113
  171.9 0.1 reshape.378
  171.9 4.5 %fusion.72 = (bf16[4096,256]{1,0:T(8,128)(2,1)}, bf16[4096,256]{1,0:T(8,128)(2,1)}) fusion(bf16[4096,1792]{1,0:T(8,128)(2,1)} %bitcast.178), kind=kLoop, calls=%fused_computation.68 | loop fusion | bytes 8388608 | tf_op jit(solution)/shard_map/slice | solution.py:93
  176.4 3.0 copy.90
  179.4 0.0 copy-done.1
  179.4 0.0 copy-done.2
  179.4 2.5 copy.64
  181.9 2.9 copy.92
  184.9 2.5 copy.67
  187.4 8.9 %fusion = (f32[2,4,128]{2,1,0:T(4,128)S(1)}, f32[2,4096,128,4]{2,1,3,0:T(8,128)}) fusion(pred[2,128,4096]{1,2,0:T(8,128)(4,1)} %or_and_fusion, bf16[2,128,4,128]{3,2,1,0:T(4,128)(2,1)S(1)} %reshape.378, bf16[4096,2,1,128]{3,0,1,2:T(8,128)(2,1)} %copy.64), kind=kOutput, calls=%fused_computation.4 | convolution fusion | flops 1086323712 | bytes 20189184 | tf_op jit(solution)/shard_map/rqkgd,rpkd->rkgqp/dot_general | solution.py:18
  196.2 25.8 %all-gather.5.cloned.1.call-done = bf16[16,2,128,512]{3,2,1,0:T(8,128)(2,1)} async-done(((bf16[1,2,128,512]{3,2,1,0:T(8,128)(2,1)}), bf16[16,2,128,512]{3,2,1,0:T(8,128)(2,1)}) %all-gather.5.cloned.1.call-update) | async-done | bytes 4194320 | tf_op jit(solution)/shard_map/all_gather | solution.py:41
  222.1 4.5 %fusion.73 = (bf16[4096,256]{1,0:T(8,128)(2,1)}, bf16[4096,256]{1,0:T(8,128)(2,1)}) fusion(bf16[4096,512]{1,0:T(8,128)(2,1)} %bitcast.174), kind=kLoop, calls=%fused_computation.69 | loop fusion | bytes 8388608 | tf_op jit(solution)/shard_map/slice | solution.py:126
  226.6 2.9 copy.76
  229.5 2.5 copy.77
  232.0 2.9 copy.73
  234.9 2.5 copy.74
  237.4 0.0 copy-start
  237.4 8.8 %fusion.1 = (f32[2,4,128]{2,1,0:T(4,128)S(1)}, f32[2,4096,128,4]{2,1,3,0:T(8,128)}) fusion(pred[2,128,4096]{1,2,0:T(8,128)(4,1)S(1)} %fusion.17, bf16[2,128,4,128]{3,2,1,0:T(4,128)(2,1)S(1)} %reshape.378, bf16[4096,2,1,128]{3,0,1,2:T(8,128)(2,1)} %copy.74), kind=kOutput, calls=%fused_computation.5 | convolution fusion | flops 1086323712 | bytes 20189184 | tf_op jit(solution)/shard_map/rqkgd,rpkd->rkgqp/dot_general | solution.py:18
  246.2 0.0 copy-done
  246.2 0.0 slice-start.2
  246.2 0.0 slice-start.3
  246.2 15.3 %fusion.2 = (f32[2,4,128]{2,1,0:T(4,128)S(1)}, f32[2,4,128]{2,1,0:T(4,128)S(1)}) fusion(f32[2,4096,128,4]{2,1,3,0:T(8,128)} %get-tuple-element.31, f32[2,4,128]{2,1,0:T(4,128)S(1)} %get-tuple-element.29, pred[2,128,4096]{1,2,0:T(8,128)(4,1)S(1)} %copy-done, f32[2,4,128]{2,1,0:T(4,128)S(1)} %get-tuple-element.28, f32[2,4096,128,4]{2,1,3,0:T(8,128)} %get-tuple-element.33, ...), kind=kLoop, calls=%fused_computation.6 | loop fusion | flops 41940992 | bytes 35667968 | tf_op jit(solution)/shard_map/reduce_sum | solution.py:25
  261.5 0.0 slice-done
  261.5 0.0 slice-done.1
  261.6 0.0 slice-done.2
  261.6 0.0 slice-done.3
  261.6 7.4 %fusion.37 = f32[2,4,128,128]{3,2,1,0:T(8,128)S(1)} fusion(bf16[4096,2,1,128]{3,0,1,2:T(8,128)(2,1)} %copy.67, f32[2,4096,128,4]{2,1,3,0:T(8,128)S(1)} %bitcast.167, f32[2,4,128]{2,1,0:T(4,128)S(1)} %get-tuple-element.29, pred[2,128,4096]{1,2,0:T(8,128)(4,1)S(1)} %copy-done, f32[2,4,128]{2,1,0:T(4,128)S(1)} %get-tuple-element.16, ...), kind=kOutput, calls=%fused_computation.33 | convolution fusion | flops 1094975488 | bytes 20459520 | tf_op jit(solution)/shard_map/rkgqp,rpkd->rkgqd/dot_general | solution.py:26
  269.0 11.6 %fusion.55 = bf16[2,128,1,4,128]{4,1,3,0,2:T(8,128)(2,1)S(1)} fusion(f32[2,4,128,128]{3,2,1,0:T(8,128)S(1)} %fusion.37, bf16[4096,2,1,128]{3,0,1,2:T(8,128)(2,1)} %copy.77, f32[2,4096,128,4]{2,1,3,0:T(8,128)} %get-tuple-element.33, f32[2,4,128]{2,1,0:T(4,128)S(1)} %get-tuple-element.28, pred[2,128,4096]{1,2,0:T(8,128)(4,1)S(1)} %fusion.17, ...), kind=kOutput, calls=%fused_computation.37 | convolution fusion | flops 1095106560 | bytes 20717568 | tf_op jit(solution)/shard_map/rkgqp,rpkd->rkgqd/dot_general | solution.py:26
  280.6 0.2 copy.79
  280.8 4.8 %convolution_convert_fusion = bf16[256,4096]{1,0:T(8,128)(2,1)} fusion(bf16[4096,1792]{1,0:T(8,128)(2,1)} %bitcast.179, bf16[32,8,4,128]{3,2,1,0:T(4,128)(2,1)S(1)} %bitcast.183), kind=kOutput, calls=%fused_computation.20 | convolution fusion | flops 1074790400 | bytes 6553600 | tf_op jit(solution)/shard_map/dot_general | solution.py:137
  285.6 3.2 reshape.394
  288.9 2.1 copy.80
  290.9 4.5 %reshape_reshape.7 = bf16[2,128,4096]{2,1,0:T(8,128)(2,1)} reshape(bf16[256,4,2,4,128]{4,3,2,1,0:T(4,128)(2,1)} %copy.80) | data formatting | bytes 4194304 | tf_op jit(solution)/shard_map/reshape;reshape | solution.py:145
  295.4 0.0 reduce-scatter.2.cloned.1.call-update
  295.4 41.3 %reduce-scatter.2.cloned.1.call-done = bf16[2,128,512]{2,1,0:T(8,128)(2,1)} async-done(((bf16[2,128,4096]{2,1,0:T(8,128)(2,1)}), bf16[2,128,512]{2,1,0:T(8,128)(2,1)}) %reduce-scatter.2.cloned.1.call-update) | async-done | bytes 262160 | tf_op jit(solution)/shard_map/reduce_scatter | solution.py:144
  (17 shorter events, 0.2 us)
Async XLA Ops:
  7.2 140.2 %all-gather.7.cloned.1.call-start = ((), (), s32[]{:S(2)}) async-start(), calls=%async_computation.3 | async-start | bytes 15597568 | tf_op jit(solution)/shard_map/all_gather | solution.py:41
  33.2 188.9 %all-gather.5.cloned.1.call-start = ((), (), s32[]{:S(2)}) async-start(), calls=%async_computation.1 | async-start | bytes 4456448 | tf_op jit(solution)/shard_map/all_gather | solution.py:41
  147.3 16.0 %copy-start.3 = (s32[2,4096]{1,0:T(2,128)S(1)}, s32[2,4096]{1,0:T(2,128)}, u32[]{:S(2)}) copy-start(s32[2,4096]{1,0:T(2,128)} %param.10) | copy-start | bytes 98308
  147.3 16.1 %copy-start.4 = (s32[2]{0:T(128)S(1)}, s32[2]{0:T(128)}, u32[]{:S(2)}) copy-start(s32[2]{0:T(128)} %param.11) | copy-start | bytes 28
  152.6 26.8 %copy-start.1 = (bf16[256,128]{1,0:T(8,128)(2,1)}, bf16[256,128]{1,0:T(8,128)(2,1)S(1)}, u32[]{:S(2)}) copy-start(bf16[256,128]{1,0:T(8,128)(2,1)S(1)} %get-tuple-element.23) | copy-start | bytes 196612
  152.6 26.8 %copy-start.2 = (bf16[256,128]{1,0:T(8,128)(2,1)}, bf16[256,128]{1,0:T(8,128)(2,1)S(1)}, u32[]{:S(2)}) copy-start(bf16[256,128]{1,0:T(8,128)(2,1)S(1)} %get-tuple-element.24) | copy-start | bytes 196612
  152.9 9.3 %collective-permute-start = (bf16[128,512]{0,1:T(8,128)(2,1)S(1)}, bf16[128,512]{0,1:T(8,128)(2,1)S(1)}, u32[]{:S(2)}, u32[]{:S(2)}) collective-permute-start(bf16[128,512]{0,1:T(8,128)(2,1)S(1)} %get-tuple-element.26), channel_id=1, source_target_pairs={{0,4},{4,0},{1,5},{5,1},{2,6},{6,2},{3,7},{7,3},{8,12},{12,8},{9,1... | collective-permute-start | bytes 393224 | tf_op jit(solution)/shard_map/ppermute | solution.py:37
  163.1 173.6 %reduce-scatter.2.cloned.1.call-start = ((), (), s32[]{:S(2)}) async-start(), calls=%async_computation.2 | async-start | bytes 2359296 | tf_op jit(solution)/shard_map/reduce_scatter | solution.py:144
  237.4 8.8 %copy-start = (pred[2,128,4096]{1,2,0:T(8,128)(4,1)S(1)}, pred[2,128,4096]{1,2,0:T(8,128)(4,1)}, u32[]{:S(2)}) copy-start(pred[2,128,4096]{1,2,0:T(8,128)(4,1)} %or_and_fusion) | copy-start | bytes 3145732
  237.4 24.1 %slice-start = ((s8[16777216]{0:T(1024)(128)(4,1)}), s8[4194304]{0:T(1024)(128)(4,1)S(1)}, s32[]{:S(2)}) async-start(s8[16777216]{0:T(1024)(128)(4,1)} %bitcast.166), calls=%async_computation.4 | async-start | bytes 8388608
  237.4 24.1 %slice-start.1 = ((s8[16777216]{0:T(1024)(128)(4,1)}), s8[4194304]{0:T(1024)(128)(4,1)S(1)}, s32[]{:S(2)}) async-start(s8[16777216]{0:T(1024)(128)(4,1)} %bitcast.166), calls=%async_computation.5 | async-start | bytes 8388608
  246.2 15.3 %slice-start.2 = ((s8[16777216]{0:T(1024)(128)(4,1)}), s8[4194304]{0:T(1024)(128)(4,1)S(1)}, s32[]{:S(2)}) async-start(s8[16777216]{0:T(1024)(128)(4,1)} %bitcast.166), calls=%async_computation.6 | async-start | bytes 8388608
  246.2 15.3 %slice-start.3 = ((s8[16777216]{0:T(1024)(128)(4,1)}), s8[4194304]{0:T(1024)(128)(4,1)S(1)}, s32[]{:S(2)}) async-start(s8[16777216]{0:T(1024)(128)(4,1)} %bitcast.166), calls=%async_computation.7 | async-start | bytes 8388608
Sparse Core Ops, SparseCore 0:
  33.3 113.9 all-gather.6
  163.2 58.7 all-gather.4
  295.6 41.0 reduce-scatter.1

commit v4 on v3

--- a/solution.py
+++ b/solution.py
@@ -89,11 +89,8 @@
     for c in (q_cols, k_cols, k_cols, o_cols, cache_k_local.shape[1], cache_v_local.shape[1]):
         offs.append(offs[-1] + c)
     w_qkv = gathered[:, : offs[3]]
-    w_out_full = gathered[:, offs[3] : offs[4]]
-    cache_k_full = gathered[:, offs[4] : offs[5]].reshape(total_rows, requests, kv_local, head_size)
-    cache_v_full = gathered[:, offs[5] : offs[6]].reshape(total_rows, requests, kv_local, head_size)
-    cache_k_full = jnp.transpose(cache_k_full, (1, 0, 2, 3))
-    cache_v_full = jnp.transpose(cache_v_full, (1, 0, 2, 3))
+    w_out_full = from_gather_order(gathered[:, offs[3] : offs[4]], 0, sizes)
+    kv_cols = kv_local * head_size
 
     qkv_sum = jnp.dot(flat_tokens, w_qkv, preferred_element_type=jnp.float32)
     qkv = qkv_sum.astype(jnp.bfloat16)
@@ -101,48 +98,64 @@
     new_keys = qkv[:, q_cols : q_cols + k_cols].reshape(requests, rows, kv_local, head_size)
     new_values = qkv[:, q_cols + k_cols :].reshape(requests, rows, kv_local, head_size)
 
-    lengths = cached_len[:, None]
-    window_floor = lengths + my_positions - window_len
-    running_state = (
-        jnp.full((requests, kv_local, group_size, rows), NEGATIVE, jnp.float32),
-        jnp.zeros((requests, kv_local, group_size, rows), jnp.float32),
-        jnp.zeros((requests, kv_local, group_size, rows, head_size), jnp.float32),
-    )
-    key_pos = to_gather_order(jnp.arange(total_rows, dtype=jnp.int32), 0, sizes)
-    key_pos = key_pos[None, None, :]
-    allowed = (key_pos < lengths[:, :, None]) & (
-        (key_pos < SINKS) | (key_pos > window_floor[:, :, None])
-    )
-    running_state = attend_block(running_state, queries, cache_k_full, cache_v_full, allowed)
-
     new_k_local = jnp.transpose(new_keys, (1, 0, 2, 3)).reshape(rows, -1)
     new_v_local = jnp.transpose(new_values, (1, 0, 2, 3)).reshape(rows, -1)
     new_gathered = gather_seq(jnp.concatenate([new_k_local, new_v_local], axis=1), z_index, True)
     half = new_k_local.shape[1]
-    new_k_full = jnp.transpose(
-        new_gathered[:, :half].reshape(total_rows, requests, kv_local, head_size), (1, 0, 2, 3)
-    )
-    new_v_full = jnp.transpose(
-        new_gathered[:, half:].reshape(total_rows, requests, kv_local, head_size), (1, 0, 2, 3)
-    )
+
+    key_pos = to_gather_order(jnp.arange(total_rows, dtype=jnp.int32), 0, sizes)
+    key_pos = key_pos[None, None, :]
     new_pos = to_gather_order(positions, 1, sizes)
+    lengths = cached_len[:, None]
+    window_floor = lengths + my_positions - window_len
+    cache_allowed = (key_pos < lengths[:, :, None]) & (
+        (key_pos < SINKS) | (key_pos > window_floor[:, :, None])
+    )
     before = my_positions[:, :, None] - new_pos[:, None, :]
-    allowed = (before >= 0) & (before < window_len)
-    running_state = attend_block(running_state, queries, new_k_full, new_v_full, allowed)
-    top_final, denom_final, numer_final = running_state
-    attended = (numer_final / denom_final[..., None]).astype(jnp.bfloat16)
-    attended = jnp.transpose(attended, (0, 3, 1, 2, 4)).reshape(
-        requests * rows, kv_local * group_size * head_size
-    )
+    new_allowed = (before >= 0) & (before < window_len)
+
+    def block_of(source, offset, r):
+        piece = source[:, offset + r * kv_cols : offset + (r + 1) * kv_cols]
+        return piece.reshape(1, total_rows, kv_local, head_size)
+
+    attended_parts = []
+    for r in range(requests):
+        running_state = (
+            jnp.full((1, kv_local, group_size, rows), NEGATIVE, jnp.float32),
+            jnp.zeros((1, kv_local, group_size, rows), jnp.float32),
+            jnp.zeros((1, kv_local, group_size, rows, head_size), jnp.float32),
+        )
+        q_r = queries[r : r + 1]
+        running_state = attend_block(
+            running_state,
+            q_r,
+            block_of(gathered, offs[4], r),
+            block_of(gathered, offs[5], r),
+            cache_allowed[r : r + 1],
+        )
+        running_state = attend_block(
+            running_state,
+            q_r,
+            block_of(new_gathered, 0, r),
+            block_of(new_gathered, half, r),
+            new_allowed[r : r + 1],
+        )
+        _, denom_final, numer_final = running_state
+        attended_r = (numer_final / denom_final[..., None]).astype(jnp.bfloat16)
+        attended_parts.append(
+            jnp.transpose(attended_r, (0, 3, 1, 2, 4)).reshape(
+                rows, kv_local * group_size * head_size
+            )
+        )
+    attended = jnp.concatenate(attended_parts, axis=0)
     partial_out = lax.dot_general(
         attended,
         w_out_full,
         (((1,), (1,)), ((), ())),
         preferred_element_type=jnp.float32,
     )
-    partial_out = from_gather_order(partial_out.astype(jnp.bfloat16), 1, sizes)
     mixed = lax.psum_scatter(
-        partial_out.reshape(requests, rows, width),
+        partial_out.reshape(requests, rows, width).astype(jnp.bfloat16),
         FSDP,
         scatter_dimension=2,
         tiled=True,

time: 344 us -> 310 us (0.901)
  local copies, waits for them, and re-layouts: 53.3 us -> 19.2 us
  waiting for transfers between devices: 179 us -> 186 us
  other arithmetic: 23.7 us -> 17.9 us
    reshape x5 -> x0, local copies, waits for them, and re-layouts: 13.3 us -> none  [the longest x1 3.23 us: from_gather_order(): return jnp.transpose(array.reshape(split), perm).reshape(shape)]
    slice x5 -> x2, local copies, waits for them, and re-layouts: 14.8 us -> 2.48 us  [the longest x1 2.46 us: shards(): w_out_full = from_gather_order(gathered[:, offs[3]:offs[4]], 0, sizes)]
    all_gather x2, waiting for transfers between devices: 134 us -> 143 us  [gather_seq(): gathered = lax.all_gather(pair, ('x', 'y'), axis=0, tiled=False)]
    dot_general x2 -> x4, matrix products: 19 us -> 13.9 us  [attend_block(): jnp.einsum('rkgqp,rpkd->rkgqd', weights.astype(jnp.bfloat16), value_block...]
    another operation x2 -> x0, local copies, waits for them, and re-layouts: 4.55 us -> none  [the longest x1 4.48 us: shards(): partial_out.reshape(requests, rows, width)]
    reduce_sum x1 -> x2, other arithmetic: 15.3 us -> 10.9 us  [attend_block(): denom_new = denom_old * rescale + jnp.sum(weights, axis=-1)]
    unnamed x25 -> x19, local copies, waits for them, and re-layouts: 9.29 us -> 5.14 us
    dot_general x2 -> x4, matrix products: 17.7 us -> 20.9 us  [attend_block(): jnp.einsum('rqkgd,rpkd->rkgqp', queries, key_block, preferred_element_typ...]
  transfers between devices with their start and end apart: 4 -> 4, of which waited for: 4 -> 4; matrix products, arithmetic and copies ran while one was open for 11% -> 10% of each run, Pallas kernels for 0% -> 0%
where the time goes in v4:
time: 310 us; the launch traced here: 309 us
  waiting for transfers between devices  186 us (60%)
  matrix products  45 us (15%)
  blocking collectives  20.7 us (7%)
  local copies, waits for them, and re-layouts  19.2 us (6%)
  other arithmetic  17.9 us (6%)
  between operations  14.1 us (5%)
  starting transfers between devices  6.12 us (2%)
    all_gather x2, waiting for transfers between devices, gather_seq(): gathered = lax.all_gather(pair, ('x', 'y'), axis=0, tiled=False)  143 us
    reduce_scatter x1, waiting for transfers between devices, shards(): lax.psum_scatter(partial_out.reshape(requests, rows, width).astype(jnp.bf...  39.8 us
    dot_general x4, matrix products, attend_block(): jnp.einsum('rqkgd,rpkd->rkgqp', queries, key_block, preferred_element_typ...  20.9 us
    all_gather x1, blocking collectives, gather_seq(): pair = lax.all_gather(piece, 'z_hi', axis=0, tiled=False)  20.7 us
    dot_general x4, matrix products, attend_block(): jnp.einsum('rkgqp,rpkd->rkgqd', weights.astype(jnp.bfloat16), value_block...  13.9 us
    reduce_sum x2, other arithmetic, attend_block(): denom_new = denom_old * rescale + jnp.sum(weights, axis=-1)  10.9 us
  transfers between devices with their start and end apart: 4, of which 4 were waited for; matrix products, arithmetic and copies ran while one was open for 10% of the time, Pallas kernels for 0%

profile of v4, /device:TPU:6, one launch (start us, length us, event | category | flops | bytes accessed | tf_op | source)
XLA Modules:
  0.0 309.3 jit_solution(17844912889850095671)
XLA Ops:
  7.2 0.0 all-gather.7.cloned.1.call-start
  7.2 0.9 constant_dynamic-update-slice_fusion.3
  8.1 0.9 copy.75
  9.0 0.9 copy.76
  10.0 0.8 constant_dynamic-update-slice_fusion.2
  10.7 0.8 constant_dynamic-update-slice_fusion.1
  11.5 0.9 constant_dynamic-update-slice_fusion
  12.4 20.7 %all-gather = bf16[256,1792]{1,0:T(8,128)(2,1)} all-gather(bf16[128,1792]{1,0:T(8,128)(2,1)S(1)} %bitcast_dynamic-update-slice_fusion), channel_id=2, replica_groups=mesh['z_lo'=4,'core'=2,'x'=4,'z_hi'=2,'y'=4] {'z_hi'}, dimensions={0}, use_global_device_ids=true | all-gather | bytes 1376256 | tf_op jit(solution)/shard_map/all_gather | solution.py:40
  33.2 0.0 all-gather.7.cloned.1.call-update
  33.2 0.0 all-gather.5.cloned.1.call-start
  33.2 3.2 %reshape_reshape.3 = bf16[256,4,2,4,128]{4,3,2,1,0:T(4,128)(2,1)S(1)} reshape(bf16[2,128,4096]{2,1,0:T(8,128)(2,1)} %param.9) | data formatting | bytes 4194304 | tf_op jit(solution)/shard_map/reshape;reshape | solution.py:51
  36.5 0.0 copy-start.1
  36.5 0.0 copy-start.2
  36.5 2.8 copy.77
  39.3 108.1 %all-gather.7.cloned.1.call-done = bf16[32,128,1792]{2,1,0:T(8,128)(2,1)} async-done(((bf16[2,128,1792]{2,1,0:T(8,128)(2,1)}), bf16[32,128,1792]{2,1,0:T(8,128)(2,1)}) %all-gather.7.cloned.1.call-update) | async-done | bytes 14680080 | tf_op jit(solution)/shard_map/all_gather | solution.py:41
  147.3 5.3 %fusion.34 = bf16[256,768]{0,1:T(8,128)(2,1)S(1)} fusion(bf16[256,4096]{0,1:T(8,128)(2,1)} %bitcast.220, bf16[4096,1792]{1,0:T(8,128)(2,1)} %bitcast.221), kind=kOutput, calls=%fused_computation.44 | convolution fusion | flops 1610809344 | bytes 8781824 | tf_op jit(solution)/shard_map/dot_general | solution.py:95
  152.7 5.8 %collective-permute-start = (bf16[128,512]{0,1:T(8,128)(2,1)S(1)}, bf16[128,512]{0,1:T(8,128)(2,1)S(1)}, u32[]{:S(2)}, u32[]{:S(2)}) collective-permute-start(bf16[128,512]{0,1:T(8,128)(2,1)S(1)} %get-tuple-element.30), channel_id=1, source_target_pairs={{0,4},{4,0},{1,5},{5,1},{2,6},{6,2},{3,7},{7,3},{8,12},{12,8},{9,1... | collective-permute-start | bytes 393224 | tf_op jit(solution)/shard_map/ppermute | solution.py:37
  158.6 3.4 %collective-permute-done = bf16[128,512]{0,1:T(8,128)(2,1)S(1)} collective-permute-done((bf16[128,512]{0,1:T(8,128)(2,1)S(1)}, bf16[128,512]{0,1:T(8,128)(2,1)S(1)}, u32[]{:S(2)}, u32[]{:S(2)}) %collective-permute-start) | collective-permute-done | bytes 131104 | tf_op jit(solution)/shard_map/ppermute | solution.py:37
  162.0 0.9 copy.84
  162.9 0.0 all-gather.5.cloned.1.call-update
  162.9 0.2 reduce-scatter.2.cloned.1.call-start
  163.1 0.0 copy-done.1
  163.3 0.0 copy-done.2
  163.3 0.1 add_add_fusion
  163.4 0.1 broadcast_compare_fusion
  163.5 3.5 %fusion.26 = pred[2,128,4096]{1,2,0:T(8,128)(4,1)S(1)} fusion(s32[2,4096]{1,0:T(2,128)S(1)} %sub.108, s32[2,128]{1,0:T(2,128)S(1)} %get-tuple-element.20), kind=kLoop, calls=%fused_computation.33 | loop fusion | flops 4194304 | bytes 1082368 | tf_op jit(solution)/shard_map/and | solution.py:115
  167.0 3.2 %or_and_fusion = pred[2,128,4096]{1,2,0:T(8,128)(4,1)S(1)} fusion(s32[2,128]{1,0:T(2,128)S(1)} %get-tuple-element.19, s32[4096]{0:T(1024)S(1)} %bitcast.230, pred[4096]{0:T(1024)(128)(4,1)S(1)} %broadcast_compare_fusion.1, pred[2,4096]{1,0:T(4,128)(4,1)S(1)} %broadcast_compare_fusion), kind=kLoop, calls=%fused_computation.38 | loop fusion | flops 3145728 | bytes 1078272 | tf_op jit(solution)/shard_map/and | solution.py:111
  170.2 0.1 slice_bitcast_fusion.2
  170.3 0.1 slice_bitcast_fusion.3
  170.3 2.5 slice.94
  172.8 2.5 copy.95
  175.3 5.7 %fusion = (f32[4,128]{1,0:T(4,128)S(1)}, f32[4096,128,4]{1,0,2:T(8,128)}) fusion(pred[128,4096]{0,1:T(8,128)(4,1)S(1)} %get-tuple-element.23, bf16[128,4,128]{0,2,1:T(8,128)(2,1)S(1)} %bitcast.240, bf16[4096,1792]{1,0:T(8,128)(2,1)} %bitcast.223), kind=kOutput, calls=%fused_computation.8 | convolution fusion | flops 543161856 | bytes 10094592 | tf_op jit(solution)/shard_map/rqkgd,rpkd->rkgqp/dot_general | solution.py:18
  181.0 5.8 %fusion.2 = (f32[4,128]{1,0:T(4,128)S(1)}, f32[4096,128,4]{1,0,2:T(8,128)}) fusion(pred[128,4096]{0,1:T(8,128)(4,1)S(1)} %get-tuple-element.24, bf16[128,4,128]{0,2,1:T(8,128)(2,1)S(1)} %bitcast.238, bf16[4096,1792]{1,0:T(8,128)(2,1)} %bitcast.224), kind=kOutput, calls=%fused_computation.10 | convolution fusion | flops 543161856 | bytes 10094592 | tf_op jit(solution)/shard_map/rqkgd,rpkd->rkgqp/dot_general | solution.py:18
  186.8 35.1 %all-gather.5.cloned.1.call-done = bf16[16,2,128,512]{3,2,1,0:T(8,128)(2,1)} async-done(((bf16[1,2,128,512]{3,2,1,0:T(8,128)(2,1)}), bf16[16,2,128,512]{3,2,1,0:T(8,128)(2,1)}) %all-gather.5.cloned.1.call-update) | async-done | bytes 4194320 | tf_op jit(solution)/shard_map/all_gather | solution.py:41
  221.8 0.0 slice-start
  221.8 0.0 copy-start
  221.8 6.8 %fusion.1 = (f32[4,128]{1,0:T(4,128)S(1)}, f32[4096,128,4]{1,0,2:T(8,128)}) fusion(pred[128,4096]{0,1:T(8,128)(4,1)S(1)} %get-tuple-element.21, bf16[128,4,128]{0,2,1:T(8,128)(2,1)S(1)} %bitcast.241, bf16[4096,512]{1,0:T(8,128)(2,1)} %bitcast.245), kind=kOutput, calls=%fused_computation.9 | convolution fusion | flops 543161856 | bytes 10094592 | tf_op jit(solution)/shard_map/rqkgd,rpkd->rkgqp/dot_general | solution.py:18
  228.7 0.0 slice-start.1
  228.7 2.6 fusion.3
  231.3 0.0 slice-done
  231.3 0.0 copy-done
  231.4 0.2 slice-done.1
  231.6 4.1 %fusion.6 = (f32[4,128]{1,0:T(4,128)S(1)}, f32[4,128]{1,0:T(4,128)S(1)}) fusion(f32[4096,128,4]{1,0,2:T(8,128)S(1)} %copy-done, f32[4,128]{1,0:T(4,128)S(1)} %get-tuple-element.33, pred[128,4096]{0,1:T(8,128)(4,1)S(1)} %get-tuple-element.23, f32[4,128]{1,0:T(4,128)S(1)} %get-tuple-element.36, f32[4096,128,4]{1,0,2:T(8,128)S(1)} %bitcast.217, ...), kind=kLoop, calls=%fused_computation.16 | loop fusion | flops 20970496 | bytes 17833984 | tf_op jit(solution)/shard_map/reduce_sum | solution.py:25
  235.7 6.8 %fusion.8 = (f32[4,128]{1,0:T(4,128)S(1)}, f32[4,128]{1,0:T(4,128)S(1)}) fusion(f32[4096,128,4]{1,0,2:T(8,128)} %get-tuple-element.44, f32[4,128]{1,0:T(4,128)S(1)} %get-tuple-element.32, pred[128,4096]{0,1:T(8,128)(4,1)S(1)} %get-tuple-element.21, f32[4,128]{1,0:T(4,128)S(1)} %get-tuple-element.35, f32[4096,128,4]{1,0,2:T(8,128)S(1)} %get-tuple-element.40, ...), kind=kLoop, calls=%fused_computation.18 | loop fusion | flops 20970496 | bytes 17833984 | tf_op jit(solution)/shard_map/reduce_sum | solution.py:25
  242.5 0.0 copy-start.3
  242.5 3.4 %fusion.52 = f32[4,128,128]{1,2,0:T(8,128)S(1)} fusion(f32[4096,128,4]{1,0,2:T(8,128)S(1)} %copy-done, f32[4,128]{1,0:T(4,128)S(1)} %get-tuple-element.33, pred[128,4096]{0,1:T(8,128)(4,1)S(1)} %get-tuple-element.23, bf16[4096,1792]{1,0:T(8,128)(2,1)} %bitcast.225, f32[4,128]{1,0:T(4,128)S(1)} %get-tuple-element.16, f32[4,128]{1,0:T(4,128)S(1)} %get-tuple-element.31), kind=kOutput, calls=%fused_computation.50 | convolution fusion | flops 547487744 | bytes 10229760 | tf_op jit(solution)/shard_map/rkgqp,rpkd->rkgqd/dot_general | solution.py:26
  245.9 0.0 copy-done.3
  246.0 5.3 %fusion.58 = bf16[4,128,128]{1,2,0:T(8,128)(2,1)S(1)} fusion(f32[4,128,128]{1,2,0:T(8,128)S(1)} %fusion.52, f32[4096,128,4]{1,0,2:T(8,128)} %get-tuple-element.44, f32[4,128]{1,0:T(4,128)S(1)} %get-tuple-element.32, pred[128,4096]{0,1:T(8,128)(4,1)S(1)} %get-tuple-element.21, bf16[4096,512]{1,0:T(8,128)(2,1)S(1)} %bitcast.247, ...), kind=kOutput, calls=%fused_computation.52 | convolution fusion | flops 547553280 | bytes 10358784 | tf_op jit(solution)/shard_map/rkgqp,rpkd->rkgqd/dot_general | solution.py:26
  251.3 3.2 %fusion.43 = f32[4,128,128]{1,2,0:T(8,128)S(1)} fusion(f32[4096,128,4]{1,0,2:T(8,128)S(1)} %bitcast.217, f32[4,128]{1,0:T(4,128)S(1)} %get-tuple-element.36, pred[128,4096]{0,1:T(8,128)(4,1)S(1)} %get-tuple-element.24, bf16[4096,1792]{1,0:T(8,128)(2,1)} %bitcast.226, f32[4,128]{1,0:T(4,128)S(1)} %get-tuple-element.18, f32[4,128]{1,0:T(4,128)S(1)} %get-tuple-element.34), kind=kOutput, calls=%fused_computation.47 | convolution fusion | flops 547487744 | bytes 10229760 | tf_op jit(solution)/shard_map/rkgqp,rpkd->rkgqd/dot_general | solution.py:26
  254.6 2.0 fusion.64
  256.6 0.1 copy.94
  256.7 4.8 %convolution_convert_fusion = bf16[2,128,4096]{2,1,0:T(8,128)(2,1)} fusion(bf16[2,128,512]{2,1,0:T(8,128)(2,1)S(1)} %bitcast.227, bf16[4096,512,1]{1,0,2:T(8,128)(2,1)} %bitcast.214), kind=kOutput, calls=%fused_computation.24 | convolution fusion | flops 1074790400 | bytes 6553600 | tf_op jit(solution)/shard_map/dot_general | solution.py:151
  261.5 0.0 reduce-scatter.2.cloned.1.call-update
  261.6 0.7 copy.96
  262.3 0.7 copy.97
  263.1 39.8 %reduce-scatter.2.cloned.1.call-done = bf16[2,128,512]{2,1,0:T(8,128)(2,1)} async-done(((bf16[2,128,4096]{2,1,0:T(8,128)(2,1)}), bf16[2,128,512]{2,1,0:T(8,128)(2,1)}) %reduce-scatter.2.cloned.1.call-update) | async-done | bytes 262160 | tf_op jit(solution)/shard_map/reduce_scatter | solution.py:157
  (21 shorter events, 0.4 us)
Async XLA Ops:
  7.2 140.2 %all-gather.7.cloned.1.call-start = ((), (), s32[]{:S(2)}) async-start(), calls=%async_computation.3 | async-start | bytes 15597568 | tf_op jit(solution)/shard_map/all_gather | solution.py:41
  33.2 188.6 %all-gather.5.cloned.1.call-start = ((), (), s32[]{:S(2)}) async-start(), calls=%async_computation.1 | async-start | bytes 4456448 | tf_op jit(solution)/shard_map/all_gather | solution.py:41
  36.5 126.7 %copy-start.1 = (s32[2,4096]{1,0:T(2,128)S(1)}, s32[2,4096]{1,0:T(2,128)}, u32[]{:S(2)}) copy-start(s32[2,4096]{1,0:T(2,128)} %param.10) | copy-start | bytes 98308
  36.5 126.8 %copy-start.2 = (s32[2]{0:T(128)S(1)}, s32[2]{0:T(128)}, u32[]{:S(2)}) copy-start(s32[2]{0:T(128)} %param.11) | copy-start | bytes 28
  152.7 9.3 %collective-permute-start = (bf16[128,512]{0,1:T(8,128)(2,1)S(1)}, bf16[128,512]{0,1:T(8,128)(2,1)S(1)}, u32[]{:S(2)}, u32[]{:S(2)}) collective-permute-start(bf16[128,512]{0,1:T(8,128)(2,1)S(1)} %get-tuple-element.30), channel_id=1, source_target_pairs={{0,4},{4,0},{1,5},{5,1},{2,6},{6,2},{3,7},{7,3},{8,12},{12,8},{9,1... | collective-permute-start | bytes 393224 | tf_op jit(solution)/shard_map/ppermute | solution.py:37
  162.9 139.9 %reduce-scatter.2.cloned.1.call-start = ((), (), s32[]{:S(2)}) async-start(), calls=%async_computation.2 | async-start | bytes 2359296 | tf_op jit(solution)/shard_map/reduce_scatter | solution.py:157
  221.8 9.5 %slice-start = ((s8[8388608]{0:T(1024)(128)(4,1)}), s8[4194304]{0:T(1024)(128)(4,1)S(1)}, s32[]{:S(2)}) async-start(s8[8388608]{0:T(1024)(128)(4,1)} %bitcast.216), calls=%async_computation.4 | async-start | bytes 8388608
  221.8 9.5 %copy-start = (f32[4096,128,4]{1,0,2:T(8,128)S(1)}, f32[4096,128,4]{1,0,2:T(8,128)}, u32[]{:S(2)}) copy-start(f32[4096,128,4]{1,0,2:T(8,128)} %get-tuple-element.42) | copy-start | bytes 25165828
  228.7 2.9 slice-start.1
  242.5 3.4 %copy-start.3 = (bf16[16,2,128,512]{3,2,1,0:T(8,128)(2,1)S(1)}, bf16[16,2,128,512]{3,2,1,0:T(8,128)(2,1)}, u32[]{:S(2)}) copy-start(bf16[16,2,128,512]{3,2,1,0:T(8,128)(2,1)} %all-gather.5.cloned.1.call-done) | copy-start | bytes 12582916
Sparse Core Ops, SparseCore 0:
  33.3 113.9 all-gather.6
  163.0 58.7 all-gather.4
  261.7 41.0 reduce-scatter.1

commit v5 on v4

--- a/solution.py
+++ b/solution.py
@@ -21,7 +21,7 @@
     scores = jnp.where(visible, scores, NEGATIVE)
     top_new = jnp.maximum(top_old, jnp.max(scores, axis=-1))
     rescale = jnp.exp(top_old - top_new)
-    weights = jnp.where(visible, jnp.exp(scores - top_new[..., None]), 0.0)
+    weights = jnp.exp(scores - top_new[..., None])
     denom_new = denom_old * rescale + jnp.sum(weights, axis=-1)
     numer_new = numer_old * rescale[..., None] + jnp.einsum(
         "rkgqp,rpkd->rkgqd",

time: 310 us -> 294 us (0.948)
  matrix products: 45 us -> 34.6 us
  other arithmetic: 17.9 us -> 11.7 us
    reduce_sum x2, other arithmetic: 10.9 us -> 4.71 us  [attend_block(): denom_new = denom_old * rescale + jnp.sum(weights, axis=-1)]
    dot_general x4, matrix products: 20.9 us -> 15.4 us  [attend_block(): jnp.einsum('rqkgd,rpkd->rkgqp', queries, key_block, preferred_element_typ...]
    dot_general x4, matrix products: 13.9 us -> 9.06 us  [attend_block(): jnp.einsum('rkgqp,rpkd->rkgqd', weights.astype(jnp.bfloat16), value_block...]
  transfers between devices with their start and end apart: 4 -> 4, of which waited for: 4 -> 4; matrix products, arithmetic and copies ran while one was open for 10% -> 11% of each run, Pallas kernels for 0% -> 0%
where the time goes in v5:
time: 294 us; the launch traced here: 293 us
  waiting for transfers between devices  186 us (63%)
  matrix products  34.6 us (12%)
  blocking collectives  20.7 us (7%)
  local copies, waits for them, and re-layouts  19.7 us (7%)
  between operations  14.1 us (5%)
  other arithmetic  11.7 us (4%)
  starting transfers between devices  6.12 us (2%)
    all_gather x2, waiting for transfers between devices, gather_seq(): gathered = lax.all_gather(pair, ('x', 'y'), axis=0, tiled=False)  143 us
    reduce_scatter x1, waiting for transfers between devices, shards(): lax.psum_scatter(partial_out.reshape(requests, rows, width).astype(jnp.bf...  39.8 us
    all_gather x1, blocking collectives, gather_seq(): pair = lax.all_gather(piece, 'z_hi', axis=0, tiled=False)  20.7 us
    dot_general x4, matrix products, attend_block(): jnp.einsum('rqkgd,rpkd->rkgqp', queries, key_block, preferred_element_typ...  15.4 us
    dot_general x4, matrix products, attend_block(): jnp.einsum('rkgqp,rpkd->rkgqd', weights.astype(jnp.bfloat16), value_block...  9.06 us
  transfers between devices with their start and end apart: 4, of which 4 were waited for; matrix products, arithmetic and copies ran while one was open for 11% of the time, Pallas kernels for 0%

profile of v5, /device:TPU:6, one launch (start us, length us, event | category | flops | bytes accessed | tf_op | source)
XLA Modules:
  0.0 293.3 jit_solution(5011549564005133284)
XLA Ops:
  7.2 0.0 all-gather.7.cloned.1.call-start
  7.2 0.9 constant_dynamic-update-slice_fusion.3
  8.1 0.9 copy.75
  9.0 0.9 copy.76
  10.0 0.8 constant_dynamic-update-slice_fusion.2
  10.7 0.8 constant_dynamic-update-slice_fusion.1
  11.5 0.9 constant_dynamic-update-slice_fusion
  12.4 20.7 %all-gather = bf16[256,1792]{1,0:T(8,128)(2,1)} all-gather(bf16[128,1792]{1,0:T(8,128)(2,1)S(1)} %bitcast_dynamic-update-slice_fusion), channel_id=2, replica_groups=mesh['z_lo'=4,'core'=2,'x'=4,'z_hi'=2,'y'=4] {'z_hi'}, dimensions={0}, use_global_device_ids=true | all-gather | bytes 1376256 | tf_op jit(solution)/shard_map/all_gather | solution.py:40
  33.2 0.0 all-gather.7.cloned.1.call-update
  33.2 0.0 all-gather.5.cloned.1.call-start
  33.2 3.2 %reshape_reshape.3 = bf16[256,4,2,4,128]{4,3,2,1,0:T(4,128)(2,1)S(1)} reshape(bf16[2,128,4096]{2,1,0:T(8,128)(2,1)} %param.9) | data formatting | bytes 4194304 | tf_op jit(solution)/shard_map/reshape;reshape | solution.py:51
  36.5 0.0 copy-start.1
  36.5 0.0 copy-start.2
  36.5 2.8 copy.77
  39.3 108.1 %all-gather.7.cloned.1.call-done = bf16[32,128,1792]{2,1,0:T(8,128)(2,1)} async-done(((bf16[2,128,1792]{2,1,0:T(8,128)(2,1)}), bf16[32,128,1792]{2,1,0:T(8,128)(2,1)}) %all-gather.7.cloned.1.call-update) | async-done | bytes 14680080 | tf_op jit(solution)/shard_map/all_gather | solution.py:41
  147.3 5.3 %fusion.30 = bf16[256,768]{0,1:T(8,128)(2,1)S(1)} fusion(bf16[256,4096]{0,1:T(8,128)(2,1)} %bitcast.164, bf16[4096,1792]{1,0:T(8,128)(2,1)} %bitcast.158), kind=kOutput, calls=%fused_computation.40 | convolution fusion | flops 1610809344 | bytes 8781824 | tf_op jit(solution)/shard_map/dot_general | solution.py:95
  152.7 5.8 %collective-permute-start = (bf16[128,512]{0,1:T(8,128)(2,1)S(1)}, bf16[128,512]{0,1:T(8,128)(2,1)S(1)}, u32[]{:S(2)}, u32[]{:S(2)}) collective-permute-start(bf16[128,512]{0,1:T(8,128)(2,1)S(1)} %get-tuple-element.30), channel_id=1, source_target_pairs={{0,4},{4,0},{1,5},{5,1},{2,6},{6,2},{3,7},{7,3},{8,12},{12,8},{9,1... | collective-permute-start | bytes 393224 | tf_op jit(solution)/shard_map/ppermute | solution.py:37
  158.6 3.4 %collective-permute-done = bf16[128,512]{0,1:T(8,128)(2,1)S(1)} collective-permute-done((bf16[128,512]{0,1:T(8,128)(2,1)S(1)}, bf16[128,512]{0,1:T(8,128)(2,1)S(1)}, u32[]{:S(2)}, u32[]{:S(2)}) %collective-permute-start) | collective-permute-done | bytes 131104 | tf_op jit(solution)/shard_map/ppermute | solution.py:37
  162.0 0.9 copy.84
  162.9 0.0 all-gather.5.cloned.1.call-update
  162.9 0.2 reduce-scatter.2.cloned.1.call-start
  163.1 0.0 copy-done.1
  163.3 0.0 copy-done.2
  163.3 0.1 add_add_fusion
  163.4 0.1 broadcast_compare_fusion
  163.5 3.5 %fusion.26 = pred[2,128,4096]{1,2,0:T(8,128)(4,1)S(1)} fusion(s32[2,4096]{1,0:T(2,128)S(1)} %sub.108, s32[2,128]{1,0:T(2,128)S(1)} %get-tuple-element.20), kind=kLoop, calls=%fused_computation.33 | loop fusion | flops 4194304 | bytes 1082368 | tf_op jit(solution)/shard_map/and | solution.py:115
  167.0 3.2 %or_and_fusion = pred[2,128,4096]{1,2,0:T(8,128)(4,1)S(1)} fusion(s32[2,128]{1,0:T(2,128)S(1)} %get-tuple-element.19, s32[4096]{0:T(1024)S(1)} %bitcast.174, pred[4096]{0:T(1024)(128)(4,1)S(1)} %broadcast_compare_fusion.1, pred[2,4096]{1,0:T(4,128)(4,1)S(1)} %broadcast_compare_fusion), kind=kLoop, calls=%fused_computation.34 | loop fusion | flops 3145728 | bytes 1078272 | tf_op jit(solution)/shard_map/and | solution.py:111
  170.2 0.1 slice_bitcast_fusion.2
  170.3 0.1 slice_bitcast_fusion.3
  170.3 2.5 slice.94
  172.8 2.4 copy.95
  175.3 5.8 %fusion.70 = (f32[4,128]{1,0:T(4,128)S(1)}, f32[1,1,4,128,4096]{3,4,2,1,0:T(8,128)}) fusion(bf16[128,4,128]{0,2,1:T(8,128)(2,1)S(1)} %bitcast.183, bf16[4096,1792]{1,0:T(8,128)(2,1)} %bitcast.160, pred[128,4096]{0,1:T(8,128)(4,1)S(1)} %get-tuple-element.21), kind=kOutput, calls=%fused_computation.89 | convolution fusion | flops 543161856 | bytes 10094592 | tf_op jit(solution)/shard_map/rqkgd,rpkd->rkgqp/dot_general | solution.py:18
  181.0 5.8 %fusion.68 = (f32[4,128]{1,0:T(4,128)S(1)}, f32[1,1,4,128,4096]{3,4,2,1,0:T(8,128)}) fusion(bf16[128,4,128]{0,2,1:T(8,128)(2,1)S(1)} %bitcast.181, bf16[4096,1792]{1,0:T(8,128)(2,1)} %bitcast.161, pred[128,4096]{0,1:T(8,128)(4,1)S(1)} %get-tuple-element.22), kind=kOutput, calls=%fused_computation.87 | convolution fusion | flops 543161856 | bytes 10094592 | tf_op jit(solution)/shard_map/rqkgd,rpkd->rkgqp/dot_general | solution.py:18
  186.8 35.0 %all-gather.5.cloned.1.call-done = bf16[16,2,128,512]{3,2,1,0:T(8,128)(2,1)} async-done(((bf16[1,2,128,512]{3,2,1,0:T(8,128)(2,1)}), bf16[16,2,128,512]{3,2,1,0:T(8,128)(2,1)}) %all-gather.5.cloned.1.call-update) | async-done | bytes 4194320 | tf_op jit(solution)/shard_map/all_gather | solution.py:41
  221.8 0.0 copy-start
  221.8 2.6 fusion.71
  224.5 0.0 slice-start.2
  224.5 0.0 copy-done
  224.5 0.0 slice-start.3
  224.5 1.2 fusion.69
  225.7 1.3 fusion.17
  227.1 0.0 slice-start
  227.1 0.0 slice-done.2
  227.1 0.8 slice-done.3
  227.9 0.0 slice-start.1
  227.9 2.2 fusion
  230.2 2.6 fusion.11
  232.8 0.0 slice-done
  232.8 0.0 slice-done.1
  232.8 2.5 fusion.4
  235.3 2.6 fusion.60
  237.9 2.6 fusion.54
  240.5 0.1 copy.94
  240.7 4.8 %convolution_convert_fusion = bf16[2,128,4096]{2,1,0:T(8,128)(2,1)} fusion(bf16[2,128,512]{2,1,0:T(8,128)(2,1)S(1)} %bitcast.165, bf16[4096,512,1]{1,0,2:T(8,128)(2,1)} %bitcast.154), kind=kOutput, calls=%fused_computation.20 | convolution fusion | flops 1074790400 | bytes 6553600 | tf_op jit(solution)/shard_map/dot_general | solution.py:151
  245.5 0.0 reduce-scatter.2.cloned.1.call-update
  245.5 0.7 copy.96
  246.2 0.7 copy.97
  247.0 39.8 %reduce-scatter.2.cloned.1.call-done = bf16[2,128,512]{2,1,0:T(8,128)(2,1)} async-done(((bf16[2,128,4096]{2,1,0:T(8,128)(2,1)}), bf16[2,128,512]{2,1,0:T(8,128)(2,1)}) %reduce-scatter.2.cloned.1.call-update) | async-done | bytes 262160 | tf_op jit(solution)/shard_map/reduce_scatter | solution.py:157
  (22 shorter events, 0.4 us)
Async XLA Ops:
  7.2 140.2 %all-gather.7.cloned.1.call-start = ((), (), s32[]{:S(2)}) async-start(), calls=%async_computation.3 | async-start | bytes 15597568 | tf_op jit(solution)/shard_map/all_gather | solution.py:41
  33.2 188.6 %all-gather.5.cloned.1.call-start = ((), (), s32[]{:S(2)}) async-start(), calls=%async_computation.1 | async-start | bytes 4456448 | tf_op jit(solution)/shard_map/all_gather | solution.py:41
  36.5 126.7 %copy-start.1 = (s32[2,4096]{1,0:T(2,128)S(1)}, s32[2,4096]{1,0:T(2,128)}, u32[]{:S(2)}) copy-start(s32[2,4096]{1,0:T(2,128)} %param.10) | copy-start | bytes 98308
  36.5 126.8 %copy-start.2 = (s32[2]{0:T(128)S(1)}, s32[2]{0:T(128)}, u32[]{:S(2)}) copy-start(s32[2]{0:T(128)} %param.11) | copy-start | bytes 28
  152.7 9.3 %collective-permute-start = (bf16[128,512]{0,1:T(8,128)(2,1)S(1)}, bf16[128,512]{0,1:T(8,128)(2,1)S(1)}, u32[]{:S(2)}, u32[]{:S(2)}) collective-permute-start(bf16[128,512]{0,1:T(8,128)(2,1)S(1)} %get-tuple-element.30), channel_id=1, source_target_pairs={{0,4},{4,0},{1,5},{5,1},{2,6},{6,2},{3,7},{7,3},{8,12},{12,8},{9,1... | collective-permute-start | bytes 393224 | tf_op jit(solution)/shard_map/ppermute | solution.py:37
  162.9 123.8 %reduce-scatter.2.cloned.1.call-start = ((), (), s32[]{:S(2)}) async-start(), calls=%async_computation.2 | async-start | bytes 2359296 | tf_op jit(solution)/shard_map/reduce_scatter | solution.py:157
  221.8 2.6 copy-start
  224.5 2.7 slice-start.2
  224.5 3.5 %slice-start.3 = ((s8[8388608]{0:T(1024)(128)(4,1)}), s8[4194304]{0:T(1024)(128)(4,1)S(1)}, s32[]{:S(2)}) async-start(s8[8388608]{0:T(1024)(128)(4,1)} %bitcast.152), calls=%async_computation.7 | async-start | bytes 8388608
  227.1 5.7 %slice-start = ((s8[8388608]{0:T(1024)(128)(4,1)}), s8[4194304]{0:T(1024)(128)(4,1)S(1)}, s32[]{:S(2)}) async-start(s8[8388608]{0:T(1024)(128)(4,1)} %bitcast.150), calls=%async_computation.4 | async-start | bytes 8388608
  227.9 4.9 %slice-start.1 = ((s8[8388608]{0:T(1024)(128)(4,1)}), s8[4194304]{0:T(1024)(128)(4,1)S(1)}, s32[]{:S(2)}) async-start(s8[8388608]{0:T(1024)(128)(4,1)} %bitcast.150), calls=%async_computation.5 | async-start | bytes 8388608
Sparse Core Ops, SparseCore 0:
  33.3 113.9 all-gather.6
  163.0 58.7 all-gather.4
  245.6 41.0 reduce-scatter.1

commit v6 on v5

--- a/solution.py
+++ b/solution.py
@@ -5,6 +5,7 @@
 from jax import lax
 from jax.sharding import Mesh
 from jax.sharding import PartitionSpec as P
+
 
 SINKS = 4
 NEGATIVE = -1e30
@@ -92,11 +93,15 @@
     w_out_full = from_gather_order(gathered[:, offs[3] : offs[4]], 0, sizes)
     kv_cols = kv_local * head_size
 
-    qkv_sum = jnp.dot(flat_tokens, w_qkv, preferred_element_type=jnp.float32)
-    qkv = qkv_sum.astype(jnp.bfloat16)
-    queries = qkv[:, :q_cols].reshape(requests, rows, kv_local, group_size, head_size)
-    new_keys = qkv[:, q_cols : q_cols + k_cols].reshape(requests, rows, kv_local, head_size)
-    new_values = qkv[:, q_cols + k_cols :].reshape(requests, rows, kv_local, head_size)
+    kv_new = jnp.dot(
+        flat_tokens, w_qkv[:, q_cols:], preferred_element_type=jnp.float32
+    ).astype(jnp.bfloat16)
+    new_keys = kv_new[:, :k_cols].reshape(requests, rows, kv_local, head_size)
+    new_values = kv_new[:, k_cols:].reshape(requests, rows, kv_local, head_size)
+    queries = jnp.dot(
+        flat_tokens, w_qkv[:, :q_cols], preferred_element_type=jnp.float32
+    ).astype(jnp.bfloat16)
+    queries = queries.reshape(requests, rows, kv_local, group_size, head_size)
 
     new_k_local = jnp.transpose(new_keys, (1, 0, 2, 3)).reshape(rows, -1)
     new_v_local = jnp.transpose(new_values, (1, 0, 2, 3)).reshape(rows, -1)

time: 294 us -> 292 us (level)
    all_gather x2, waiting for transfers between devices: 143 us -> 139 us  [gather_seq(): gathered = lax.all_gather(pair, ('x', 'y'), axis=0, tiled=False)]
    dot_general x1 -> x2, matrix products: 5.26 us -> 6.7 us  [the longest x1 3.54 us: shards(): jnp.dot(flat_tokens, w_qkv[:, :q_cols], preferred_element_type=jnp.float32)]
where the time goes in v6:
time: 292 us; the launch traced here: 291 us
  waiting for transfers between devices  184 us (63%)
  matrix products  35.9 us (12%)
  blocking collectives  20.7 us (7%)
  local copies, waits for them, and re-layouts  18.6 us (6%)
  between operations  14.1 us (5%)
  other arithmetic  11.7 us (4%)
  starting transfers between devices  6.12 us (2%)
    all_gather x2, waiting for transfers between devices, gather_seq(): gathered = lax.all_gather(pair, ('x', 'y'), axis=0, tiled=False)  139 us
    reduce_scatter x1, waiting for transfers between devices, shards(): lax.psum_scatter(partial_out.reshape(requests, rows, width).astype(jnp.bf...  41.3 us
    all_gather x1, blocking collectives, gather_seq(): pair = lax.all_gather(piece, 'z_hi', axis=0, tiled=False)  20.7 us
    dot_general x4, matrix products, attend_block(): jnp.einsum('rqkgd,rpkd->rkgqp', queries, key_block, preferred_element_typ...  15.4 us
    dot_general x4, matrix products, attend_block(): jnp.einsum('rkgqp,rpkd->rkgqd', weights.astype(jnp.bfloat16), value_block...  9.06 us
  transfers between devices with their start and end apart: 4, of which 4 were waited for; matrix products, arithmetic and copies ran while one was open for 11% of the time, Pallas kernels for 0%

profile of v6, /device:TPU:6, one launch (start us, length us, event | category | flops | bytes accessed | tf_op | source)
XLA Modules:
  0.0 291.4 jit_solution(3409627065118947119)
XLA Ops:
  7.2 0.0 all-gather.7.cloned.1.call-start
  7.2 0.9 constant_dynamic-update-slice_fusion.3
  8.1 0.9 copy.75
  9.0 0.9 copy.76
  10.0 0.8 constant_dynamic-update-slice_fusion.2
  10.7 0.8 constant_dynamic-update-slice_fusion.1
  11.5 0.9 constant_dynamic-update-slice_fusion
  12.4 20.7 %all-gather = bf16[256,1792]{1,0:T(8,128)(2,1)} all-gather(bf16[128,1792]{1,0:T(8,128)(2,1)S(1)} %bitcast_dynamic-update-slice_fusion), channel_id=2, replica_groups=mesh['z_lo'=4,'core'=2,'x'=4,'z_hi'=2,'y'=4] {'z_hi'}, dimensions={0}, use_global_device_ids=true | all-gather | bytes 1376256 | tf_op jit(solution)/shard_map/all_gather | solution.py:41
  33.2 0.0 all-gather.7.cloned.1.call-update
  33.2 0.0 copy-start.4
  33.2 0.0 copy-start.5
  33.2 0.0 all-gather.5.cloned.1.call-start
  33.3 3.2 %reshape_reshape.3 = bf16[256,4,2,4,128]{4,3,2,1,0:T(4,128)(2,1)S(1)} reshape(bf16[2,128,4096]{2,1,0:T(8,128)(2,1)} %param.9) | data formatting | bytes 4194304 | tf_op jit(solution)/shard_map/reshape;reshape | solution.py:52
  36.5 2.8 copy.77
  39.3 108.1 %all-gather.7.cloned.1.call-done = bf16[32,128,1792]{2,1,0:T(8,128)(2,1)} async-done(((bf16[2,128,1792]{2,1,0:T(8,128)(2,1)}), bf16[32,128,1792]{2,1,0:T(8,128)(2,1)}) %all-gather.7.cloned.1.call-update) | async-done | bytes 14680080 | tf_op jit(solution)/shard_map/all_gather | solution.py:42
  147.3 3.2 %fusion.68 = bf16[256,256]{1,0:T(8,128)(2,1)S(1)} fusion(bf16[256,4096]{0,1:T(8,128)(2,1)} %bitcast.170, bf16[4096,1792]{1,0:T(8,128)(2,1)} %bitcast.163), kind=kOutput, calls=%fused_computation.54 | convolution fusion | flops 536936448 | bytes 4325376 | tf_op jit(solution)/shard_map/dot_general | solution.py:96
  150.5 0.0 copy-start.2
  150.5 0.0 copy-start.3
  150.6 0.1 copy.82
  150.7 0.1 copy.83
  150.8 5.8 %collective-permute-start = (bf16[128,512]{0,1:T(8,128)(2,1)S(1)}, bf16[128,512]{0,1:T(8,128)(2,1)S(1)}, u32[]{:S(2)}, u32[]{:S(2)}) collective-permute-start(bf16[128,512]{0,1:T(8,128)(2,1)S(1)} %get-tuple-element.28), channel_id=1, source_target_pairs={{0,4},{4,0},{1,5},{5,1},{2,6},{6,2},{3,7},{7,3},{8,12},{12,8},{9,1... | collective-permute-start | bytes 393224 | tf_op jit(solution)/shard_map/ppermute | solution.py:38
  156.7 3.4 %collective-permute-done = bf16[128,512]{0,1:T(8,128)(2,1)S(1)} collective-permute-done((bf16[128,512]{0,1:T(8,128)(2,1)S(1)}, bf16[128,512]{0,1:T(8,128)(2,1)S(1)}, u32[]{:S(2)}, u32[]{:S(2)}) %collective-permute-start) | collective-permute-done | bytes 131104 | tf_op jit(solution)/shard_map/ppermute | solution.py:38
  160.1 0.9 copy.84
  161.0 0.0 all-gather.5.cloned.1.call-update
  161.0 0.2 reduce-scatter.2.cloned.1.call-start
  161.2 0.0 copy-done.4
  161.4 0.0 copy-done.5
  161.4 0.1 add_add_fusion
  161.5 0.1 broadcast_compare_fusion
  161.6 3.5 %fusion.26 = pred[2,128,4096]{1,2,0:T(8,128)(4,1)S(1)} fusion(s32[2,4096]{1,0:T(2,128)S(1)} %sub.108, s32[2,128]{1,0:T(2,128)S(1)} %get-tuple-element.20), kind=kLoop, calls=%fused_computation.33 | loop fusion | flops 4194304 | bytes 1082368 | tf_op jit(solution)/shard_map/and | solution.py:120
  165.1 3.2 %or_and_fusion = pred[2,128,4096]{1,2,0:T(8,128)(4,1)S(1)} fusion(s32[2,128]{1,0:T(2,128)S(1)} %get-tuple-element.19, s32[4096]{0:T(1024)S(1)} %bitcast.181, pred[4096]{0:T(1024)(128)(4,1)S(1)} %broadcast_compare_fusion.1, pred[2,4096]{1,0:T(4,128)(4,1)S(1)} %broadcast_compare_fusion), kind=kLoop, calls=%fused_computation.34 | loop fusion | flops 3145728 | bytes 1078272 | tf_op jit(solution)/shard_map/and | solution.py:116
  168.3 0.1 slice_bitcast_fusion.2
  168.4 0.1 slice_bitcast_fusion.3
  168.4 0.0 copy-start
  168.4 2.6 slice.99
  171.1 0.0 copy-done.2
  171.1 0.0 copy-done.3
  171.1 2.4 copy.95
  173.5 0.0 copy-done
  173.5 3.5 %fusion.32 = bf16[256,512]{0,1:T(8,128)(2,1)S(1)} fusion(bf16[256,4096]{0,1:T(8,128)(2,1)S(1)} %bitcast.171, bf16[4096,1792]{1,0:T(8,128)(2,1)} %bitcast.165), kind=kOutput, calls=%fused_computation.42 | convolution fusion | flops 1073872896 | bytes 6553600 | tf_op jit(solution)/shard_map/dot_general | solution.py:101
  177.1 5.8 %fusion.78 = (f32[4,128]{1,0:T(4,128)S(1)}, f32[1,1,4,128,4096]{3,4,2,1,0:T(8,128)}) fusion(bf16[128,4,128]{0,2,1:T(8,128)(2,1)S(1)} %bitcast.194, bf16[4096,1792]{1,0:T(8,128)(2,1)} %bitcast.166, pred[128,4096]{0,1:T(8,128)(4,1)S(1)} %get-tuple-element.21), kind=kOutput, calls=%fused_computation.93 | convolution fusion | flops 543161856 | bytes 10094592 | tf_op jit(solution)/shard_map/rqkgd,rpkd->rkgqp/dot_general | solution.py:19
  182.8 5.7 %fusion.76 = (f32[4,128]{1,0:T(4,128)S(1)}, f32[1,1,4,128,4096]{3,4,2,1,0:T(8,128)}) fusion(bf16[128,4,128]{0,2,1:T(8,128)(2,1)S(1)} %bitcast.192, bf16[4096,1792]{1,0:T(8,128)(2,1)} %bitcast.167, pred[128,4096]{0,1:T(8,128)(4,1)S(1)} %get-tuple-element.22), kind=kOutput, calls=%fused_computation.91 | convolution fusion | flops 543161856 | bytes 10094592 | tf_op jit(solution)/shard_map/rqkgd,rpkd->rkgqp/dot_general | solution.py:19
  188.6 31.3 %all-gather.5.cloned.1.call-done = bf16[16,2,128,512]{3,2,1,0:T(8,128)(2,1)} async-done(((bf16[1,2,128,512]{3,2,1,0:T(8,128)(2,1)}), bf16[16,2,128,512]{3,2,1,0:T(8,128)(2,1)}) %all-gather.5.cloned.1.call-update) | async-done | bytes 4194320 | tf_op jit(solution)/shard_map/all_gather | solution.py:42
  219.9 0.0 copy-start.1
  219.9 2.6 fusion.79
  222.6 0.0 slice-start.2
  222.6 0.0 copy-done.1
  222.6 0.0 slice-start.3
  222.6 1.2 fusion.77
  223.8 1.3 fusion.15
  225.2 0.0 slice-start
  225.2 0.0 slice-done.2
  225.2 0.8 slice-done.3
  226.0 2.2 fusion
  228.3 2.6 fusion.9
  230.9 0.0 slice-done
  230.9 0.0 slice-done.1
  230.9 2.5 fusion.4
  233.4 2.6 fusion.65
  236.0 2.6 fusion.59
  238.6 0.1 copy.94
  238.8 4.8 %convolution_convert_fusion = bf16[2,128,4096]{2,1,0:T(8,128)(2,1)} fusion(bf16[2,128,512]{2,1,0:T(8,128)(2,1)S(1)} %bitcast.172, bf16[4096,512,1]{1,0,2:T(8,128)(2,1)} %bitcast.159), kind=kOutput, calls=%fused_computation.18 | convolution fusion | flops 1074790400 | bytes 6553600 | tf_op jit(solution)/shard_map/dot_general | solution.py:156
  243.6 0.0 reduce-scatter.2.cloned.1.call-update
  243.6 41.3 %reduce-scatter.2.cloned.1.call-done = bf16[2,128,512]{2,1,0:T(8,128)(2,1)} async-done(((bf16[2,128,4096]{2,1,0:T(8,128)(2,1)}), bf16[2,128,512]{2,1,0:T(8,128)(2,1)}) %reduce-scatter.2.cloned.1.call-update) | async-done | bytes 262160 | tf_op jit(solution)/shard_map/reduce_scatter | solution.py:162
  (19 shorter events, 0.3 us)
Async XLA Ops:
  7.2 140.2 %all-gather.7.cloned.1.call-start = ((), (), s32[]{:S(2)}) async-start(), calls=%async_computation.3 | async-start | bytes 15597568 | tf_op jit(solution)/shard_map/all_gather | solution.py:42
  33.2 128.1 %copy-start.4 = (s32[2,4096]{1,0:T(2,128)S(1)}, s32[2,4096]{1,0:T(2,128)}, u32[]{:S(2)}) copy-start(s32[2,4096]{1,0:T(2,128)} %param.10) | copy-start | bytes 98308
  33.2 128.2 %copy-start.5 = (s32[2]{0:T(128)S(1)}, s32[2]{0:T(128)}, u32[]{:S(2)}) copy-start(s32[2]{0:T(128)} %param.11) | copy-start | bytes 28
  33.2 186.7 %all-gather.5.cloned.1.call-start = ((), (), s32[]{:S(2)}) async-start(), calls=%async_computation.1 | async-start | bytes 4456448 | tf_op jit(solution)/shard_map/all_gather | solution.py:42
  150.5 20.5 %copy-start.2 = (bf16[256,128]{1,0:T(8,128)(2,1)}, bf16[256,128]{1,0:T(8,128)(2,1)S(1)}, u32[]{:S(2)}) copy-start(bf16[256,128]{1,0:T(8,128)(2,1)S(1)} %get-tuple-element.29) | copy-start | bytes 196612
  150.5 20.5 %copy-start.3 = (bf16[256,128]{1,0:T(8,128)(2,1)}, bf16[256,128]{1,0:T(8,128)(2,1)S(1)}, u32[]{:S(2)}) copy-start(bf16[256,128]{1,0:T(8,128)(2,1)S(1)} %get-tuple-element.30) | copy-start | bytes 196612
  150.8 9.3 %collective-permute-start = (bf16[128,512]{0,1:T(8,128)(2,1)S(1)}, bf16[128,512]{0,1:T(8,128)(2,1)S(1)}, u32[]{:S(2)}, u32[]{:S(2)}) collective-permute-start(bf16[128,512]{0,1:T(8,128)(2,1)S(1)} %get-tuple-element.28), channel_id=1, source_target_pairs={{0,4},{4,0},{1,5},{5,1},{2,6},{6,2},{3,7},{7,3},{8,12},{12,8},{9,1... | collective-permute-start | bytes 393224 | tf_op jit(solution)/shard_map/ppermute | solution.py:38
  161.0 123.9 %reduce-scatter.2.cloned.1.call-start = ((), (), s32[]{:S(2)}) async-start(), calls=%async_computation.2 | async-start | bytes 2359296 | tf_op jit(solution)/shard_map/reduce_scatter | solution.py:162
  168.4 5.1 %copy-start = (bf16[256,4,4,2,128]{0,4,3,2,1:T(8,128)(2,1)S(1)}, bf16[256,4,4,2,128]{0,4,3,2,1:T(8,128)(2,1)}, u32[]{:S(2)}) copy-start(bf16[256,4,4,2,128]{0,4,3,2,1:T(8,128)(2,1)} %copy.77) | copy-start | bytes 6291460
  219.9 2.6 copy-start.1
  222.6 2.7 slice-start.2
  222.6 3.5 %slice-start.3 = ((s8[8388608]{0:T(1024)(128)(4,1)}), s8[4194304]{0:T(1024)(128)(4,1)S(1)}, s32[]{:S(2)}) async-start(s8[8388608]{0:T(1024)(128)(4,1)} %bitcast.157), calls=%async_computation.7 | async-start | bytes 8388608
  225.2 5.7 %slice-start = ((s8[8388608]{0:T(1024)(128)(4,1)}), s8[4194304]{0:T(1024)(128)(4,1)S(1)}, s32[]{:S(2)}) async-start(s8[8388608]{0:T(1024)(128)(4,1)} %bitcast.155), calls=%async_computation.4 | async-start | bytes 8388608
  226.0 4.9 %slice-start.1 = ((s8[8388608]{0:T(1024)(128)(4,1)}), s8[4194304]{0:T(1024)(128)(4,1)S(1)}, s32[]{:S(2)}) async-start(s8[8388608]{0:T(1024)(128)(4,1)} %bitcast.155), calls=%async_computation.5 | async-start | bytes 8388608
Sparse Core Ops, SparseCore 0:
  33.3 113.9 all-gather.6
  161.1 58.7 all-gather.4
  243.7 41.1 reduce-scatter.1

commit v7 on v6

--- a/solution.py
+++ b/solution.py
@@ -116,8 +116,9 @@
     cache_allowed = (key_pos < lengths[:, :, None]) & (
         (key_pos < SINKS) | (key_pos > window_floor[:, :, None])
     )
-    before = my_positions[:, :, None] - new_pos[:, None, :]
-    new_allowed = (before >= 0) & (before < window_len)
+    blk = rows // 2
+    n_blocks = total_rows // blk
+    window_blocks = window_len // blk + 1
 
     def block_of(source, offset, r):
         piece = source[:, offset + r * kv_cols : offset + (r + 1) * kv_cols]
@@ -138,12 +139,37 @@
             block_of(gathered, offs[5], r),
             cache_allowed[r : r + 1],
         )
-        running_state = attend_block(
-            running_state,
-            q_r,
-            block_of(new_gathered, 0, r),
-            block_of(new_gathered, half, r),
-            new_allowed[r : r + 1],
+        keys_r = block_of(new_gathered, 0, r).reshape(n_blocks, blk, kv_local, head_size)
+        values_r = block_of(new_gathered, half, r).reshape(n_blocks, blk, kv_local, head_size)
+        pos_blocks = new_pos[r].reshape(n_blocks, blk)
+        slot_of_block = (
+            jnp.zeros((n_blocks,), jnp.int32)
+            .at[pos_blocks[:, 0] // blk]
+            .set(jnp.arange(n_blocks, dtype=jnp.int32))
+        )
+        halves = []
+        for h in range(rows // blk):
+            lo = h * blk
+            t = my_positions[r, lo : lo + blk]
+            wanted = t[0] // blk - window_blocks + 1 + jnp.arange(window_blocks, dtype=jnp.int32)
+            slots = slot_of_block[jnp.maximum(wanted, 0)]
+            key_pos_sel = pos_blocks[slots].reshape(-1)
+            valid = jnp.repeat(wanted >= 0, blk)
+            before = t[:, None] - key_pos_sel[None, :]
+            allowed_h = valid[None, :] & (before >= 0) & (before < window_len)
+            state_h = tuple(
+                lax.slice_in_dim(part, lo, lo + blk, axis=3) for part in running_state
+            )
+            state_h = attend_block(
+                state_h,
+                q_r[:, lo : lo + blk],
+                keys_r[slots].reshape(1, window_blocks * blk, kv_local, head_size),
+                values_r[slots].reshape(1, window_blocks * blk, kv_local, head_size),
+                allowed_h[None],
+            )
+            halves.append(state_h)
+        running_state = tuple(
+            jnp.concatenate([half_state[i] for half_state in halves], axis=3) for i in range(3)
         )
         _, denom_final, numer_final = running_state
         attended_r = (numer_final / denom_final[..., None]).astype(jnp.bfloat16)

time: 292 us -> 297 us (1.017)
  local copies, waits for them, and re-layouts: 18.6 us -> 45.1 us
  waiting for transfers between devices: 184 us -> 164 us
  matrix products: 35.9 us -> 23.4 us
  between operations: 14.1 us -> 24.6 us
    all_gather x2, waiting for transfers between devices: 139 us -> 121 us  [gather_seq(): gathered = lax.all_gather(pair, ('x', 'y'), axis=0, tiled=False)]
    gather x0 -> x16, local copies, waits for them, and re-layouts: none -> 16.3 us  [the longest x4 6.7 us: shards(): keys_r[slots].reshape(1, window_blocks * blk, kv_local, head_size)]
    dot_general x4 -> x6, matrix products: 15.4 us -> 7.77 us  [attend_block(): jnp.einsum('rqkgd,rpkd->rkgqp', queries, key_block, preferred_element_typ...]
    slice x0 -> x3, local copies, waits for them, and re-layouts: none -> 4.18 us  [the longest x1 3.53 us: block_of(): piece = source[:, offset + r * kv_cols:offset + (r + 1) * kv_cols]]
    dot_general x4 -> x6, matrix products: 9.06 us -> 6.95 us  [attend_block(): jnp.einsum('rkgqp,rpkd->rkgqd', weights.astype(jnp.bfloat16), value_block...]
    unnamed x25 -> x33, local copies, waits for them, and re-layouts: 4.24 us -> 6.3 us
  transfers between devices with their start and end apart: 4 -> 4, of which waited for: 4 -> 4; matrix products, arithmetic and copies ran while one was open for 11% -> 14% of each run, Pallas kernels for 0% -> 0%
where the time goes in v7:
time: 297 us; the launch traced here: 296 us
  waiting for transfers between devices  164 us (55%)
  local copies, waits for them, and re-layouts  45.1 us (15%)
  between operations  24.6 us (8%)
  matrix products  23.4 us (8%)
  blocking collectives  20.7 us (7%)
  other arithmetic  12.4 us (4%)
  starting transfers between devices  5.94 us (2%)
    all_gather x2, waiting for transfers between devices, gather_seq(): gathered = lax.all_gather(pair, ('x', 'y'), axis=0, tiled=False)  121 us
    reduce_scatter x1, waiting for transfers between devices, shards(): lax.psum_scatter(partial_out.reshape(requests, rows, width).astype(jnp.bf...  41.3 us
    all_gather x1, blocking collectives, gather_seq(): pair = lax.all_gather(piece, 'z_hi', axis=0, tiled=False)  20.7 us
    dot_general x6, matrix products, attend_block(): jnp.einsum('rqkgd,rpkd->rkgqp', queries, key_block, preferred_element_typ...  7.77 us
    dot_general x6, matrix products, attend_block(): jnp.einsum('rkgqp,rpkd->rkgqd', weights.astype(jnp.bfloat16), value_block...  6.95 us
    gather x4, local copies, waits for them, and re-layouts, shards(): keys_r[slots].reshape(1, window_blocks * blk, kv_local, head_size)  6.7 us
    unnamed x33, local copies, waits for them, and re-layouts  6.3 us
  transfers between devices with their start and end apart: 4, of which 4 were waited for; matrix products, arithmetic and copies ran while one was open for 14% of the time, Pallas kernels for 0%

profile of v7, /device:TPU:6, one launch (start us, length us, event | category | flops | bytes accessed | tf_op | source)
XLA Modules:
  0.0 296.2 jit_solution(7745202630754715725)
XLA Ops:
  7.2 0.9 constant_dynamic-update-slice_fusion.3
  8.1 0.9 copy.66
  9.1 0.9 copy.67
  10.0 0.8 constant_dynamic-update-slice_fusion.2
  10.7 0.8 constant_dynamic-update-slice_fusion.1
  11.5 0.9 constant_dynamic-update-slice_fusion
  12.5 20.7 %all-gather = bf16[256,1792]{1,0:T(8,128)(2,1)} all-gather(bf16[128,1792]{1,0:T(8,128)(2,1)S(1)} %bitcast_dynamic-update-slice_fusion), channel_id=2, replica_groups=mesh['z_lo'=4,'core'=2,'x'=4,'z_hi'=2,'y'=4] {'z_hi'}, dimensions={0}, use_global_device_ids=true | all-gather | bytes 1376256 | tf_op jit(solution)/shard_map/all_gather | solution.py:41
  33.4 0.7 fusion.113
  44.6 0.8 scatter_custom_fusion
  45.4 0.8 gather_fusion
  46.2 0.8 gather_fusion.4
  47.0 3.2 %reshape_reshape.15 = bf16[256,4,2,4,128]{4,3,2,1,0:T(4,128)(2,1)S(1)} reshape(bf16[2,128,4096]{2,1,0:T(8,128)(2,1)} %param.9) | data formatting | bytes 4194304 | tf_op jit(solution)/shard_map/reshape;reshape | solution.py:52
  50.2 2.8 copy.68
  53.0 0.6 gather_fusion.1
  53.9 0.6 gather_fusion.5
  54.9 0.8 scatter_custom_fusion.1
  55.7 0.8 gather_fusion.8
  56.5 0.8 gather_fusion.12
  57.3 0.6 gather_fusion.13
  58.2 0.9 fusion.73
  59.1 0.9 fusion.75
  60.0 87.4 %all-gather.7.cloned.1.call-done = bf16[32,128,1792]{2,1,0:T(8,128)(2,1)} async-done(((bf16[2,128,1792]{2,1,0:T(8,128)(2,1)}), bf16[32,128,1792]{2,1,0:T(8,128)(2,1)}) %all-gather.7.cloned.1.call-update) | async-done | bytes 14680080 | tf_op jit(solution)/shard_map/all_gather | solution.py:42
  147.4 2.5 fusion.53
  150.3 5.8 %collective-permute-start = (bf16[128,512]{0,1:T(8,128)(2,1)S(1)}, bf16[128,512]{0,1:T(8,128)(2,1)S(1)}, u32[]{:S(2)}, u32[]{:S(2)}) collective-permute-start(bf16[128,512]{0,1:T(8,128)(2,1)S(1)} %get-tuple-element.26), channel_id=1, source_target_pairs={{0,4},{4,0},{1,5},{5,1},{2,6},{6,2},{3,7},{7,3},{8,12},{12,8},{9,1... | collective-permute-start | bytes 393224 | tf_op jit(solution)/shard_map/ppermute | solution.py:38
  156.1 0.9 fusion.79
  157.0 0.6 gather_fusion.9
  157.8 1.7 collective-permute-done
  159.5 0.9 copy.74
  160.5 0.9 fusion.77
  161.5 3.4 %or_and_fusion = pred[2,128,4096]{1,2,0:T(8,128)(4,1)S(1)} fusion(s32[2,128]{1,0:T(2,128)S(1)} %get-tuple-element.15, s32[4096]{0:T(1024)S(1)} %bitcast.376, pred[4096]{0:T(1024)(128)(4,1)S(1)} %broadcast_compare_fusion.1, pred[2,4096]{1,0:T(4,128)(4,1)S(1)} %broadcast_compare_fusion), kind=kLoop, calls=%fused_computation.39 | loop fusion | flops 3145728 | bytes 1078272 | tf_op jit(solution)/shard_map/and | solution.py:116
  164.8 0.9 slice_bitcast_fusion.1
  165.7 2.6 slice.261
  168.4 2.6 copy.84
  171.0 2.7 copy-done
  173.7 1.3 fusion.35
  175.0 1.3 fusion.118
  176.3 1.1 fusion
  177.4 2.3 fusion.115
  179.7 1.1 fusion.2
  180.9 2.4 fusion.41
  183.2 2.4 fusion.47
  185.6 33.7 %all-gather.5.cloned.1.call-done = bf16[16,2,128,512]{3,2,1,0:T(8,128)(2,1)} async-done(((bf16[1,2,128,512]{3,2,1,0:T(8,128)(2,1)}), bf16[16,2,128,512]{3,2,1,0:T(8,128)(2,1)}) %all-gather.5.cloned.1.call-update) | async-done | bytes 4194320 | tf_op jit(solution)/shard_map/all_gather | solution.py:42
  219.3 3.5 %fusion.109 = (bf16[4096,128]{1,0:T(8,128)(2,1)S(1)}, bf16[4096,128]{1,0:T(8,128)(2,1)S(1)}, bf16[4096,128]{1,0:T(8,128)(2,1)S(1)}, bf16[4096,128]{1,0:T(8,128)(2,1)}) fusion(bf16[4096,512]{1,0:T(8,128)(2,1)} %bitcast.346), kind=kLoop, calls=%fused_computation.218 | loop fusion | bytes 8388608 | tf_op jit(solution)/shard_map/slice | solution.py:124
  222.9 2.7 gather_fusion.2
  225.6 2.7 gather_fusion.6
  228.3 1.5 gather_fusion.3
  229.7 1.5 gather_fusion.7
  231.2 0.6 gather_fusion.14
  231.8 0.7 gather_fusion.10
  232.5 0.7 gather_fusion.11
  233.1 0.7 gather_fusion.15
  233.8 1.8 fusion.117
  235.7 1.0 fusion.119
  237.2 0.5 fusion.24
  237.8 0.6 fusion.56
  238.4 0.6 fusion.57
  239.3 0.8 fusion.116
  240.1 0.7 fusion.114
  240.9 0.5 fusion.30
  241.3 0.5 fusion.28
  241.9 0.6 fusion.58
  242.4 0.6 fusion.59
  243.5 4.8 %convolution_convert_fusion = bf16[2,128,4096]{2,1,0:T(8,128)(2,1)} fusion(bf16[2,128,512]{2,1,0:T(8,128)(2,1)S(1)} %bitcast.371, bf16[4096,512,1]{1,0,2:T(8,128)(2,1)} %bitcast.335), kind=kOutput, calls=%fused_computation.26 | convolution fusion | flops 1074790400 | bytes 6553600 | tf_op jit(solution)/shard_map/dot_general | solution.py:182
  248.4 41.3 %reduce-scatter.2.cloned.1.call-done = bf16[2,128,512]{2,1,0:T(8,128)(2,1)} async-done(((bf16[2,128,4096]{2,1,0:T(8,128)(2,1)}), bf16[2,128,512]{2,1,0:T(8,128)(2,1)}) %reduce-scatter.2.cloned.1.call-update) | async-done | bytes 262160 | tf_op jit(solution)/shard_map/reduce_scatter | solution.py:188
  (102 shorter events, 4.2 us)
Async XLA Ops:
  7.2 26.1 %copy-start.12 = (s32[2,4096]{1,0:T(2,128)S(1)}, s32[2,4096]{1,0:T(2,128)}, u32[]{:S(2)}) copy-start(s32[2,4096]{1,0:T(2,128)} %param.10) | copy-start | bytes 98308
  7.2 26.1 %copy-start.13 = (s32[2]{0:T(128)S(1)}, s32[2]{0:T(128)}, u32[]{:S(2)}) copy-start(s32[2]{0:T(128)} %param.11) | copy-start | bytes 28
  7.2 140.2 %all-gather.7.cloned.1.call-start = ((), (), s32[]{:S(2)}) async-start(), calls=%async_computation.3 | async-start | bytes 15597568 | tf_op jit(solution)/shard_map/all_gather | solution.py:42
  33.2 186.1 %all-gather.5.cloned.1.call-start = ((), (), s32[]{:S(2)}) async-start(), calls=%async_computation.1 | async-start | bytes 4456448 | tf_op jit(solution)/shard_map/all_gather | solution.py:42
  53.0 94.4 %copy-start.4 = (bf16[256,4,4,2,128]{0,4,3,2,1:T(8,128)(2,1)S(1)}, bf16[256,4,4,2,128]{0,4,3,2,1:T(8,128)(2,1)}, u32[]{:S(2)}) copy-start(bf16[256,4,4,2,128]{0,4,3,2,1:T(8,128)(2,1)} %copy.68) | copy-start | bytes 6291460
  149.9 9.6 %copy-start.11 = (bf16[256,128]{1,0:T(8,128)(2,1)}, bf16[256,128]{1,0:T(8,128)(2,1)S(1)}, u32[]{:S(2)}) copy-start(bf16[256,128]{1,0:T(8,128)(2,1)S(1)} %get-tuple-element.28) | copy-start | bytes 196612
  149.9 15.8 %copy-start.10 = (bf16[256,128]{1,0:T(8,128)(2,1)}, bf16[256,128]{1,0:T(8,128)(2,1)S(1)}, u32[]{:S(2)}) copy-start(bf16[256,128]{1,0:T(8,128)(2,1)S(1)} %get-tuple-element.27) | copy-start | bytes 196612
  150.3 9.3 %collective-permute-start = (bf16[128,512]{0,1:T(8,128)(2,1)S(1)}, bf16[128,512]{0,1:T(8,128)(2,1)S(1)}, u32[]{:S(2)}, u32[]{:S(2)}) collective-permute-start(bf16[128,512]{0,1:T(8,128)(2,1)S(1)} %get-tuple-element.26), channel_id=1, source_target_pairs={{0,4},{4,0},{1,5},{5,1},{2,6},{6,2},{3,7},{7,3},{8,12},{12,8},{9,1... | collective-permute-start | bytes 393224 | tf_op jit(solution)/shard_map/ppermute | solution.py:38
  160.4 129.3 %reduce-scatter.2.cloned.1.call-start = ((), (), s32[]{:S(2)}) async-start(), calls=%async_computation.2 | async-start | bytes 2359296 | tf_op jit(solution)/shard_map/reduce_scatter | solution.py:188
  165.7 8.0 %copy-start = (bf16[32,128,1792]{2,1,0:T(8,128)(2,1)S(1)}, bf16[32,128,1792]{2,1,0:T(8,128)(2,1)}, u32[]{:S(2)}) copy-start(bf16[32,128,1792]{2,1,0:T(8,128)(2,1)} %all-gather.7.cloned.1.call-done) | copy-start | bytes 44040196
  233.8 1.8 copy-start.3
  233.8 1.8 copy-start.8
  236.7 1.1 copy-start.2
  236.7 1.1 copy-start.6
  237.2 1.2 copy-start.1
  238.4 1.0 copy-start.7
  239.0 1.1 copy-start.9
  240.9 1.0 copy-start.5
Sparse Core Ops, SparseCore 0:
  33.3 113.9 all-gather.6
  160.5 58.7 all-gather.4
  248.5 41.1 reduce-scatter.1

commit v8 on v6

--- a/solution.py
+++ b/solution.py
@@ -33,6 +33,13 @@
     return (top_new, denom_new, numer_new)
 
 
+def z_first_pair(piece, z_index, use_permute):
+    if use_permute:
+        other = lax.ppermute(piece, "z_hi", [(0, 1), (1, 0)])
+        return jnp.where(z_index == 0, jnp.stack([piece, other]), jnp.stack([other, piece]))
+    return lax.all_gather(piece, "z_hi", axis=0, tiled=False)
+
+
 def gather_seq(piece, z_index, use_permute):
     if use_permute:
         other = lax.ppermute(piece, "z_hi", [(0, 1), (1, 0)])
@@ -81,14 +88,41 @@
     o_cols = w_out_t.shape[1]
     cache_k_local = jnp.transpose(cache_keys, (1, 0, 2, 3)).reshape(rows, -1)
     cache_v_local = jnp.transpose(cache_values, (1, 0, 2, 3)).reshape(rows, -1)
-    packed = jnp.concatenate(
-        [w_query, w_key, w_value, w_out_t, cache_k_local, cache_v_local], axis=1
-    )
+    packed = jnp.concatenate([w_query, w_key, w_value, w_out_t], axis=1)
     gathered = gather_seq(packed, z_index, False)
     total_rows = gathered.shape[0]
     offs = [0]
-    for c in (q_cols, k_cols, k_cols, o_cols, cache_k_local.shape[1], cache_v_local.shape[1]):
+    for c in (q_cols, k_cols, k_cols, o_cols):
         offs.append(offs[-1] + c)
+
+    x_index = lax.axis_index("x")
+    y_index = lax.axis_index("y")
+    cache_pair = z_first_pair(
+        jnp.concatenate([cache_k_local, cache_v_local], axis=1), z_index, True
+    )
+    cache_blocks = [cache_pair]
+    block_sources = [(x_index, y_index)]
+    for dx in range(nx):
+        for dy in range(ny):
+            if dx == 0 and dy == 0:
+                continue
+            perm = [
+                (sx * ny + sy, ((sx + dx) % nx) * ny + (sy + dy) % ny)
+                for sx in range(nx)
+                for sy in range(ny)
+            ]
+            cache_blocks.append(lax.ppermute(cache_pair, ("x", "y"), perm))
+            block_sources.append(((x_index - dx) % nx, (y_index - dy) % ny))
+    cache_gathered = jnp.stack(cache_blocks).reshape(total_rows, -1)
+    source_x = jnp.stack([sx for sx, _ in block_sources])
+    source_y = jnp.stack([sy for _, sy in block_sources])
+    seq_of_block = (source_x[:, None] * nz + jnp.arange(nz)[None, :]) * ny + source_y[:, None]
+    cache_pos = (
+        seq_of_block[:, :, None] * rows + jnp.arange(rows, dtype=jnp.int32)[None, None, :]
+    ).reshape(total_rows)
+    offs.append(offs[-1] + cache_k_local.shape[1])
+    offs.append(offs[-1] + cache_v_local.shape[1])
+    flat_tokens, cache_gathered = lax.optimization_barrier((flat_tokens, cache_gathered))
     w_qkv = gathered[:, : offs[3]]
     w_out_full = from_gather_order(gathered[:, offs[3] : offs[4]], 0, sizes)
     kv_cols = kv_local * head_size
@@ -108,8 +142,7 @@
     new_gathered = gather_seq(jnp.concatenate([new_k_local, new_v_local], axis=1), z_index, True)
     half = new_k_local.shape[1]
 
-    key_pos = to_gather_order(jnp.arange(total_rows, dtype=jnp.int32), 0, sizes)
-    key_pos = key_pos[None, None, :]
+    key_pos = cache_pos[None, None, :]
     new_pos = to_gather_order(positions, 1, sizes)
     lengths = cached_len[:, None]
     window_floor = lengths + my_positions - window_len
@@ -134,8 +167,8 @@
         running_state = attend_block(
             running_state,
             q_r,
-            block_of(gathered, offs[4], r),
-            block_of(gathered, offs[5], r),
+            block_of(cache_gathered, 0, r),
+            block_of(cache_gathered, offs[5] - offs[4], r),
             cache_allowed[r : r + 1],
         )
         running_state = attend_block(

time: 292 us -> 314 us (1.075)
  starting transfers between devices: 6.12 us -> 51.1 us
  waiting for transfers between devices: 184 us -> 155 us
  local copies, waits for them, and re-layouts: 18.6 us -> 32.1 us
  matrix products: 35.9 us -> 30.5 us
  blocking collectives: 20.7 us -> 16.8 us
    all_gather x2, waiting for transfers between devices: 139 us -> 33.1 us  [gather_seq(): gathered = lax.all_gather(pair, ('x', 'y'), axis=0, tiled=False)]
    ppermute x0 -> x16, waiting for transfers between devices: none -> 75.8 us  [the longest x15 71.9 us: shards(): cache_blocks.append(lax.ppermute(cache_pair, ('x', 'y'), perm))]
    ppermute x0 -> x16, starting transfers between devices: none -> 39.1 us  [the longest x15 28.1 us: shards(): cache_blocks.append(lax.ppermute(cache_pair, ('x', 'y'), perm))]
    unnamed x25 -> x41, local copies, waits for them, and re-layouts: 4.24 us -> 12.1 us
    another operation x0 -> x4, local copies, waits for them, and re-layouts: none -> 7.48 us  [the longest x2 7.29 us: shards(): cache_gathered = jnp.stack(cache_blocks).reshape(total_rows, -1)]
    ppermute x1, starting transfers between devices: 5.82 us -> 11.6 us  [gather_seq(): other = lax.ppermute(piece, 'z_hi', [(0, 1), (1, 0)])]
    all_gather x1, blocking collectives: 20.7 us -> 16.8 us  [gather_seq(): pair = lax.all_gather(piece, 'z_hi', axis=0, tiled=False)]
  transfers between devices with their start and end apart: 4 -> 20, of which waited for: 4 -> 16; matrix products, arithmetic and copies ran while one was open for 11% -> 16% of each run, Pallas kernels for 0% -> 0%
where the time goes in v8:
time: 314 us
  waiting for transfers between devices  155 us (49%)
  starting transfers between devices  51.1 us (16%)
  local copies, waits for them, and re-layouts  32.1 us (10%)
  matrix products  30.5 us (10%)
  blocking collectives  16.8 us (5%)
  between operations  14.4 us (5%)
  other arithmetic  13.8 us (4%)
    ppermute x15, waiting for transfers between devices, shards(): cache_blocks.append(lax.ppermute(cache_pair, ('x', 'y'), perm))  71.9 us
    reduce_scatter x1, waiting for transfers between devices, shards(): lax.psum_scatter(partial_out.reshape(requests, rows, width).astype(jnp.bf...  41.3 us
    all_gather x2, waiting for transfers between devices, gather_seq(): gathered = lax.all_gather(pair, ('x', 'y'), axis=0, tiled=False)  33.1 us
    ppermute x15, starting transfers between devices, shards(): cache_blocks.append(lax.ppermute(cache_pair, ('x', 'y'), perm))  28.1 us
    all_gather x1, blocking collectives, gather_seq(): pair = lax.all_gather(piece, 'z_hi', axis=0, tiled=False)  16.8 us
    dot_general x4, matrix products, attend_block(): jnp.einsum('rqkgd,rpkd->rkgqp', queries, key_block, preferred_element_typ...  12.9 us
    unnamed x41, local copies, waits for them, and re-layouts  12.1 us
    ppermute x1, starting transfers between devices, gather_seq(): other = lax.ppermute(piece, 'z_hi', [(0, 1), (1, 0)])  11.6 us
  transfers between devices with their start and end apart: 20, of which 16 were waited for; matrix products, arithmetic and copies ran while one was open for 16% of the time, Pallas kernels for 0%

profile of v8, /device:TPU:6, one launch (start us, length us, event | category | flops | bytes accessed | tf_op | source)
XLA Modules:
  0.0 313.9 jit_solution(1436796253862571938)
XLA Ops:
  7.2 1.0 pad_maximum_fusion
  8.2 16.8 %all-gather = bf16[256,1280]{1,0:T(8,128)(2,1)} all-gather(bf16[128,1280]{1,0:T(8,128)(2,1)S(1)} %pad_maximum_fusion), channel_id=2, replica_groups=mesh['z_lo'=4,'core'=2,'x'=4,'z_hi'=2,'y'=4] {'z_hi'}, dimensions={0}, use_global_device_ids=true | all-gather | bytes 983040 | tf_op jit(solution)/shard_map/all_gather | solution.py:48
  25.1 1.0 copy.77
  26.1 1.0 copy.78
  27.1 11.0 %collective-permute-start = (bf16[128,512]{0,1:T(8,128)(2,1)S(1)}, bf16[128,512]{0,1:T(8,128)(2,1)S(1)}, u32[]{:S(2)}, u32[]{:S(2)}) collective-permute-start(bf16[128,512]{0,1:T(8,128)(2,1)S(1)} %get-tuple-element.37), channel_id=1, source_target_pairs={{0,4},{4,0},{1,5},{5,1},{2,6},{6,2},{3,7},{7,3},{8,12},{12,8},{9,1... | collective-permute-start | bytes 393224 | tf_op jit(solution)/shard_map/ppermute | solution.py:38
  38.1 3.9 %collective-permute-done = bf16[128,512]{0,1:T(8,128)(2,1)S(1)} collective-permute-done((bf16[128,512]{0,1:T(8,128)(2,1)S(1)}, bf16[128,512]{0,1:T(8,128)(2,1)S(1)}, u32[]{:S(2)}, u32[]{:S(2)}) %collective-permute-start) | collective-permute-done | bytes 131104 | tf_op jit(solution)/shard_map/ppermute | solution.py:38
  42.0 1.7 collective-permute-start.1
  43.7 3.4 %reshape_reshape.3 = bf16[256,4,2,4,128]{4,3,2,1,0:T(4,128)(2,1)S(1)} reshape(bf16[2,128,4096]{2,1,0:T(8,128)(2,1)} %param.9) | data formatting | bytes 4194304 | tf_op jit(solution)/shard_map/reshape;reshape | solution.py:59
  47.1 2.8 copy.76
  49.8 1.9 collective-permute-start.15
  51.7 2.0 collective-permute-start.14
  54.3 1.8 collective-permute-start.2
  56.1 0.8 fusion.73
  56.9 1.7 collective-permute-start.3
  59.3 19.1 %collective-permute-done.2 = bf16[2,128,512]{1,2,0:T(8,128)(2,1)S(1)} collective-permute-done((bf16[2,128,512]{1,2,0:T(8,128)(2,1)S(1)}, bf16[2,128,512]{1,2,0:T(8,128)(2,1)S(1)}, u32[]{:S(2)}, u32[]{:S(2)}) %collective-permute-start.2) | collective-permute-done | bytes 262176 | tf_op jit(solution)/shard_map/ppermute | solution.py:114
  79.5 1.3 collective-permute-done.3
  82.2 5.3 %collective-permute-done.4 = bf16[2,128,512]{1,2,0:T(8,128)(2,1)S(1)} collective-permute-done((bf16[2,128,512]{1,2,0:T(8,128)(2,1)S(1)}, bf16[2,128,512]{1,2,0:T(8,128)(2,1)S(1)}, u32[]{:S(2)}, u32[]{:S(2)}) %collective-permute-start.4) | collective-permute-done | bytes 262176 | tf_op jit(solution)/shard_map/ppermute | solution.py:114
  88.2 3.9 %collective-permute-done.5 = bf16[2,128,512]{1,2,0:T(8,128)(2,1)S(1)} collective-permute-done((bf16[2,128,512]{1,2,0:T(8,128)(2,1)S(1)}, bf16[2,128,512]{1,2,0:T(8,128)(2,1)S(1)}, u32[]{:S(2)}, u32[]{:S(2)}) %collective-permute-start.5) | collective-permute-done | bytes 262176 | tf_op jit(solution)/shard_map/ppermute | solution.py:114
  92.2 1.5 collective-permute-start.7
  93.7 0.7 bitcast_dynamic-update-slice_fusion.10
  94.4 4.5 %collective-permute-done.6 = bf16[2,128,512]{1,2,0:T(8,128)(2,1)S(1)} collective-permute-done((bf16[2,128,512]{1,2,0:T(8,128)(2,1)S(1)}, bf16[2,128,512]{1,2,0:T(8,128)(2,1)S(1)}, u32[]{:S(2)}, u32[]{:S(2)}) %collective-permute-start.6) | collective-permute-done | bytes 262176 | tf_op jit(solution)/shard_map/ppermute | solution.py:114
  98.9 2.1 collective-permute-start.8
  101.0 0.7 bitcast_dynamic-update-slice_fusion.9
  101.7 7.3 %collective-permute-done.7 = bf16[2,128,512]{1,2,0:T(8,128)(2,1)S(1)} collective-permute-done((bf16[2,128,512]{1,2,0:T(8,128)(2,1)S(1)}, bf16[2,128,512]{1,2,0:T(8,128)(2,1)S(1)}, u32[]{:S(2)}, u32[]{:S(2)}) %collective-permute-start.7) | collective-permute-done | bytes 262176 | tf_op jit(solution)/shard_map/ppermute | solution.py:114
  109.0 1.6 collective-permute-start.9
  110.6 0.7 bitcast_dynamic-update-slice_fusion.8
  111.3 3.9 %collective-permute-done.8 = bf16[2,128,512]{1,2,0:T(8,128)(2,1)S(1)} collective-permute-done((bf16[2,128,512]{1,2,0:T(8,128)(2,1)S(1)}, bf16[2,128,512]{1,2,0:T(8,128)(2,1)S(1)}, u32[]{:S(2)}, u32[]{:S(2)}) %collective-permute-start.8) | collective-permute-done | bytes 262176 | tf_op jit(solution)/shard_map/ppermute | solution.py:114
  115.2 5.2 %collective-permute-start.10 = (bf16[2,128,512]{1,2,0:T(8,128)(2,1)S(1)}, bf16[2,128,512]{1,2,0:T(8,128)(2,1)S(1)}, u32[]{:S(2)}, u32[]{:S(2)}) collective-permute-start(bf16[2,128,512]{1,2,0:T(8,128)(2,1)S(1)} %maximum_select_fusion.1), channel_id=1, source_target_pairs={{0,18},{1,19},{2,16},{3,17},{8,26},{9,27},{10,24},{11,25},{16,2},{... | collective-permute-start | bytes 786440 | tf_op jit(solution)/shard_map/ppermute | solution.py:114
  120.4 0.7 bitcast_dynamic-update-slice_fusion.7
  121.2 6.8 %collective-permute-done.9 = bf16[2,128,512]{1,2,0:T(8,128)(2,1)S(1)} collective-permute-done((bf16[2,128,512]{1,2,0:T(8,128)(2,1)S(1)}, bf16[2,128,512]{1,2,0:T(8,128)(2,1)S(1)}, u32[]{:S(2)}, u32[]{:S(2)}) %collective-permute-start.9) | collective-permute-done | bytes 262176 | tf_op jit(solution)/shard_map/ppermute | solution.py:114
  128.0 4.4 %collective-permute-start.11 = (bf16[2,128,512]{1,2,0:T(8,128)(2,1)S(1)}, bf16[2,128,512]{1,2,0:T(8,128)(2,1)S(1)}, u32[]{:S(2)}, u32[]{:S(2)}) collective-permute-start(bf16[2,128,512]{1,2,0:T(8,128)(2,1)S(1)} %maximum_select_fusion.1), channel_id=1, source_target_pairs={{0,19},{1,16},{2,17},{3,18},{8,27},{9,24},{10,25},{11,26},{16,3},{... | collective-permute-start | bytes 786440 | tf_op jit(solution)/shard_map/ppermute | solution.py:114
  132.4 0.7 bitcast_dynamic-update-slice_fusion.6
  133.2 9.3 %collective-permute-done.10 = bf16[2,128,512]{1,2,0:T(8,128)(2,1)S(1)} collective-permute-done((bf16[2,128,512]{1,2,0:T(8,128)(2,1)S(1)}, bf16[2,128,512]{1,2,0:T(8,128)(2,1)S(1)}, u32[]{:S(2)}, u32[]{:S(2)}) %collective-permute-start.10) | collective-permute-done | bytes 262176 | tf_op jit(solution)/shard_map/ppermute | solution.py:114
  142.5 2.5 collective-permute-start.12
  145.0 0.7 bitcast_dynamic-update-slice_fusion.5
  145.8 2.7 collective-permute-done.11
  149.1 7.7 %collective-permute-done.12 = bf16[2,128,512]{1,2,0:T(8,128)(2,1)S(1)} collective-permute-done((bf16[2,128,512]{1,2,0:T(8,128)(2,1)S(1)}, bf16[2,128,512]{1,2,0:T(8,128)(2,1)S(1)}, u32[]{:S(2)}, u32[]{:S(2)}) %collective-permute-start.12) | collective-permute-done | bytes 262176 | tf_op jit(solution)/shard_map/ppermute | solution.py:114
  156.8 0.7 bitcast_dynamic-update-slice_fusion.3
  157.6 0.7 bitcast_dynamic-update-slice_fusion.2
  158.3 0.7 bitcast_dynamic-update-slice_fusion.1
  159.0 0.7 bitcast_dynamic-update-slice_fusion
  159.8 6.5 %copy.79 = bf16[16,2,128,512]{3,2,1,0:T(8,128)(2,1)} copy(bf16[16,2,128,512]{2,3,1,0:T(8,128)(2,1)} %bitcast_dynamic-update-slice_fusion) | data formatting | bytes 8388608 | tf_op jit(solution)/shard_map/stack | solution.py:116
  166.7 2.3 fusion.50
  169.4 11.6 %collective-permute-start.16 = (bf16[128,512]{0,1:T(8,128)(2,1)S(1)}, bf16[128,512]{0,1:T(8,128)(2,1)S(1)}, u32[]{:S(2)}, u32[]{:S(2)}) collective-permute-start(bf16[128,512]{0,1:T(8,128)(2,1)S(1)} %get-tuple-element.32), channel_id=1, source_target_pairs={{0,4},{4,0},{1,5},{5,1},{2,6},{6,2},{3,7},{7,3},{8,12},{12,8},{9,1... | collective-permute-start | bytes 393224 | tf_op jit(solution)/shard_map/ppermute | solution.py:45
  181.0 5.1 %collective-permute-done.16 = bf16[128,512]{0,1:T(8,128)(2,1)S(1)} collective-permute-done((bf16[128,512]{0,1:T(8,128)(2,1)S(1)}, bf16[128,512]{0,1:T(8,128)(2,1)S(1)}, u32[]{:S(2)}, u32[]{:S(2)}) %collective-permute-start.16) | collective-permute-done | bytes 131104 | tf_op jit(solution)/shard_map/ppermute | solution.py:45
  186.2 0.9 copy.86
  188.2 3.5 %fusion.26 = pred[2,128,4096]{1,2,0:T(8,128)(4,1)S(1)} fusion(s32[2,4096]{1,0:T(2,128)S(1)} %sub.150, s32[2,128]{1,0:T(2,128)S(1)} %get-tuple-element.24), kind=kLoop, calls=%fused_computation.33 | loop fusion | flops 4194304 | bytes 1082368 | tf_op jit(solution)/shard_map/and | solution.py:153
  191.7 3.2 %or_and_fusion = pred[2,128,4096]{1,2,0:T(8,128)(4,1)S(1)} fusion(s32[2,128]{1,0:T(2,128)S(1)} %get-tuple-element.23, s32[4096]{0:T(1024)S(1)} %bitcast.236, pred[4096]{0:T(1024)(128)(4,1)S(1)} %broadcast_compare_fusion.1, pred[2,4096]{1,0:T(4,128)(4,1)S(1)} %broadcast_compare_fusion), kind=kLoop, calls=%fused_computation.34 | loop fusion | flops 3145728 | bytes 1078272 | tf_op jit(solution)/shard_map/and | solution.py:149
  195.1 2.5 slice.95
  197.6 2.5 copy.97
  200.0 3.8 %fusion.29 = bf16[256,512]{1,0:T(8,128)(2,1)S(1)} fusion(bf16[256,4096]{0,1:T(8,128)(2,1)S(1)} %bitcast.221, bf16[4096,1280]{1,0:T(8,128)(2,1)} %bitcast.224), kind=kOutput, calls=%fused_computation.41 | convolution fusion | flops 1073872896 | bytes 6553600 | tf_op jit(solution)/shard_map/dot_general | solution.py:135
  203.8 4.5 %fusion.88 = (f32[4,128]{1,0:T(4,128)S(1)}, f32[1,1,4,128,4096]{3,4,2,1,0:T(8,128)}) fusion(bf16[16,4,8,128]{3,2,1,0:T(8,128)(2,1)S(1)} %get-tuple-element.30, bf16[4096,512]{1,0:T(8,128)(2,1)S(1)} %bitcast.214, pred[128,4096]{0,1:T(8,128)(4,1)S(1)} %get-tuple-element.26), kind=kOutput, calls=%fused_computation.120 | convolution fusion | flops 543161856 | bytes 10094592 | tf_op jit(solution)/shard_map/rqkgd,rpkd->rkgqp/dot_general | solution.py:19
  208.3 4.5 %fusion.90 = (f32[4,128]{1,0:T(4,128)S(1)}, f32[1,1,4,128,4096]{3,4,2,1,0:T(8,128)}) fusion(bf16[16,4,8,128]{3,2,1,0:T(8,128)(2,1)S(1)} %get-tuple-element.29, bf16[4096,512]{1,0:T(8,128)(2,1)S(1)} %bitcast.215, pred[128,4096]{0,1:T(8,128)(4,1)S(1)} %get-tuple-element.25), kind=kOutput, calls=%fused_computation.122 | convolution fusion | flops 543161856 | bytes 10094592 | tf_op jit(solution)/shard_map/rqkgd,rpkd->rkgqp/dot_general | solution.py:19
  212.9 32.7 %all-gather.5.cloned.1.call-done = bf16[16,2,128,512]{3,2,1,0:T(8,128)(2,1)} async-done(((bf16[1,2,128,512]{3,2,1,0:T(8,128)(2,1)}), bf16[16,2,128,512]{3,2,1,0:T(8,128)(2,1)}) %all-gather.5.cloned.1.call-update) | async-done | bytes 4194320 | tf_op jit(solution)/shard_map/all_gather | solution.py:49
  245.6 2.6 fusion.89
  248.3 1.3 fusion.91
  249.5 1.3 fusion.9
  250.9 2.2 fusion.4
  253.2 2.6 fusion.15
  255.8 2.5 fusion
  258.4 1.3 fusion.56
  259.7 1.3 fusion.62
  261.3 4.8 %convolution_convert_fusion = bf16[2,128,4096]{2,1,0:T(8,128)(2,1)} fusion(bf16[2,128,512]{2,1,0:T(8,128)(2,1)S(1)} %bitcast.225, bf16[4096,512,1]{1,0,2:T(8,128)(2,1)} %bitcast.212), kind=kOutput, calls=%fused_computation.18 | convolution fusion | flops 1074790400 | bytes 6553600 | tf_op jit(solution)/shard_map/dot_general | solution.py:189
  266.1 41.3 %reduce-scatter.2.cloned.1.call-done = bf16[2,128,512]{2,1,0:T(8,128)(2,1)} async-done(((bf16[2,128,4096]{2,1,0:T(8,128)(2,1)}), bf16[2,128,512]{2,1,0:T(8,128)(2,1)}) %reduce-scatter.2.cloned.1.call-update) | async-done | bytes 262160 | tf_op jit(solution)/shard_map/reduce_scatter | solution.py:195
  (73 shorter events, 7.5 us)
Async XLA Ops:
  7.2 159.5 %all-gather.7.cloned.1.call-start = ((), (), s32[]{:S(2)}) async-start(), calls=%async_computation.3 | async-start | bytes 11141120 | tf_op jit(solution)/shard_map/all_gather | solution.py:49
  25.1 220.5 %all-gather.5.cloned.1.call-start = ((), (), s32[]{:S(2)}) async-start(), calls=%async_computation.1 | async-start | bytes 4456448 | tf_op jit(solution)/shard_map/all_gather | solution.py:49
  27.1 14.9 %collective-permute-start = (bf16[128,512]{0,1:T(8,128)(2,1)S(1)}, bf16[128,512]{0,1:T(8,128)(2,1)S(1)}, u32[]{:S(2)}, u32[]{:S(2)}) collective-permute-start(bf16[128,512]{0,1:T(8,128)(2,1)S(1)} %get-tuple-element.37), channel_id=1, source_target_pairs={{0,4},{4,0},{1,5},{5,1},{2,6},{6,2},{3,7},{7,3},{8,12},{12,8},{9,1... | collective-permute-start | bytes 393224 | tf_op jit(solution)/shard_map/ppermute | solution.py:38
  42.0 14.9 %collective-permute-start.1 = (bf16[2,128,512]{1,2,0:T(8,128)(2,1)S(1)}, bf16[2,128,512]{1,2,0:T(8,128)(2,1)S(1)}, u32[]{:S(2)}, u32[]{:S(2)}) collective-permute-start(bf16[2,128,512]{1,2,0:T(8,128)(2,1)S(1)} %maximum_select_fusion.1), channel_id=1, source_target_pairs={{0,1},{1,2},{2,3},{3,0},{8,9},{9,10},{10,11},{11,8},{16,17},{17,18... | collective-permute-start | bytes 786440 | tf_op jit(solution)/shard_map/ppermute | solution.py:114
  49.8 109.2 %collective-permute-start.15 = (bf16[2,128,512]{1,2,0:T(8,128)(2,1)S(1)}, bf16[2,128,512]{1,2,0:T(8,128)(2,1)S(1)}, u32[]{:S(2)}, u32[]{:S(2)}) collective-permute-start(bf16[2,128,512]{1,2,0:T(8,128)(2,1)S(1)} %maximum_select_fusion.1), channel_id=1, source_target_pairs={{0,27},{1,24},{2,25},{3,26},{8,3},{9,0},{10,1},{11,2},{16,11},{17,... | collective-permute-start | bytes 786440 | tf_op jit(solution)/shard_map/ppermute | solution.py:114
  51.7 106.6 %collective-permute-start.14 = (bf16[2,128,512]{1,2,0:T(8,128)(2,1)S(1)}, bf16[2,128,512]{1,2,0:T(8,128)(2,1)S(1)}, u32[]{:S(2)}, u32[]{:S(2)}) collective-permute-start(bf16[2,128,512]{1,2,0:T(8,128)(2,1)S(1)} %maximum_select_fusion.1), channel_id=1, source_target_pairs={{0,26},{1,27},{2,24},{3,25},{8,2},{9,3},{10,0},{11,1},{16,10},{17,... | collective-permute-start | bytes 786440 | tf_op jit(solution)/shard_map/ppermute | solution.py:114
  53.7 103.9 %collective-permute-start.13 = (bf16[2,128,512]{1,2,0:T(8,128)(2,1)S(1)}, bf16[2,128,512]{1,2,0:T(8,128)(2,1)S(1)}, u32[]{:S(2)}, u32[]{:S(2)}) collective-permute-start(bf16[2,128,512]{1,2,0:T(8,128)(2,1)S(1)} %maximum_select_fusion.1), channel_id=1, source_target_pairs={{0,25},{1,26},{2,27},{3,24},{8,1},{9,2},{10,3},{11,0},{16,9},{17,1... | collective-permute-start | bytes 786440 | tf_op jit(solution)/shard_map/ppermute | solution.py:114
  54.3 24.0 %collective-permute-start.2 = (bf16[2,128,512]{1,2,0:T(8,128)(2,1)S(1)}, bf16[2,128,512]{1,2,0:T(8,128)(2,1)S(1)}, u32[]{:S(2)}, u32[]{:S(2)}) collective-permute-start(bf16[2,128,512]{1,2,0:T(8,128)(2,1)S(1)} %maximum_select_fusion.1), channel_id=1, source_target_pairs={{0,2},{1,3},{2,0},{3,1},{8,10},{9,11},{10,8},{11,9},{16,18},{17,19... | collective-permute-start | bytes 786440 | tf_op jit(solution)/shard_map/ppermute | solution.py:114
  56.9 24.0 %collective-permute-start.3 = (bf16[2,128,512]{1,2,0:T(8,128)(2,1)S(1)}, bf16[2,128,512]{1,2,0:T(8,128)(2,1)S(1)}, u32[]{:S(2)}, u32[]{:S(2)}) collective-permute-start(bf16[2,128,512]{1,2,0:T(8,128)(2,1)S(1)} %maximum_select_fusion.1), channel_id=1, source_target_pairs={{0,3},{1,0},{2,1},{3,2},{8,11},{9,8},{10,9},{11,10},{16,19},{17,16... | collective-permute-start | bytes 786440 | tf_op jit(solution)/shard_map/ppermute | solution.py:114
  78.3 9.2 %collective-permute-start.4 = (bf16[2,128,512]{1,2,0:T(8,128)(2,1)S(1)}, bf16[2,128,512]{1,2,0:T(8,128)(2,1)S(1)}, u32[]{:S(2)}, u32[]{:S(2)}) collective-permute-start(bf16[2,128,512]{1,2,0:T(8,128)(2,1)S(1)} %maximum_select_fusion.1), channel_id=1, source_target_pairs={{0,8},{1,9},{2,10},{3,11},{8,16},{9,17},{10,18},{11,19},{16,24},{1... | collective-permute-start | bytes 786440 | tf_op jit(solution)/shard_map/ppermute | solution.py:114
  80.9 11.3 %collective-permute-start.5 = (bf16[2,128,512]{1,2,0:T(8,128)(2,1)S(1)}, bf16[2,128,512]{1,2,0:T(8,128)(2,1)S(1)}, u32[]{:S(2)}, u32[]{:S(2)}) collective-permute-start(bf16[2,128,512]{1,2,0:T(8,128)(2,1)S(1)} %maximum_select_fusion.1), channel_id=1, source_target_pairs={{0,9},{1,10},{2,11},{3,8},{8,17},{9,18},{10,19},{11,16},{16,25},{1... | collective-permute-start | bytes 786440 | tf_op jit(solution)/shard_map/ppermute | solution.py:114
  87.5 11.4 %collective-permute-start.6 = (bf16[2,128,512]{1,2,0:T(8,128)(2,1)S(1)}, bf16[2,128,512]{1,2,0:T(8,128)(2,1)S(1)}, u32[]{:S(2)}, u32[]{:S(2)}) collective-permute-start(bf16[2,128,512]{1,2,0:T(8,128)(2,1)S(1)} %maximum_select_fusion.1), channel_id=1, source_target_pairs={{0,10},{1,11},{2,8},{3,9},{8,18},{9,19},{10,16},{11,17},{16,26},{1... | collective-permute-start | bytes 786440 | tf_op jit(solution)/shard_map/ppermute | solution.py:114
  92.2 16.8 %collective-permute-start.7 = (bf16[2,128,512]{1,2,0:T(8,128)(2,1)S(1)}, bf16[2,128,512]{1,2,0:T(8,128)(2,1)S(1)}, u32[]{:S(2)}, u32[]{:S(2)}) collective-permute-start(bf16[2,128,512]{1,2,0:T(8,128)(2,1)S(1)} %maximum_select_fusion.1), channel_id=1, source_target_pairs={{0,11},{1,8},{2,9},{3,10},{8,19},{9,16},{10,17},{11,18},{16,27},{1... | collective-permute-start | bytes 786440 | tf_op jit(solution)/shard_map/ppermute | solution.py:114
  98.9 16.3 %collective-permute-start.8 = (bf16[2,128,512]{1,2,0:T(8,128)(2,1)S(1)}, bf16[2,128,512]{1,2,0:T(8,128)(2,1)S(1)}, u32[]{:S(2)}, u32[]{:S(2)}) collective-permute-start(bf16[2,128,512]{1,2,0:T(8,128)(2,1)S(1)} %maximum_select_fusion.1), channel_id=1, source_target_pairs={{0,16},{1,17},{2,18},{3,19},{8,24},{9,25},{10,26},{11,27},{16,0},{... | collective-permute-start | bytes 786440 | tf_op jit(solution)/shard_map/ppermute | solution.py:114
  109.0 19.0 %collective-permute-start.9 = (bf16[2,128,512]{1,2,0:T(8,128)(2,1)S(1)}, bf16[2,128,512]{1,2,0:T(8,128)(2,1)S(1)}, u32[]{:S(2)}, u32[]{:S(2)}) collective-permute-start(bf16[2,128,512]{1,2,0:T(8,128)(2,1)S(1)} %maximum_select_fusion.1), channel_id=1, source_target_pairs={{0,17},{1,18},{2,19},{3,16},{8,25},{9,26},{10,27},{11,24},{16,1},{... | collective-permute-start | bytes 786440 | tf_op jit(solution)/shard_map/ppermute | solution.py:114
  115.2 27.3 %collective-permute-start.10 = (bf16[2,128,512]{1,2,0:T(8,128)(2,1)S(1)}, bf16[2,128,512]{1,2,0:T(8,128)(2,1)S(1)}, u32[]{:S(2)}, u32[]{:S(2)}) collective-permute-start(bf16[2,128,512]{1,2,0:T(8,128)(2,1)S(1)} %maximum_select_fusion.1), channel_id=1, source_target_pairs={{0,18},{1,19},{2,16},{3,17},{8,26},{9,27},{10,24},{11,25},{16,2},{... | collective-permute-start | bytes 786440 | tf_op jit(solution)/shard_map/ppermute | solution.py:114
  128.0 20.4 %collective-permute-start.11 = (bf16[2,128,512]{1,2,0:T(8,128)(2,1)S(1)}, bf16[2,128,512]{1,2,0:T(8,128)(2,1)S(1)}, u32[]{:S(2)}, u32[]{:S(2)}) collective-permute-start(bf16[2,128,512]{1,2,0:T(8,128)(2,1)S(1)} %maximum_select_fusion.1), channel_id=1, source_target_pairs={{0,19},{1,16},{2,17},{3,18},{8,27},{9,24},{10,25},{11,26},{16,3},{... | collective-permute-start | bytes 786440 | tf_op jit(solution)/shard_map/ppermute | solution.py:114
  142.5 14.4 %collective-permute-start.12 = (bf16[2,128,512]{1,2,0:T(8,128)(2,1)S(1)}, bf16[2,128,512]{1,2,0:T(8,128)(2,1)S(1)}, u32[]{:S(2)}, u32[]{:S(2)}) collective-permute-start(bf16[2,128,512]{1,2,0:T(8,128)(2,1)S(1)} %maximum_select_fusion.1), channel_id=1, source_target_pairs={{0,24},{1,25},{2,26},{3,27},{8,0},{9,1},{10,2},{11,3},{16,8},{17,9... | collective-permute-start | bytes 786440 | tf_op jit(solution)/shard_map/ppermute | solution.py:114
  159.8 6.9 %copy-start.2 = (bf16[256,4,4,2,128]{0,4,3,2,1:T(8,128)(2,1)S(1)}, bf16[256,4,4,2,128]{0,4,3,2,1:T(8,128)(2,1)}, u32[]{:S(2)}) copy-start(bf16[256,4,4,2,128]{0,4,3,2,1:T(8,128)(2,1)} %copy.76) | copy-start | bytes 6291460
  166.7 20.7 %copy-start.6 = (s32[2,4096]{1,0:T(2,128)S(1)}, s32[2,4096]{1,0:T(2,128)}, u32[]{:S(2)}) copy-start(s32[2,4096]{1,0:T(2,128)} %param.10) | copy-start | bytes 98308
  166.7 21.1 %copy-start.7 = (s32[2]{0:T(128)S(1)}, s32[2]{0:T(128)}, u32[]{:S(2)}) copy-start(s32[2]{0:T(128)} %param.11) | copy-start | bytes 28
  169.1 26.0 %copy-start.4 = (bf16[256,128]{1,0:T(8,128)(2,1)}, bf16[256,128]{1,0:T(8,128)(2,1)S(1)}, u32[]{:S(2)}) copy-start(bf16[256,128]{1,0:T(8,128)(2,1)S(1)} %get-tuple-element.33) | copy-start | bytes 196612
  169.1 26.0 %copy-start.5 = (bf16[256,128]{1,0:T(8,128)(2,1)}, bf16[256,128]{1,0:T(8,128)(2,1)S(1)}, u32[]{:S(2)}) copy-start(bf16[256,128]{1,0:T(8,128)(2,1)S(1)} %get-tuple-element.34) | copy-start | bytes 196612
  169.4 16.7 %collective-permute-start.16 = (bf16[128,512]{0,1:T(8,128)(2,1)S(1)}, bf16[128,512]{0,1:T(8,128)(2,1)S(1)}, u32[]{:S(2)}, u32[]{:S(2)}) collective-permute-start(bf16[128,512]{0,1:T(8,128)(2,1)S(1)} %get-tuple-element.32), channel_id=1, source_target_pairs={{0,4},{4,0},{1,5},{5,1},{2,6},{6,2},{3,7},{7,3},{8,12},{12,8},{9,1... | collective-permute-start | bytes 393224 | tf_op jit(solution)/shard_map/ppermute | solution.py:45
  187.0 120.4 %reduce-scatter.2.cloned.1.call-start = ((), (), s32[]{:S(2)}) async-start(), calls=%async_computation.2 | async-start | bytes 2359296 | tf_op jit(solution)/shard_map/reduce_scatter | solution.py:195
  200.0 3.8 %copy-start = (bf16[16,2,128,512]{3,2,1,0:T(8,128)(2,1)S(1)}, bf16[16,2,128,512]{3,2,1,0:T(8,128)(2,1)}, u32[]{:S(2)}) copy-start(bf16[16,2,128,512]{3,2,1,0:T(8,128)(2,1)} %copy.79) | copy-start | bytes 12582916
  245.6 2.6 copy-start.3
  245.6 5.3 %slice-start.2 = ((s8[8388608]{0:T(1024)(128)(4,1)}), s8[4194304]{0:T(1024)(128)(4,1)S(1)}, s32[]{:S(2)}) async-start(s8[8388608]{0:T(1024)(128)(4,1)} %bitcast.210), calls=%async_computation.6 | async-start | bytes 8388608
  248.2 2.6 slice-start.3
  249.5 6.2 %slice-start = ((s8[8388608]{0:T(1024)(128)(4,1)}), s8[4194304]{0:T(1024)(128)(4,1)S(1)}, s32[]{:S(2)}) async-start(s8[8388608]{0:T(1024)(128)(4,1)} %bitcast.208), calls=%async_computation.4 | async-start | bytes 8388608
  250.9 4.9 %slice-start.1 = ((s8[8388608]{0:T(1024)(128)(4,1)}), s8[4194304]{0:T(1024)(128)(4,1)S(1)}, s32[]{:S(2)}) async-start(s8[8388608]{0:T(1024)(128)(4,1)} %bitcast.208), calls=%async_computation.5 | async-start | bytes 8388608
  255.8 2.6 copy-start.1
Sparse Core Ops, SparseCore 0:
  25.2 141.4 all-gather.6
  187.1 58.3 all-gather.4
  266.2 41.1 reduce-scatter.1

commit v9 on v6

--- a/solution.py
+++ b/solution.py
@@ -33,10 +33,10 @@
     return (top_new, denom_new, numer_new)
 
 
-def gather_seq(piece, z_index, use_permute):
+def gather_seq(piece, use_permute):
     if use_permute:
         other = lax.ppermute(piece, "z_hi", [(0, 1), (1, 0)])
-        pair = jnp.where(z_index == 0, jnp.stack([piece, other]), jnp.stack([other, piece]))
+        pair = jnp.stack([piece, other])
     else:
         pair = lax.all_gather(piece, "z_hi", axis=0, tiled=False)
     gathered = lax.all_gather(pair, ("x", "y"), axis=0, tiled=False)
@@ -84,7 +84,7 @@
     packed = jnp.concatenate(
         [w_query, w_key, w_value, w_out_t, cache_k_local, cache_v_local], axis=1
     )
-    gathered = gather_seq(packed, z_index, False)
+    gathered = gather_seq(packed, False)
     total_rows = gathered.shape[0]
     offs = [0]
     for c in (q_cols, k_cols, k_cols, o_cols, cache_k_local.shape[1], cache_v_local.shape[1]):
@@ -105,12 +105,14 @@
 
     new_k_local = jnp.transpose(new_keys, (1, 0, 2, 3)).reshape(rows, -1)
     new_v_local = jnp.transpose(new_values, (1, 0, 2, 3)).reshape(rows, -1)
-    new_gathered = gather_seq(jnp.concatenate([new_k_local, new_v_local], axis=1), z_index, True)
+    new_gathered = gather_seq(jnp.concatenate([new_k_local, new_v_local], axis=1), True)
     half = new_k_local.shape[1]
 
     key_pos = to_gather_order(jnp.arange(total_rows, dtype=jnp.int32), 0, sizes)
     key_pos = key_pos[None, None, :]
     new_pos = to_gather_order(positions, 1, sizes)
+    pos_pairs = new_pos.reshape(requests, nx * ny, nz, rows)
+    new_pos = jnp.where(z_index == 0, pos_pairs, pos_pairs[:, :, ::-1]).reshape(new_pos.shape)
     lengths = cached_len[:, None]
     window_floor = lengths + my_positions - window_len
     cache_allowed = (key_pos < lengths[:, :, None]) & (

time: 292 us -> 292 us (level)
  no operation moved by 1% of the time
where the time goes in v9:
time: 292 us; the launch traced here: 291 us
  waiting for transfers between devices  184 us (63%)
  matrix products  36 us (12%)
  blocking collectives  20.7 us (7%)
  local copies, waits for them, and re-layouts  18.6 us (6%)
  between operations  14.1 us (5%)
  other arithmetic  11.9 us (4%)
  starting transfers between devices  5.94 us (2%)
    all_gather x2, waiting for transfers between devices, gather_seq(): gathered = lax.all_gather(pair, ('x', 'y'), axis=0, tiled=False)  139 us
    reduce_scatter x1, waiting for transfers between devices, shards(): lax.psum_scatter(partial_out.reshape(requests, rows, width).astype(jnp.bf...  41.3 us
    all_gather x1, blocking collectives, gather_seq(): pair = lax.all_gather(piece, 'z_hi', axis=0, tiled=False)  20.7 us
    dot_general x4, matrix products, attend_block(): jnp.einsum('rqkgd,rpkd->rkgqp', queries, key_block, preferred_element_typ...  15.4 us
    dot_general x4, matrix products, attend_block(): jnp.einsum('rkgqp,rpkd->rkgqd', weights.astype(jnp.bfloat16), value_block...  9.06 us
  transfers between devices with their start and end apart: 4, of which 4 were waited for; matrix products, arithmetic and copies ran while one was open for 11% of the time, Pallas kernels for 0%

profile of v9, /device:TPU:6, one launch (start us, length us, event | category | flops | bytes accessed | tf_op | source)
XLA Modules:
  0.0 291.4 jit_solution(2121906143423366057)
XLA Ops:
  7.2 0.0 all-gather.6.cloned.1.call-start
  7.2 0.9 constant_dynamic-update-slice_fusion.3
  8.1 0.9 copy.76
  9.0 0.9 copy.77
  10.0 0.8 constant_dynamic-update-slice_fusion.2
  10.7 0.8 constant_dynamic-update-slice_fusion.1
  11.5 0.9 constant_dynamic-update-slice_fusion
  12.4 20.7 %all-gather = bf16[256,1792]{1,0:T(8,128)(2,1)} all-gather(bf16[128,1792]{1,0:T(8,128)(2,1)S(1)} %bitcast_dynamic-update-slice_fusion), channel_id=2, replica_groups=mesh['z_lo'=4,'core'=2,'x'=4,'z_hi'=2,'y'=4] {'z_hi'}, dimensions={0}, use_global_device_ids=true | all-gather | bytes 1376256 | tf_op jit(solution)/shard_map/all_gather | solution.py:41
  33.2 0.0 all-gather.6.cloned.1.call-update
  33.2 0.0 copy-start.4
  33.2 0.0 copy-start.5
  33.2 0.0 all-gather.8.cloned.1.call-start
  33.3 3.2 %reshape_reshape.6 = bf16[256,4,2,4,128]{4,3,2,1,0:T(4,128)(2,1)S(1)} reshape(bf16[2,128,4096]{2,1,0:T(8,128)(2,1)} %param.9) | data formatting | bytes 4194304 | tf_op jit(solution)/shard_map/reshape;reshape | solution.py:52
  36.5 2.8 copy.78
  39.3 108.1 %all-gather.6.cloned.1.call-done = bf16[32,128,1792]{2,1,0:T(8,128)(2,1)} async-done(((bf16[2,128,1792]{2,1,0:T(8,128)(2,1)}), bf16[32,128,1792]{2,1,0:T(8,128)(2,1)}) %all-gather.6.cloned.1.call-update) | async-done | bytes 14680080 | tf_op jit(solution)/shard_map/all_gather | solution.py:42
  147.3 3.2 %fusion.68 = bf16[256,256]{1,0:T(8,128)(2,1)S(1)} fusion(bf16[256,4096]{0,1:T(8,128)(2,1)} %bitcast.170, bf16[4096,1792]{1,0:T(8,128)(2,1)} %bitcast.163), kind=kOutput, calls=%fused_computation.54 | convolution fusion | flops 536936448 | bytes 4325376 | tf_op jit(solution)/shard_map/dot_general | solution.py:96
  150.5 0.0 copy-start.2
  150.5 0.0 copy-start.3
  150.6 0.1 copy.84
  150.7 0.1 copy.85
  150.8 5.8 %collective-permute-start = (bf16[128,512]{0,1:T(8,128)(2,1)S(1)}, bf16[128,512]{0,1:T(8,128)(2,1)S(1)}, u32[]{:S(2)}, u32[]{:S(2)}) collective-permute-start(bf16[128,512]{0,1:T(8,128)(2,1)S(1)} %get-tuple-element.28), channel_id=1, source_target_pairs={{0,4},{4,0},{1,5},{5,1},{2,6},{6,2},{3,7},{7,3},{8,12},{12,8},{9,1... | collective-permute-start | bytes 393224 | tf_op jit(solution)/shard_map/ppermute | solution.py:38
  156.7 3.4 %collective-permute-done = bf16[128,512]{0,1:T(8,128)(2,1)S(1)} collective-permute-done((bf16[128,512]{0,1:T(8,128)(2,1)S(1)}, bf16[128,512]{0,1:T(8,128)(2,1)S(1)}, u32[]{:S(2)}, u32[]{:S(2)}) %collective-permute-start) | collective-permute-done | bytes 131104 | tf_op jit(solution)/shard_map/ppermute | solution.py:38
  160.1 0.9 copy.86
  161.0 0.0 all-gather.8.cloned.1.call-update
  161.0 0.0 reduce-scatter.2.cloned.1.call-start
  161.1 0.0 copy-done.4
  161.2 0.0 copy-done.5
  161.2 0.1 add_add_fusion
  161.3 0.1 broadcast_compare_fusion
  161.4 3.7 %fusion.26 = pred[2,128,4096]{1,2,0:T(8,128)(4,1)S(1)} fusion(s32[2,4096]{1,0:T(2,128)S(1)} %sub.108, s32[2,128]{1,0:T(2,128)S(1)} %get-tuple-element.20), kind=kLoop, calls=%fused_computation.33 | loop fusion | flops 4194304 | bytes 1082368 | tf_op jit(solution)/shard_map/and | solution.py:122
  165.1 3.2 %or_and_fusion = pred[2,128,4096]{1,2,0:T(8,128)(4,1)S(1)} fusion(s32[2,128]{1,0:T(2,128)S(1)} %get-tuple-element.19, s32[4096]{0:T(1024)S(1)} %bitcast.181, pred[4096]{0:T(1024)(128)(4,1)S(1)} %broadcast_compare_fusion.1, pred[2,4096]{1,0:T(4,128)(4,1)S(1)} %broadcast_compare_fusion), kind=kLoop, calls=%fused_computation.34 | loop fusion | flops 3145728 | bytes 1078272 | tf_op jit(solution)/shard_map/and | solution.py:118
  168.3 0.1 slice_bitcast_fusion.2
  168.4 0.1 slice_bitcast_fusion.3
  168.5 0.0 copy-start
  168.5 2.6 slice.99
  171.1 0.0 copy-done.2
  171.1 0.0 copy-done.3
  171.1 2.4 copy.97
  173.5 0.0 copy-done
  173.5 3.5 %fusion.32 = bf16[256,512]{0,1:T(8,128)(2,1)S(1)} fusion(bf16[256,4096]{0,1:T(8,128)(2,1)S(1)} %bitcast.171, bf16[4096,1792]{1,0:T(8,128)(2,1)} %bitcast.165), kind=kOutput, calls=%fused_computation.42 | convolution fusion | flops 1073872896 | bytes 6553600 | tf_op jit(solution)/shard_map/dot_general | solution.py:101
  177.1 5.8 %fusion.78 = (f32[4,128]{1,0:T(4,128)S(1)}, f32[1,1,4,128,4096]{3,4,2,1,0:T(8,128)}) fusion(bf16[128,4,128]{0,2,1:T(8,128)(2,1)S(1)} %bitcast.193, bf16[4096,1792]{1,0:T(8,128)(2,1)} %bitcast.166, pred[128,4096]{0,1:T(8,128)(4,1)S(1)} %get-tuple-element.21), kind=kOutput, calls=%fused_computation.93 | convolution fusion | flops 543161856 | bytes 10094592 | tf_op jit(solution)/shard_map/rqkgd,rpkd->rkgqp/dot_general | solution.py:19
  182.9 5.7 %fusion.76 = (f32[4,128]{1,0:T(4,128)S(1)}, f32[1,1,4,128,4096]{3,4,2,1,0:T(8,128)}) fusion(bf16[128,4,128]{0,2,1:T(8,128)(2,1)S(1)} %bitcast.191, bf16[4096,1792]{1,0:T(8,128)(2,1)} %bitcast.167, pred[128,4096]{0,1:T(8,128)(4,1)S(1)} %get-tuple-element.22), kind=kOutput, calls=%fused_computation.91 | convolution fusion | flops 543161856 | bytes 10094592 | tf_op jit(solution)/shard_map/rqkgd,rpkd->rkgqp/dot_general | solution.py:19
  188.6 31.3 %all-gather.8.cloned.1.call-done = bf16[32,128,512]{2,1,0:T(8,128)(2,1)} async-done(((bf16[2,128,512]{2,1,0:T(8,128)(2,1)}), bf16[32,128,512]{2,1,0:T(8,128)(2,1)}) %all-gather.8.cloned.1.call-update) | async-done | bytes 4194320 | tf_op jit(solution)/shard_map/all_gather | solution.py:42
  219.9 0.0 copy-start.1
  219.9 2.6 fusion.79
  222.6 0.0 slice-start.2
  222.6 0.0 copy-done.1
  222.6 0.0 slice-start.3
  222.6 1.2 fusion.77
  223.8 1.3 fusion.15
  225.2 0.0 slice-start
  225.2 0.0 slice-done.2
  225.2 0.8 slice-done.3
  226.0 2.2 fusion
  228.3 2.6 fusion.9
  230.9 0.0 slice-done
  230.9 0.0 slice-done.1
  230.9 2.5 fusion.4
  233.4 2.6 fusion.65
  236.0 2.6 fusion.59
  238.6 0.1 copy.96
  238.8 4.8 %convolution_convert_fusion = bf16[2,128,4096]{2,1,0:T(8,128)(2,1)} fusion(bf16[2,128,512]{2,1,0:T(8,128)(2,1)S(1)} %bitcast.172, bf16[4096,512,1]{1,0,2:T(8,128)(2,1)} %bitcast.159), kind=kOutput, calls=%fused_computation.18 | convolution fusion | flops 1074790400 | bytes 6553600 | tf_op jit(solution)/shard_map/dot_general | solution.py:158
  243.6 0.0 reduce-scatter.2.cloned.1.call-update
  243.6 41.3 %reduce-scatter.2.cloned.1.call-done = bf16[2,128,512]{2,1,0:T(8,128)(2,1)} async-done(((bf16[2,128,4096]{2,1,0:T(8,128)(2,1)}), bf16[2,128,512]{2,1,0:T(8,128)(2,1)}) %reduce-scatter.2.cloned.1.call-update) | async-done | bytes 262160 | tf_op jit(solution)/shard_map/reduce_scatter | solution.py:164
  (21 shorter events, 0.3 us)
Async XLA Ops:
  7.2 140.2 %all-gather.6.cloned.1.call-start = ((), (), s32[]{:S(2)}) async-start(), calls=%async_computation.2 | async-start | bytes 15597568 | tf_op jit(solution)/shard_map/all_gather | solution.py:42
  33.2 127.9 %copy-start.4 = (s32[2,4096]{1,0:T(2,128)S(1)}, s32[2,4096]{1,0:T(2,128)}, u32[]{:S(2)}) copy-start(s32[2,4096]{1,0:T(2,128)} %param.10) | copy-start | bytes 98308
  33.2 128.0 %copy-start.5 = (s32[2]{0:T(128)S(1)}, s32[2]{0:T(128)}, u32[]{:S(2)}) copy-start(s32[2]{0:T(128)} %param.11) | copy-start | bytes 28
  33.2 186.7 %all-gather.8.cloned.1.call-start = ((), (), s32[]{:S(2)}) async-start(), calls=%async_computation.3 | async-start | bytes 4456448 | tf_op jit(solution)/shard_map/all_gather | solution.py:42
  150.5 20.6 %copy-start.2 = (bf16[256,128]{1,0:T(8,128)(2,1)}, bf16[256,128]{1,0:T(8,128)(2,1)S(1)}, u32[]{:S(2)}) copy-start(bf16[256,128]{1,0:T(8,128)(2,1)S(1)} %get-tuple-element.29) | copy-start | bytes 196612
  150.5 20.6 %copy-start.3 = (bf16[256,128]{1,0:T(8,128)(2,1)}, bf16[256,128]{1,0:T(8,128)(2,1)S(1)}, u32[]{:S(2)}) copy-start(bf16[256,128]{1,0:T(8,128)(2,1)S(1)} %get-tuple-element.30) | copy-start | bytes 196612
  150.8 9.3 %collective-permute-start = (bf16[128,512]{0,1:T(8,128)(2,1)S(1)}, bf16[128,512]{0,1:T(8,128)(2,1)S(1)}, u32[]{:S(2)}, u32[]{:S(2)}) collective-permute-start(bf16[128,512]{0,1:T(8,128)(2,1)S(1)} %get-tuple-element.28), channel_id=1, source_target_pairs={{0,4},{4,0},{1,5},{5,1},{2,6},{6,2},{3,7},{7,3},{8,12},{12,8},{9,1... | collective-permute-start | bytes 393224 | tf_op jit(solution)/shard_map/ppermute | solution.py:38
  161.0 123.9 %reduce-scatter.2.cloned.1.call-start = ((), (), s32[]{:S(2)}) async-start(), calls=%async_computation.1 | async-start | bytes 2359296 | tf_op jit(solution)/shard_map/reduce_scatter | solution.py:164
  168.5 5.1 %copy-start = (bf16[256,4,4,2,128]{0,4,3,2,1:T(8,128)(2,1)S(1)}, bf16[256,4,4,2,128]{0,4,3,2,1:T(8,128)(2,1)}, u32[]{:S(2)}) copy-start(bf16[256,4,4,2,128]{0,4,3,2,1:T(8,128)(2,1)} %copy.78) | copy-start | bytes 6291460
  219.9 2.6 copy-start.1
  222.6 2.7 slice-start.2
  222.6 3.5 %slice-start.3 = ((s8[8388608]{0:T(1024)(128)(4,1)}), s8[4194304]{0:T(1024)(128)(4,1)S(1)}, s32[]{:S(2)}) async-start(s8[8388608]{0:T(1024)(128)(4,1)} %bitcast.157), calls=%async_computation.7 | async-start | bytes 8388608
  225.2 5.7 %slice-start = ((s8[8388608]{0:T(1024)(128)(4,1)}), s8[4194304]{0:T(1024)(128)(4,1)S(1)}, s32[]{:S(2)}) async-start(s8[8388608]{0:T(1024)(128)(4,1)} %bitcast.155), calls=%async_computation.4 | async-start | bytes 8388608
  226.0 4.9 %slice-start.1 = ((s8[8388608]{0:T(1024)(128)(4,1)}), s8[4194304]{0:T(1024)(128)(4,1)S(1)}, s32[]{:S(2)}) async-start(s8[8388608]{0:T(1024)(128)(4,1)} %bitcast.155), calls=%async_computation.5 | async-start | bytes 8388608
Sparse Core Ops, SparseCore 0:
  33.3 113.9 all-gather.5
  161.1 58.7 all-gather.7
  243.7 41.1 reduce-scatter.1

commit v10 on v6

--- a/solution.py
+++ b/solution.py
@@ -17,12 +17,12 @@
 def attend_block(running_state, queries, key_block, value_block, allowed):
     top_old, denom_old, numer_old = running_state
     scores = jnp.einsum("rqkgd,rpkd->rkgqp", queries, key_block, preferred_element_type=jnp.float32)
-    scores = scores * (1.0 / math.sqrt(queries.shape[-1]))
+    scale = 1.0 / math.sqrt(queries.shape[-1])
     visible = allowed[:, None, None, :, :]
     scores = jnp.where(visible, scores, NEGATIVE)
     top_new = jnp.maximum(top_old, jnp.max(scores, axis=-1))
-    rescale = jnp.exp(top_old - top_new)
-    weights = jnp.exp(scores - top_new[..., None])
+    rescale = jnp.exp((top_old - top_new) * scale)
+    weights = jnp.exp((scores - top_new[..., None]) * scale)
     denom_new = denom_old * rescale + jnp.sum(weights, axis=-1)
     numer_new = numer_old * rescale[..., None] + jnp.einsum(
         "rkgqp,rpkd->rkgqd",

time: 292 us -> 307 us (1.051)
  matrix products: 35.9 us -> 46.4 us
  other arithmetic: 11.7 us -> 17.1 us
    dot_general x4, matrix products: 15.4 us -> 21 us  [attend_block(): jnp.einsum('rqkgd,rpkd->rkgqp', queries, key_block, preferred_element_typ...]
    reduce_sum x2, other arithmetic: 4.71 us -> 10.1 us  [attend_block(): denom_new = denom_old * rescale + jnp.sum(weights, axis=-1)]
    dot_general x4, matrix products: 9.06 us -> 13.9 us  [attend_block(): jnp.einsum('rkgqp,rpkd->rkgqd', weights.astype(jnp.bfloat16), value_block...]
where the time goes in v10:
time: 307 us
  waiting for transfers between devices  184 us (60%)
  matrix products  46.4 us (15%)
  blocking collectives  20.7 us (7%)
  local copies, waits for them, and re-layouts  18.1 us (6%)
  other arithmetic  17.1 us (6%)
  between operations  14.1 us (5%)
  starting transfers between devices  6.12 us (2%)
    all_gather x2, waiting for transfers between devices, gather_seq(): gathered = lax.all_gather(pair, ('x', 'y'), axis=0, tiled=False)  139 us
    reduce_scatter x1, waiting for transfers between devices, shards(): lax.psum_scatter(partial_out.reshape(requests, rows, width).astype(jnp.bf...  41.3 us
    dot_general x4, matrix products, attend_block(): jnp.einsum('rqkgd,rpkd->rkgqp', queries, key_block, preferred_element_typ...  21 us
    all_gather x1, blocking collectives, gather_seq(): pair = lax.all_gather(piece, 'z_hi', axis=0, tiled=False)  20.7 us
    dot_general x4, matrix products, attend_block(): jnp.einsum('rkgqp,rpkd->rkgqd', weights.astype(jnp.bfloat16), value_block...  13.9 us
    reduce_sum x2, other arithmetic, attend_block(): denom_new = denom_old * rescale + jnp.sum(weights, axis=-1)  10.1 us
  transfers between devices with their start and end apart: 4, of which 4 were waited for; matrix products, arithmetic and copies ran while one was open for 11% of the time, Pallas kernels for 0%

profile of v10, /device:TPU:6, one launch (start us, length us, event | category | flops | bytes accessed | tf_op | source)
XLA Modules:
  0.0 306.5 jit_solution(11573465630016029908)
XLA Ops:
  7.2 0.0 all-gather.7.cloned.1.call-start
  7.2 0.9 constant_dynamic-update-slice_fusion.3
  8.1 0.9 copy.75
  9.0 0.9 copy.76
  10.0 0.8 constant_dynamic-update-slice_fusion.2
  10.7 0.8 constant_dynamic-update-slice_fusion.1
  11.5 0.9 constant_dynamic-update-slice_fusion
  12.4 20.7 %all-gather = bf16[256,1792]{1,0:T(8,128)(2,1)} all-gather(bf16[128,1792]{1,0:T(8,128)(2,1)S(1)} %bitcast_dynamic-update-slice_fusion), channel_id=2, replica_groups=mesh['z_lo'=4,'core'=2,'x'=4,'z_hi'=2,'y'=4] {'z_hi'}, dimensions={0}, use_global_device_ids=true | all-gather | bytes 1376256 | tf_op jit(solution)/shard_map/all_gather | solution.py:41
  33.2 0.0 all-gather.7.cloned.1.call-update
  33.2 0.0 copy-start.5
  33.2 0.0 copy-start.6
  33.2 0.0 all-gather.5.cloned.1.call-start
  33.3 3.2 %reshape_reshape.3 = bf16[256,4,2,4,128]{4,3,2,1,0:T(4,128)(2,1)S(1)} reshape(bf16[2,128,4096]{2,1,0:T(8,128)(2,1)} %param.9) | data formatting | bytes 4194304 | tf_op jit(solution)/shard_map/reshape;reshape | solution.py:52
  36.5 2.8 copy.77
  39.3 108.1 %all-gather.7.cloned.1.call-done = bf16[32,128,1792]{2,1,0:T(8,128)(2,1)} async-done(((bf16[2,128,1792]{2,1,0:T(8,128)(2,1)}), bf16[32,128,1792]{2,1,0:T(8,128)(2,1)}) %all-gather.7.cloned.1.call-update) | async-done | bytes 14680080 | tf_op jit(solution)/shard_map/all_gather | solution.py:42
  147.3 3.2 %fusion.60 = bf16[256,256]{1,0:T(8,128)(2,1)S(1)} fusion(bf16[256,4096]{0,1:T(8,128)(2,1)} %bitcast.232, bf16[4096,1792]{1,0:T(8,128)(2,1)} %bitcast.225), kind=kOutput, calls=%fused_computation.54 | convolution fusion | flops 536936448 | bytes 4325376 | tf_op jit(solution)/shard_map/dot_general | solution.py:96
  150.5 0.0 copy-start.3
  150.5 0.0 copy-start.4
  150.6 0.1 copy.82
  150.7 0.1 copy.83
  150.8 5.8 %collective-permute-start = (bf16[128,512]{0,1:T(8,128)(2,1)S(1)}, bf16[128,512]{0,1:T(8,128)(2,1)S(1)}, u32[]{:S(2)}, u32[]{:S(2)}) collective-permute-start(bf16[128,512]{0,1:T(8,128)(2,1)S(1)} %get-tuple-element.28), channel_id=1, source_target_pairs={{0,4},{4,0},{1,5},{5,1},{2,6},{6,2},{3,7},{7,3},{8,12},{12,8},{9,1... | collective-permute-start | bytes 393224 | tf_op jit(solution)/shard_map/ppermute | solution.py:38
  156.7 3.4 %collective-permute-done = bf16[128,512]{0,1:T(8,128)(2,1)S(1)} collective-permute-done((bf16[128,512]{0,1:T(8,128)(2,1)S(1)}, bf16[128,512]{0,1:T(8,128)(2,1)S(1)}, u32[]{:S(2)}, u32[]{:S(2)}) %collective-permute-start) | collective-permute-done | bytes 131104 | tf_op jit(solution)/shard_map/ppermute | solution.py:38
  160.1 0.9 copy.84
  161.0 0.0 all-gather.5.cloned.1.call-update
  161.0 0.2 reduce-scatter.2.cloned.1.call-start
  161.2 0.0 copy-done.5
  161.4 0.0 copy-done.6
  161.4 0.1 add_add_fusion
  161.5 0.1 broadcast_compare_fusion
  161.6 3.5 %fusion.26 = pred[2,128,4096]{1,2,0:T(8,128)(4,1)S(1)} fusion(s32[2,4096]{1,0:T(2,128)S(1)} %sub.108, s32[2,128]{1,0:T(2,128)S(1)} %get-tuple-element.20), kind=kLoop, calls=%fused_computation.33 | loop fusion | flops 4194304 | bytes 1082368 | tf_op jit(solution)/shard_map/and | solution.py:120
  165.1 3.2 %or_and_fusion = pred[2,128,4096]{1,2,0:T(8,128)(4,1)S(1)} fusion(s32[2,128]{1,0:T(2,128)S(1)} %get-tuple-element.19, s32[4096]{0:T(1024)S(1)} %bitcast.245, pred[4096]{0:T(1024)(128)(4,1)S(1)} %broadcast_compare_fusion.1, pred[2,4096]{1,0:T(4,128)(4,1)S(1)} %broadcast_compare_fusion), kind=kLoop, calls=%fused_computation.38 | loop fusion | flops 3145728 | bytes 1078272 | tf_op jit(solution)/shard_map/and | solution.py:116
  168.3 0.1 slice_bitcast_fusion.2
  168.4 0.1 slice_bitcast_fusion.3
  168.4 0.0 copy-start.1
  168.4 2.6 slice.99
  171.1 0.0 copy-done.3
  171.1 0.0 copy-done.4
  171.1 2.5 copy.95
  173.5 0.0 copy-done.1
  173.5 3.5 %fusion.36 = bf16[256,512]{0,1:T(8,128)(2,1)S(1)} fusion(bf16[256,4096]{0,1:T(8,128)(2,1)S(1)} %bitcast.233, bf16[4096,1792]{1,0:T(8,128)(2,1)} %bitcast.227), kind=kOutput, calls=%fused_computation.46 | convolution fusion | flops 1073872896 | bytes 6553600 | tf_op jit(solution)/shard_map/dot_general | solution.py:101
  177.1 5.7 %fusion = (f32[4,128]{1,0:T(4,128)S(1)}, f32[4096,128,4]{1,0,2:T(8,128)}) fusion(pred[128,4096]{0,1:T(8,128)(4,1)S(1)} %get-tuple-element.23, bf16[128,4,128]{0,2,1:T(8,128)(2,1)S(1)} %bitcast.236, bf16[4096,1792]{1,0:T(8,128)(2,1)} %bitcast.228), kind=kOutput, calls=%fused_computation.8 | convolution fusion | flops 541064704 | bytes 10094592 | tf_op jit(solution)/shard_map/rqkgd,rpkd->rkgqp/dot_general | solution.py:19
  182.8 5.8 %fusion.2 = (f32[4,128]{1,0:T(4,128)S(1)}, f32[4096,128,4]{1,0,2:T(8,128)}) fusion(pred[128,4096]{0,1:T(8,128)(4,1)S(1)} %get-tuple-element.24, bf16[128,4,128]{0,2,1:T(8,128)(2,1)S(1)} %bitcast.234, bf16[4096,1792]{1,0:T(8,128)(2,1)} %bitcast.229), kind=kOutput, calls=%fused_computation.10 | convolution fusion | flops 541064704 | bytes 10094592 | tf_op jit(solution)/shard_map/rqkgd,rpkd->rkgqp/dot_general | solution.py:19
  188.6 31.3 %all-gather.5.cloned.1.call-done = bf16[16,2,128,512]{3,2,1,0:T(8,128)(2,1)} async-done(((bf16[1,2,128,512]{3,2,1,0:T(8,128)(2,1)}), bf16[16,2,128,512]{3,2,1,0:T(8,128)(2,1)}) %all-gather.5.cloned.1.call-update) | async-done | bytes 4194320 | tf_op jit(solution)/shard_map/all_gather | solution.py:42
  219.9 0.0 slice-start
  219.9 0.0 copy-start
  219.9 6.9 %fusion.1 = (f32[4,128]{1,0:T(4,128)S(1)}, f32[4096,128,4]{1,0,2:T(8,128)}) fusion(pred[128,4096]{0,1:T(8,128)(4,1)S(1)} %get-tuple-element.21, bf16[128,4,128]{0,2,1:T(8,128)(2,1)S(1)} %bitcast.237, bf16[4096,512]{1,0:T(8,128)(2,1)} %bitcast.238), kind=kOutput, calls=%fused_computation.9 | convolution fusion | flops 541064704 | bytes 10094592 | tf_op jit(solution)/shard_map/rqkgd,rpkd->rkgqp/dot_general | solution.py:19
  226.8 0.0 slice-start.1
  226.8 2.6 fusion.3
  229.4 0.0 slice-done
  229.4 0.0 copy-done
  229.4 0.3 slice-done.1
  229.7 3.6 %fusion.4 = (f32[4,128]{1,0:T(4,128)S(1)}, f32[4,128]{1,0:T(4,128)S(1)}) fusion(f32[4096,128,4]{1,0,2:T(8,128)S(1)} %copy-done, f32[4,128]{1,0:T(4,128)S(1)} %get-tuple-element.33, pred[128,4096]{0,1:T(8,128)(4,1)S(1)} %get-tuple-element.23, f32[4,128]{1,0:T(4,128)S(1)} %get-tuple-element.36, f32[4096,128,4]{1,0,2:T(8,128)S(1)} %bitcast.220, ...), kind=kLoop, calls=%fused_computation.12 | loop fusion | flops 16776192 | bytes 17833984 | tf_op jit(solution)/shard_map/reduce_sum | solution.py:26
  233.3 6.5 %fusion.6 = (f32[4,128]{1,0:T(4,128)S(1)}, f32[4,128]{1,0:T(4,128)S(1)}) fusion(f32[4096,128,4]{1,0,2:T(8,128)} %get-tuple-element.44, f32[4,128]{1,0:T(4,128)S(1)} %get-tuple-element.32, pred[128,4096]{0,1:T(8,128)(4,1)S(1)} %get-tuple-element.21, f32[4,128]{1,0:T(4,128)S(1)} %get-tuple-element.35, f32[4096,128,4]{1,0,2:T(8,128)S(1)} %get-tuple-element.40, ...), kind=kLoop, calls=%fused_computation.14 | loop fusion | flops 16776192 | bytes 17833984 | tf_op jit(solution)/shard_map/reduce_sum | solution.py:26
  239.8 0.0 copy-start.2
  239.8 3.4 %fusion.54 = f32[4,128,128]{1,2,0:T(8,128)S(1)} fusion(f32[4096,128,4]{1,0,2:T(8,128)S(1)} %copy-done, f32[4,128]{1,0:T(4,128)S(1)} %get-tuple-element.33, pred[128,4096]{0,1:T(8,128)(4,1)S(1)} %get-tuple-element.23, bf16[4096,1792]{1,0:T(8,128)(2,1)} %bitcast.230, f32[4,128]{1,0:T(4,128)S(1)} %get-tuple-element.16, f32[4,128]{1,0:T(4,128)S(1)} %get-tuple-element.31), kind=kOutput, calls=%fused_computation.52 | convolution fusion | flops 545390592 | bytes 10229760 | tf_op jit(solution)/shard_map/rkgqp,rpkd->rkgqd/dot_general | solution.py:27
  243.2 0.0 copy-done.2
  243.2 5.3 %fusion.66 = bf16[4,128,128]{1,2,0:T(8,128)(2,1)S(1)} fusion(f32[4,128,128]{1,2,0:T(8,128)S(1)} %fusion.54, f32[4096,128,4]{1,0,2:T(8,128)} %get-tuple-element.44, f32[4,128]{1,0:T(4,128)S(1)} %get-tuple-element.32, pred[128,4096]{0,1:T(8,128)(4,1)S(1)} %get-tuple-element.21, bf16[4096,512]{1,0:T(8,128)(2,1)S(1)} %bitcast.240, ...), kind=kOutput, calls=%fused_computation.56 | convolution fusion | flops 545456128 | bytes 10358784 | tf_op jit(solution)/shard_map/rkgqp,rpkd->rkgqd/dot_general | solution.py:27
  248.6 3.2 %fusion.45 = f32[4,128,128]{1,2,0:T(8,128)S(1)} fusion(f32[4096,128,4]{1,0,2:T(8,128)S(1)} %bitcast.220, f32[4,128]{1,0:T(4,128)S(1)} %get-tuple-element.36, pred[128,4096]{0,1:T(8,128)(4,1)S(1)} %get-tuple-element.24, bf16[4096,1792]{1,0:T(8,128)(2,1)} %bitcast.231, f32[4,128]{1,0:T(4,128)S(1)} %get-tuple-element.18, f32[4,128]{1,0:T(4,128)S(1)} %get-tuple-element.34), kind=kOutput, calls=%fused_computation.49 | convolution fusion | flops 545390592 | bytes 10229760 | tf_op jit(solution)/shard_map/rkgqp,rpkd->rkgqd/dot_general | solution.py:27
  251.8 2.0 fusion.72
  253.8 0.1 copy.94
  253.9 4.8 %convolution_convert_fusion = bf16[2,128,4096]{2,1,0:T(8,128)(2,1)} fusion(bf16[2,128,512]{2,1,0:T(8,128)(2,1)S(1)} %bitcast.242, bf16[4096,512,1]{1,0,2:T(8,128)(2,1)} %bitcast.221), kind=kOutput, calls=%fused_computation.22 | convolution fusion | flops 1074790400 | bytes 6553600 | tf_op jit(solution)/shard_map/dot_general | solution.py:156
  258.7 0.0 reduce-scatter.2.cloned.1.call-update
  258.8 41.3 %reduce-scatter.2.cloned.1.call-done = bf16[2,128,512]{2,1,0:T(8,128)(2,1)} async-done(((bf16[2,128,4096]{2,1,0:T(8,128)(2,1)}), bf16[2,128,512]{2,1,0:T(8,128)(2,1)}) %reduce-scatter.2.cloned.1.call-update) | async-done | bytes 262160 | tf_op jit(solution)/shard_map/reduce_scatter | solution.py:162
  (17 shorter events, 0.3 us)
Async XLA Ops:
  7.2 140.2 %all-gather.7.cloned.1.call-start = ((), (), s32[]{:S(2)}) async-start(), calls=%async_computation.3 | async-start | bytes 15597568 | tf_op jit(solution)/shard_map/all_gather | solution.py:42
  33.2 128.1 %copy-start.5 = (s32[2,4096]{1,0:T(2,128)S(1)}, s32[2,4096]{1,0:T(2,128)}, u32[]{:S(2)}) copy-start(s32[2,4096]{1,0:T(2,128)} %param.10) | copy-start | bytes 98308
  33.2 128.2 %copy-start.6 = (s32[2]{0:T(128)S(1)}, s32[2]{0:T(128)}, u32[]{:S(2)}) copy-start(s32[2]{0:T(128)} %param.11) | copy-start | bytes 28
  33.2 186.7 %all-gather.5.cloned.1.call-start = ((), (), s32[]{:S(2)}) async-start(), calls=%async_computation.1 | async-start | bytes 4456448 | tf_op jit(solution)/shard_map/all_gather | solution.py:42
  150.5 20.5 %copy-start.3 = (bf16[256,128]{1,0:T(8,128)(2,1)}, bf16[256,128]{1,0:T(8,128)(2,1)S(1)}, u32[]{:S(2)}) copy-start(bf16[256,128]{1,0:T(8,128)(2,1)S(1)} %get-tuple-element.29) | copy-start | bytes 196612
  150.5 20.5 %copy-start.4 = (bf16[256,128]{1,0:T(8,128)(2,1)}, bf16[256,128]{1,0:T(8,128)(2,1)S(1)}, u32[]{:S(2)}) copy-start(bf16[256,128]{1,0:T(8,128)(2,1)S(1)} %get-tuple-element.30) | copy-start | bytes 196612
  150.8 9.3 %collective-permute-start = (bf16[128,512]{0,1:T(8,128)(2,1)S(1)}, bf16[128,512]{0,1:T(8,128)(2,1)S(1)}, u32[]{:S(2)}, u32[]{:S(2)}) collective-permute-start(bf16[128,512]{0,1:T(8,128)(2,1)S(1)} %get-tuple-element.28), channel_id=1, source_target_pairs={{0,4},{4,0},{1,5},{5,1},{2,6},{6,2},{3,7},{7,3},{8,12},{12,8},{9,1... | collective-permute-start | bytes 393224 | tf_op jit(solution)/shard_map/ppermute | solution.py:38
  161.0 139.0 %reduce-scatter.2.cloned.1.call-start = ((), (), s32[]{:S(2)}) async-start(), calls=%async_computation.2 | async-start | bytes 2359296 | tf_op jit(solution)/shard_map/reduce_scatter | solution.py:162
  168.4 5.1 %copy-start.1 = (bf16[256,4,4,2,128]{0,4,3,2,1:T(8,128)(2,1)S(1)}, bf16[256,4,4,2,128]{0,4,3,2,1:T(8,128)(2,1)}, u32[]{:S(2)}) copy-start(bf16[256,4,4,2,128]{0,4,3,2,1:T(8,128)(2,1)} %copy.77) | copy-start | bytes 6291460
  219.9 9.5 %slice-start = ((s8[8388608]{0:T(1024)(128)(4,1)}), s8[4194304]{0:T(1024)(128)(4,1)S(1)}, s32[]{:S(2)}) async-start(s8[8388608]{0:T(1024)(128)(4,1)} %bitcast.219), calls=%async_computation.4 | async-start | bytes 8388608
  219.9 9.5 %copy-start = (f32[4096,128,4]{1,0,2:T(8,128)S(1)}, f32[4096,128,4]{1,0,2:T(8,128)}, u32[]{:S(2)}) copy-start(f32[4096,128,4]{1,0,2:T(8,128)} %get-tuple-element.42) | copy-start | bytes 25165828
  226.8 2.9 slice-start.1
  239.8 3.4 %copy-start.2 = (bf16[16,2,128,512]{3,2,1,0:T(8,128)(2,1)S(1)}, bf16[16,2,128,512]{3,2,1,0:T(8,128)(2,1)}, u32[]{:S(2)}) copy-start(bf16[16,2,128,512]{3,2,1,0:T(8,128)(2,1)} %all-gather.5.cloned.1.call-done) | copy-start | bytes 12582916
Sparse Core Ops, SparseCore 0:
  33.3 113.9 all-gather.6
  161.1 58.7 all-gather.4
  258.9 41.0 reduce-scatter.1
